TPU v7x, 512 devices: a whole 4x8x8 slice. The times are simulated.
512 devices in a mesh: slab: 16 (over y, core), gen: 32 (over z, x).
Axes of the slice: x: 4, y: 8, z: 8, core: 2. Of those that a mesh axis runs over, the one named last changes fastest.
Arguments:
- center: float32 [64, 4096], P('slab'), may hold values from -24 to 24
- generators: float32 [512, 64, 4096], P('gen', 'slab'), may hold values from -0.3 to 0.3
- conductivity: int32 [64, 4096], P('slab'), may hold values from 0 to 7
- cond_table: float32 [8], replicated, may hold values from 0.1 to 1
- direction_bank: float32 [32, 64, 4096], P(None, 'slab'), may hold values from -0.01171875 to 0.01171875
- selection: int32 [128], replicated, may hold values from 0 to 31
Outputs:
- hull_lo: float32 [64, 4096], P('slab', 'gen')
- hull_hi: float32 [64, 4096], P('slab', 'gen')
- supports: float32 [128], replicated
All inputs are finite; a program needn't handle non-finite values.
Results may differ from a plain program's by a relative error of at most 0.00014.
Values sent between devices are 32-bit elements; how exact they have to be, the bound alone decides.
No kernel may reach another device: no remote copies, remote signals or barrier semaphores. Data moves between devices by JAX's collectives and lax.ppermute only.
A program may use at most 64 MiB of HBM per device.

v0:
```python
import jax
import jax.numpy as jnp
from jax import lax
from jax.sharding import PartitionSpec as P

NX = 64
NY = 64


TIME_STEP = 0.16


def padded_2(x, sides, width):
    for axis, dim in sides:
        size, length = (lax.axis_size(axis), x.shape[dim])
        up = [(i, (i + 1) % size) for i in range(size - 1)]
        down = [(j, i) for i, j in up]
        last = lax.slice_in_dim(x, length - width, length, axis=dim)
        leading = lax.slice_in_dim(x, 0, width, axis=dim)
        before = lax.ppermute(last, axis, up)
        after = lax.ppermute(leading, axis, down)
        x = jnp.concatenate([before, x, after], axis=dim)
    return x


def lookup_rate(conductivity, cond_table):
    classes = jnp.arange(cond_table.shape[0], dtype=jnp.int32)
    picked = jnp.where(
        conductivity[None] == classes[:, None, None], cond_table[:, None, None], jnp.float32(0.0)
    )
    return TIME_STEP * jnp.sum(picked, axis=0)


def lateral(middle):
    cells = NX * NY
    column = jnp.arange(cells, dtype=jnp.int32) % NY
    widths = [(0, 0)] * (middle.ndim - 1) + [(NY, NY)]
    padded = jnp.pad(middle, widths)
    total = padded[..., 2 * NY :] + padded[..., :cells]
    plus = jnp.where(column < NY - 1, padded[..., NY + 1 : NY + 1 + cells], jnp.float32(0.0))
    minus = jnp.where(column > 0, padded[..., NY - 1 : NY - 1 + cells], jnp.float32(0.0))
    return total + plus + minus


def update(extended, rate_field):
    middle = extended[:, 1:-1]
    zsum = extended[:, 2:] + extended[:, :-2]
    return middle + rate_field * (zsum + lateral(middle) - 6.0 * middle)


def select_rows(selection, values):
    entries = jnp.arange(values.shape[0], dtype=jnp.int32)
    return jnp.sum(
        jnp.where(selection[:, None] == entries[None, :], values[None, :], jnp.float32(0.0)), axis=1
    )


def per_device(center, generators, conductivity, cond_table, direction_bank, selection):
    rate_field = lookup_rate(conductivity, cond_table)
    fields = jnp.concatenate([center[None], generators], axis=0)
    for turn in range(2):
        extended = padded_2(fields, (("slab", 1),), 1)
        fields = update(extended, rate_field)
    centre_moved = fields[0]
    gens_moved = fields[1:]
    radius_local = jnp.sum(jnp.abs(gens_moved), axis=0)
    radius = lax.psum_scatter(radius_local, "gen", scatter_dimension=1, tiled=True)
    columns = radius.shape[1]
    centre_cols = lax.dynamic_slice_in_dim(
        centre_moved, lax.axis_index("gen") * columns, columns, 1
    )
    hull_lo = centre_cols - radius
    hull_hi = centre_cols + radius
    bank_proj = jnp.einsum(
        "bzc,gzc->bg", direction_bank, gens_moved, precision=lax.Precision.HIGHEST
    )
    centre_proj = jnp.einsum(
        "bzc,zc->b", direction_bank, centre_moved, precision=lax.Precision.HIGHEST
    )
    summed_proj, summed_centre = lax.psum((bank_proj, centre_proj), "slab")
    partial_value = jnp.sum(jnp.abs(summed_proj), axis=1)
    magnitude = lax.psum(partial_value, "gen")
    bank_support = summed_centre + magnitude
    supports = select_rows(selection, bank_support)
    return (hull_lo, hull_hi, supports)


def solution(mesh):
    in_specs = (
        P("slab", None),
        P("gen", "slab", None),
        P("slab", None),
        P(),
        P(None, "slab", None),
        P(),
    )
    out_specs = (P("slab", "gen"), P("slab", "gen"), P())
    return jax.shard_map(
        per_device, mesh=mesh, in_specs=in_specs, out_specs=out_specs, check_vma=False
    )
```

profile of v0, /device:TPU:1, one launch (start us, length us, event | category | flops | bytes accessed | tf_op | source)
XLA Modules:
  0.0 306.8 jit_solution(5161368892599426088)
XLA Ops:
  7.2 0.0 copy-start
  7.2 0.0 copy-start.2
  7.2 0.0 copy-start.3
  7.2 0.0 copy-start.4
  7.2 0.0 reduce-scatter.4.cloned.1.call-start
  7.3 2.0 copy.13
  9.3 0.1 fusion.23
  9.4 8.8 %collective-permute-start = (f32[17,1,4096]{2,0,1:T(8,128)S(1)}, f32[17,1,4096]{2,0,1:T(8,128)S(1)}, u32[]{:S(2)}, u32[]{:S(2)}) collective-permute-start(f32[17,1,4096]{2,0,1:T(8,128)S(1)} %get-tuple-element.7), channel_id=1, source_target_pairs={{32,0},{64,32},{96,64},{128,96},{160,128},{192,160},{224,192},{256... | collective-permute-start | bytes 835592 | tf_op jit(solution)/shard_map/ppermute | solution.py:21
  18.2 1.9 collective-permute-start.1
  20.1 0.2 select_reduce_fusion
  20.4 0.2 pad_maximum_fusion
  20.6 0.0 collective-permute-done
  20.6 4.2 %collective-permute-done.1 = f32[17,1,4096]{2,0,1:T(8,128)S(1)} collective-permute-done((f32[17,1,4096]{2,0,1:T(8,128)S(1)}, f32[17,1,4096]{2,0,1:T(8,128)S(1)}, u32[]{:S(2)}, u32[]{:S(2)}) %collective-permute-start.1) | collective-permute-done | bytes 278560 | tf_op jit(solution)/shard_map/ppermute | solution.py:20
  24.8 1.7 fusion.13
  26.5 1.1 copy-done.1
  27.7 0.1 fusion.32
  27.7 1.9 collective-permute-start.2
  29.7 4.4 %collective-permute-start.3 = (f32[17,1,4096]{2,0,1:T(8,128)S(1)}, f32[17,1,4096]{2,0,1:T(8,128)}, u32[]{:S(2)}, u32[]{:S(2)}) collective-permute-start(f32[17,1,4096]{2,0,1:T(8,128)S(1)} %get-tuple-element.6), channel_id=1, source_target_pairs={{0,32},{32,64},{64,96},{96,128},{128,160},{160,192},{192,224},{224... | collective-permute-start | bytes 835592 | tf_op jit(solution)/shard_map/ppermute | solution.py:20
  34.1 3.5 %collective-permute-done.2 = f32[17,1,4096]{2,0,1:T(8,128)S(1)} collective-permute-done((f32[17,1,4096]{2,0,1:T(8,128)S(1)}, f32[17,1,4096]{2,0,1:T(8,128)S(1)}, u32[]{:S(2)}, u32[]{:S(2)}) %collective-permute-start.2) | collective-permute-done | bytes 278560 | tf_op jit(solution)/shard_map/ppermute | solution.py:21
  37.6 1.2 collective-permute-done.3
  38.8 6.8 %fusion.8 = f32[17,4,4096]{2,0,1:T(8,128)S(1)} fusion(f32[17,4,4096]{2,0,1:T(8,128)} %copy-done.1, f32[17,1,4096]{2,0,1:T(8,128)} %collective-permute-done.3, f32[17,1,4096]{2,0,1:T(8,128)S(1)} %collective-permute-done.2, f32[4,4096]{1,0:T(4,128)S(1)} %broadcast_multiply_fusion, pred[4096]{0:T(1024)(128)(4,1)S(1)} %get-tuple-element.11, ...), kind=kLoop, calls=%fused_computation.14 | loop fusion | flops 3620864 | bytes 2859008 | tf_op jit(solution)/shard_map/add | solution.py:48
  45.6 2.8 fusion.16
  48.4 2.6 fusion.19
  51.0 0.3 abs_reduce_fusion
  51.3 23.2 %all-reduce.2 = (f32[32]{0:T(128)S(1)}, f32[32,16]{0,1:T(8,128)S(1)}) all-reduce(f32[32]{0:T(128)S(1)} %fusion.19, f32[32,16]{0,1:T(8,128)S(1)} %fusion.16), channel_id=1, replica_groups=mesh['slab'=16,'gen'=32] {'slab'}, use_global_device_ids=true, to_apply=%region_3.4 | all-reduce | flops 544 | bytes 4352 | tf_op jit(solution)/shard_map/psum | solution.py:80
  74.6 2.0 copy.16
  76.6 0.0 reduce-scatter.4.cloned.1.call-update
  76.7 66.2 %psum.23 = f32[32]{0:T(128)S(1)} all-reduce(f32[32]{0:T(128)S(1)} %abs_reduce_fusion.1), channel_id=1, replica_groups=mesh['slab'=16,'gen'=32] {'gen'}, use_global_device_ids=true, to_apply=%region_6.7 | all-reduce | flops 32 | bytes 256 | tf_op jit(solution)/shard_map/psum | solution.py:82
  142.9 0.6 select_reduce_fusion.1
  143.5 155.0 %reduce-scatter.4.cloned.1.call-done = f32[128,4]{1,0:T(8,128)} async-done(((f32[4096,4]{1,0:T(8,128)}), f32[128,4]{1,0:T(8,128)}) %reduce-scatter.4.cloned.1.call-update) | async-done | bytes 2064
  298.5 0.9 copy.17
  299.4 0.6 fusion.33
  (14 shorter events, 0.2 us)
Async XLA Ops:
  7.2 38.5 %copy-start = (f32[32,4,4096]{2,1,0:T(4,128)S(1)}, f32[32,4,4096]{2,1,0:T(4,128)}, u32[]{:S(2)}) copy-start(f32[32,4,4096]{2,1,0:T(4,128)} %param.10) | copy-start | bytes 6291460
  7.2 2.1 copy-start.2
  7.2 12.9 %copy-start.3 = (s32[4,4096]{1,0:T(4,128)S(1)}, s32[4,4096]{1,0:T(4,128)}, u32[]{:S(2)}) copy-start(s32[4,4096]{1,0:T(4,128)} %param.8) | copy-start | bytes 196612
  7.2 12.9 %copy-start.4 = (f32[8]{0:T(128)S(1)}, f32[8]{0:T(128)}, u32[]{:S(2)}) copy-start(f32[8]{0:T(128)} %param.9) | copy-start | bytes 100
  7.2 291.3 %reduce-scatter.4.cloned.1.call-start = ((), (), s32[]{:S(2)}) async-start(), calls=%async_computation.1 | async-start | bytes 2162688
  9.4 11.2 %collective-permute-start = (f32[17,1,4096]{2,0,1:T(8,128)S(1)}, f32[17,1,4096]{2,0,1:T(8,128)S(1)}, u32[]{:S(2)}, u32[]{:S(2)}) collective-permute-start(f32[17,1,4096]{2,0,1:T(8,128)S(1)} %get-tuple-element.7), channel_id=1, source_target_pairs={{32,0},{64,32},{96,64},{128,96},{160,128},{192,160},{224,192},{256... | collective-permute-start | bytes 835592 | tf_op jit(solution)/shard_map/ppermute | solution.py:21
  18.2 6.6 %collective-permute-start.1 = (f32[17,1,4096]{2,0,1:T(8,128)S(1)}, f32[17,1,4096]{2,0,1:T(8,128)S(1)}, u32[]{:S(2)}, u32[]{:S(2)}) collective-permute-start(f32[17,1,4096]{2,0,1:T(8,128)S(1)} %get-tuple-element.8), channel_id=1, source_target_pairs={{0,32},{32,64},{64,96},{96,128},{128,160},{160,192},{192,224},{224... | collective-permute-start | bytes 835592 | tf_op jit(solution)/shard_map/ppermute | solution.py:20
  26.5 1.2 copy-start.1
  27.7 9.8 %collective-permute-start.2 = (f32[17,1,4096]{2,0,1:T(8,128)S(1)}, f32[17,1,4096]{2,0,1:T(8,128)S(1)}, u32[]{:S(2)}, u32[]{:S(2)}) collective-permute-start(f32[17,1,4096]{2,0,1:T(8,128)S(1)} %get-tuple-element.5), channel_id=1, source_target_pairs={{32,0},{64,32},{96,64},{128,96},{160,128},{192,160},{224,192},{256... | collective-permute-start | bytes 835592 | tf_op jit(solution)/shard_map/ppermute | solution.py:21
  29.7 9.1 %collective-permute-start.3 = (f32[17,1,4096]{2,0,1:T(8,128)S(1)}, f32[17,1,4096]{2,0,1:T(8,128)}, u32[]{:S(2)}, u32[]{:S(2)}) collective-permute-start(f32[17,1,4096]{2,0,1:T(8,128)S(1)} %get-tuple-element.6), channel_id=1, source_target_pairs={{0,32},{32,64},{64,96},{96,128},{128,160},{160,192},{192,224},{224... | collective-permute-start | bytes 835592 | tf_op jit(solution)/shard_map/ppermute | solution.py:20
  76.6 66.3 %copy-start.5 = (s32[128]{0:T(128)S(1)}, s32[128]{0:T(128)}, u32[]{:S(2)}) copy-start(s32[128]{0:T(128)} %param.11) | copy-start | bytes 1540
Sparse Core Ops, SparseCore 0:
  76.8 221.6 reduce-scatter.3
where the time goes:
time: 311 us; the launch traced here: 307 us
  waiting for transfers between devices  164 us (53%)
  blocking collectives  89.5 us (29%)
  starting transfers between devices  17.1 us (5%)
  between operations  14.2 us (5%)
  other arithmetic  10.6 us (3%)
  local copies, waits for them, and re-layouts  6.2 us (2%)
  matrix products  5.37 us (2%)
    unnamed x2, waiting for transfers between devices  155 us
    psum x1, blocking collectives, per_device(): magnitude = lax.psum(partial_value, 'gen')  66.2 us
    psum x1, blocking collectives, per_device(): summed_proj, summed_centre = lax.psum((bank_proj, centre_proj), 'slab')  23.2 us
    ppermute x2, starting transfers between devices, padded_2(): after = lax.ppermute(leading, axis, down)  10.7 us
    add x2, other arithmetic, update(): return middle + rate_field * (zsum + lateral(middle) - 6.0 * middle)  8.56 us
    ppermute x2, starting transfers between devices, padded_2(): before = lax.ppermute(last, axis, up)  6.31 us
  transfers between devices with their start and end apart: 5, of which 4 were waited for; matrix products, arithmetic and copies ran while one was open for 0% of the time, Pallas kernels for 0%

commit v1 on v0

--- a/solution.py
+++ b/solution.py
@@ -55,6 +55,32 @@
     )
 
 
+def butterfly_sum(x, axis):
+    size = lax.axis_size(axis)
+    bit = 1
+    while bit < size:
+        pairs = [(i, i ^ bit) for i in range(size)]
+        x = x + lax.ppermute(x, axis, pairs)
+        bit *= 2
+    return x
+
+
+def butterfly_scatter(x, axis):
+    size = lax.axis_size(axis)
+    me = lax.axis_index(axis)
+    bit = size // 2
+    while bit >= 1:
+        half = x.shape[1] // 2
+        lo, hi = x[:, :half], x[:, half:]
+        upper = (me // bit) % 2 == 1
+        keep = jnp.where(upper, hi, lo)
+        send = jnp.where(upper, lo, hi)
+        pairs = [(i, i ^ bit) for i in range(size)]
+        x = keep + lax.ppermute(send, axis, pairs)
+        bit //= 2
+    return x
+
+
 def per_device(center, generators, conductivity, cond_table, direction_bank, selection):
     rate_field = lookup_rate(conductivity, cond_table)
     fields = jnp.concatenate([center[None], generators], axis=0)
@@ -64,7 +90,7 @@
     centre_moved = fields[0]
     gens_moved = fields[1:]
     radius_local = jnp.sum(jnp.abs(gens_moved), axis=0)
-    radius = lax.psum_scatter(radius_local, "gen", scatter_dimension=1, tiled=True)
+    radius = butterfly_scatter(radius_local, "gen")
     columns = radius.shape[1]
     centre_cols = lax.dynamic_slice_in_dim(
         centre_moved, lax.axis_index("gen") * columns, columns, 1
@@ -77,9 +103,10 @@
     centre_proj = jnp.einsum(
         "bzc,zc->b", direction_bank, centre_moved, precision=lax.Precision.HIGHEST
     )
-    summed_proj, summed_centre = lax.psum((bank_proj, centre_proj), "slab")
+    both = butterfly_sum(jnp.concatenate([bank_proj, centre_proj[:, None]], axis=1), "slab")
+    summed_proj, summed_centre = both[:, :-1], both[:, -1]
     partial_value = jnp.sum(jnp.abs(summed_proj), axis=1)
-    magnitude = lax.psum(partial_value, "gen")
+    magnitude = butterfly_sum(partial_value, "gen")
     bank_support = summed_centre + magnitude
     supports = select_rows(selection, bank_support)
     return (hull_lo, hull_hi, supports)

time: 311 us -> 123 us (0.40)
  the two profiles are of different devices: /device:TPU:1 before, /device:TPU:36 now
where the time goes in v1:
time: 123 us; the launch traced here: 122 us
  starting transfers between devices  53.6 us (44%)
  waiting for transfers between devices  46 us (37%)
  other arithmetic  11.5 us (9%)
  matrix products  5.37 us (4%)
  local copies, waits for them, and re-layouts  4.37 us (4%)
    ppermute x9, waiting for transfers between devices, butterfly_sum(): x = x + lax.ppermute(x, axis, pairs)  28.9 us
    ppermute x5, starting transfers between devices, butterfly_scatter(): x = keep + lax.ppermute(send, axis, pairs)  24.1 us
    ppermute x9, starting transfers between devices, butterfly_sum(): x = x + lax.ppermute(x, axis, pairs)  20.9 us
    ppermute x2, waiting for transfers between devices, padded_2(): before = lax.ppermute(last, axis, up)  10.2 us
    add x2, other arithmetic, update(): return middle + rate_field * (zsum + lateral(middle) - 6.0 * middle)  8.82 us
    ppermute x2, waiting for transfers between devices, padded_2(): after = lax.ppermute(leading, axis, down)  5.17 us
    ppermute x2, starting transfers between devices, padded_2(): before = lax.ppermute(last, axis, up)  4.81 us
    ppermute x2, starting transfers between devices, padded_2(): after = lax.ppermute(leading, axis, down)  3.84 us
  transfers between devices with their start and end apart: 18, of which 13 were waited for; matrix products, arithmetic and copies ran while one was open for 2% of the time, Pallas kernels for 0%

profile of v1, /device:TPU:36, one launch (start us, length us, event | category | flops | bytes accessed | tf_op | source)
XLA Modules:
  0.0 122.1 jit_solution(13606307755744303611)
XLA Ops:
  0.7 2.0 %copy.11 = f32[16,4,4096]{2,0,1:T(8,128)S(1)} copy(f32[16,4,4096]{2,1,0:T(4,128)} %param.7) | data formatting | bytes 2097152 | tf_op args[1]
  2.8 1.9 %collective-permute-start = (f32[17,1,4096]{2,0,1:T(8,128)S(1)}, f32[17,1,4096]{2,0,1:T(8,128)S(1)}, u32[]{:S(2)}, u32[]{:S(2)}) collective-permute-start(f32[17,1,4096]{2,0,1:T(8,128)S(1)} %get-tuple-element.7), channel_id=1, source_target_pairs={{32,0},{64,32},{96,64},{128,96},{160,128},{192,160},{224,192},{256... | collective-permute-start | bytes 835592 | tf_op jit(solution)/shard_map/ppermute | solution.py:21
  4.7 2.4 %collective-permute-start.1 = (f32[17,1,4096]{2,0,1:T(8,128)S(1)}, f32[17,1,4096]{2,0,1:T(8,128)S(1)}, u32[]{:S(2)}, u32[]{:S(2)}) collective-permute-start(f32[17,1,4096]{2,0,1:T(8,128)S(1)} %get-tuple-element.8), channel_id=1, source_target_pairs={{0,32},{32,64},{64,96},{96,128},{128,160},{160,192},{192,224},{224... | collective-permute-start | bytes 835592 | tf_op jit(solution)/shard_map/ppermute | solution.py:20
  7.7 2.3 %collective-permute-done = f32[17,1,4096]{2,0,1:T(8,128)S(1)} collective-permute-done((f32[17,1,4096]{2,0,1:T(8,128)S(1)}, f32[17,1,4096]{2,0,1:T(8,128)S(1)}, u32[]{:S(2)}, u32[]{:S(2)}) %collective-permute-start) | collective-permute-done | bytes 278560 | tf_op jit(solution)/shard_map/ppermute | solution.py:21
  10.0 5.0 %collective-permute-done.1 = f32[17,1,4096]{2,0,1:T(8,128)S(1)} collective-permute-done((f32[17,1,4096]{2,0,1:T(8,128)S(1)}, f32[17,1,4096]{2,0,1:T(8,128)S(1)}, u32[]{:S(2)}, u32[]{:S(2)}) %collective-permute-start.1) | collective-permute-done | bytes 278560 | tf_op jit(solution)/shard_map/ppermute | solution.py:20
  18.0 1.9 %collective-permute-start.2 = (f32[17,1,4096]{2,0,1:T(8,128)S(1)}, f32[17,1,4096]{2,0,1:T(8,128)S(1)}, u32[]{:S(2)}, u32[]{:S(2)}) collective-permute-start(f32[17,1,4096]{2,0,1:T(8,128)S(1)} %get-tuple-element.5), channel_id=1, source_target_pairs={{32,0},{64,32},{96,64},{128,96},{160,128},{192,160},{224,192},{256... | collective-permute-start | bytes 835592 | tf_op jit(solution)/shard_map/ppermute | solution.py:21
  19.9 2.4 %collective-permute-start.3 = (f32[17,1,4096]{2,0,1:T(8,128)S(1)}, f32[17,1,4096]{2,0,1:T(8,128)}, u32[]{:S(2)}, u32[]{:S(2)}) collective-permute-start(f32[17,1,4096]{2,0,1:T(8,128)S(1)} %get-tuple-element.6), channel_id=1, source_target_pairs={{0,32},{32,64},{64,96},{96,128},{128,160},{160,192},{192,224},{224... | collective-permute-start | bytes 835592 | tf_op jit(solution)/shard_map/ppermute | solution.py:20
  22.4 2.8 %collective-permute-done.2 = f32[17,1,4096]{2,0,1:T(8,128)S(1)} collective-permute-done((f32[17,1,4096]{2,0,1:T(8,128)S(1)}, f32[17,1,4096]{2,0,1:T(8,128)S(1)}, u32[]{:S(2)}, u32[]{:S(2)}) %collective-permute-start.2) | collective-permute-done | bytes 278560 | tf_op jit(solution)/shard_map/ppermute | solution.py:21
  25.2 5.1 %collective-permute-done.3 = f32[17,1,4096]{2,0,1:T(8,128)} collective-permute-done((f32[17,1,4096]{2,0,1:T(8,128)S(1)}, f32[17,1,4096]{2,0,1:T(8,128)}, u32[]{:S(2)}, u32[]{:S(2)}) %collective-permute-start.3) | collective-permute-done | bytes 278560 | tf_op jit(solution)/shard_map/ppermute | solution.py:20
  30.3 7.1 %fusion.8 = f32[17,4,4096]{2,0,1:T(8,128)S(1)} fusion(f32[17,4,4096]{2,0,1:T(8,128)} %copy-done.2, f32[17,1,4096]{2,0,1:T(8,128)} %collective-permute-done.3, f32[17,1,4096]{2,0,1:T(8,128)S(1)} %collective-permute-done.2, f32[4,4096]{1,0:T(4,128)S(1)} %broadcast_multiply_fusion, pred[4096]{0:T(1024)(128)(4,1)S(1)} %get-tuple-element.9, ...), kind=kLoop, calls=%fused_computation.14 | loop fusion | flops 3620864 | bytes 2859008 | tf_op jit(solution)/shard_map/add | solution.py:48
  37.5 2.8 %fusion.16 = f32[32,16]{0,1:T(8,128)S(1)} fusion(f32[32,4,4096]{2,1,0:T(4,128)S(1)} %copy-done, f32[17,4,4096]{2,0,1:T(8,128)S(1)} %fusion.8), kind=kOutput, calls=%fused_computation.31 | convolution fusion | flops 100663296 | bytes 3147776 | tf_op jit(solution)/shard_map/bzc,gzc->bg/dot_general | solution.py:100
  40.2 2.6 %fusion.19 = f32[32,1]{0,1:T(1,128)S(1)} fusion(f32[32,4,4096]{2,1,0:T(4,128)S(1)} %copy-done, f32[17,4,4096]{2,0,1:T(8,128)S(1)} %fusion.8), kind=kOutput, calls=%fused_computation.32 | convolution fusion | flops 6291456 | bytes 2162816 | tf_op jit(solution)/shard_map/bzc,zc->b/dot_general | solution.py:103
  43.1 1.9 %collective-permute-start.9 = (f32[32,17]{0,1:T(8,128)S(1)}, f32[32,17]{0,1:T(8,128)S(1)}, u32[]{:S(2)}, u32[]{:S(2)}) collective-permute-start(f32[32,17]{0,1:T(8,128)S(1)} %pad_maximum_fusion.7), channel_id=1, source_target_pairs={{0,32},{32,0},{64,96},{96,64},{128,160},{160,128},{192,224},{224,1... | collective-permute-start | bytes 6536 | tf_op jit(solution)/shard_map/ppermute | solution.py:63
  45.1 10.9 %collective-permute-start.4 = (f32[4,2048]{1,0:T(4,128)S(1)}, f32[4,2048]{1,0:T(4,128)S(1)}, u32[]{:S(2)}, u32[]{:S(2)}) collective-permute-start(f32[4,2048]{1,0:T(4,128)S(1)} %slice_select_fusion), channel_id=1, source_target_pairs={{0,16},{1,17},{2,18},{3,19},{4,20},{5,21},{6,22},{7,23},{8,24},{9,... | collective-permute-start | bytes 98312 | tf_op jit(solution)/shard_map/ppermute | solution.py:79
  56.0 1.9 %collective-permute-start.10 = (f32[32,17]{0,1:T(8,128)S(1)}, f32[32,17]{0,1:T(8,128)S(1)}, u32[]{:S(2)}, u32[]{:S(2)}) collective-permute-start(f32[32,17]{0,1:T(8,128)S(1)} %fusion.33), channel_id=1, source_target_pairs={{0,64},{32,96},{64,0},{96,32},{128,192},{160,224},{192,128},{224,1... | collective-permute-start | bytes 6536 | tf_op jit(solution)/shard_map/ppermute | solution.py:63
  58.0 3.7 %collective-permute-done.10 = f32[32,17]{0,1:T(8,128)S(1)} collective-permute-done((f32[32,17]{0,1:T(8,128)S(1)}, f32[32,17]{0,1:T(8,128)S(1)}, u32[]{:S(2)}, u32[]{:S(2)}) %collective-permute-start.10) | collective-permute-done | bytes 2208 | tf_op jit(solution)/shard_map/ppermute | solution.py:63
  61.6 1.9 %collective-permute-start.11 = (f32[32,17]{0,1:T(8,128)S(1)}, f32[32,17]{0,1:T(8,128)S(1)}, u32[]{:S(2)}, u32[]{:S(2)}) collective-permute-start(f32[32,17]{0,1:T(8,128)S(1)} %add.152), channel_id=1, source_target_pairs={{0,128},{32,160},{64,192},{96,224},{128,0},{160,32},{192,64},{224,... | collective-permute-start | bytes 6536 | tf_op jit(solution)/shard_map/ppermute | solution.py:63
  63.6 4.5 %collective-permute-done.11 = f32[32,17]{0,1:T(8,128)S(1)} collective-permute-done((f32[32,17]{0,1:T(8,128)S(1)}, f32[32,17]{0,1:T(8,128)S(1)}, u32[]{:S(2)}, u32[]{:S(2)}) %collective-permute-start.11) | collective-permute-done | bytes 2208 | tf_op jit(solution)/shard_map/ppermute | solution.py:63
  68.1 1.9 %collective-permute-start.12 = (f32[32,17]{0,1:T(8,128)S(1)}, f32[32,17]{0,1:T(8,128)S(1)}, u32[]{:S(2)}, u32[]{:S(2)}) collective-permute-start(f32[32,17]{0,1:T(8,128)S(1)} %add.153), channel_id=1, source_target_pairs={{0,256},{32,288},{64,320},{96,352},{128,384},{160,416},{192,448},{... | collective-permute-start | bytes 6536 | tf_op jit(solution)/shard_map/ppermute | solution.py:63
  70.1 7.5 %collective-permute-done.12 = f32[32,17]{0,1:T(8,128)S(1)} collective-permute-done((f32[32,17]{0,1:T(8,128)S(1)}, f32[32,17]{0,1:T(8,128)S(1)}, u32[]{:S(2)}, u32[]{:S(2)}) %collective-permute-start.12) | collective-permute-done | bytes 2208 | tf_op jit(solution)/shard_map/ppermute | solution.py:63
  77.6 4.3 %collective-permute-start.5 = (f32[4,1024]{1,0:T(4,128)S(1)}, f32[4,1024]{1,0:T(4,128)S(1)}, u32[]{:S(2)}, u32[]{:S(2)}) collective-permute-start(f32[4,1024]{1,0:T(4,128)S(1)} %slice_select_fusion.1), channel_id=1, source_target_pairs={{0,8},{1,9},{2,10},{3,11},{4,12},{5,13},{6,14},{7,15},{8,0},{9,1},... | collective-permute-start | bytes 49160 | tf_op jit(solution)/shard_map/ppermute | solution.py:79
  82.0 3.1 %collective-permute-start.13 = (f32[32]{0:T(128)S(1)}, f32[32]{0:T(128)S(1)}, u32[]{:S(2)}, u32[]{:S(2)}) collective-permute-start(f32[32]{0:T(128)S(1)} %fusion.31), channel_id=1, source_target_pairs={{0,1},{1,0},{2,3},{3,2},{4,5},{5,4},{6,7},{7,6},{8,9},{9,8},{10,11... | collective-permute-start | bytes 392 | tf_op jit(solution)/shard_map/ppermute | solution.py:63
  85.1 2.3 %collective-permute-done.13 = f32[32]{0:T(128)S(1)} collective-permute-done((f32[32]{0:T(128)S(1)}, f32[32]{0:T(128)S(1)}, u32[]{:S(2)}, u32[]{:S(2)}) %collective-permute-start.13) | collective-permute-done | bytes 160 | tf_op jit(solution)/shard_map/ppermute | solution.py:63
  87.4 2.4 %collective-permute-start.14 = (f32[32]{0:T(128)S(1)}, f32[32]{0:T(128)S(1)}, u32[]{:S(2)}, u32[]{:S(2)}) collective-permute-start(f32[32]{0:T(128)S(1)} %add.155), channel_id=1, source_target_pairs={{0,2},{1,3},{2,0},{3,1},{4,6},{5,7},{6,4},{7,5},{8,10},{9,11},{10,... | collective-permute-start | bytes 392 | tf_op jit(solution)/shard_map/ppermute | solution.py:63
  89.8 4.5 %collective-permute-done.14 = f32[32]{0:T(128)S(1)} collective-permute-done((f32[32]{0:T(128)S(1)}, f32[32]{0:T(128)S(1)}, u32[]{:S(2)}, u32[]{:S(2)}) %collective-permute-start.14) | collective-permute-done | bytes 160 | tf_op jit(solution)/shard_map/ppermute | solution.py:63
  94.3 3.4 %collective-permute-start.15 = (f32[32]{0:T(128)S(1)}, f32[32]{0:T(128)S(1)}, u32[]{:S(2)}, u32[]{:S(2)}) collective-permute-start(f32[32]{0:T(128)S(1)} %add.156), channel_id=1, source_target_pairs={{0,4},{1,5},{2,6},{3,7},{4,0},{5,1},{6,2},{7,3},{8,12},{9,13},{10,... | collective-permute-start | bytes 392 | tf_op jit(solution)/shard_map/ppermute | solution.py:63
  99.8 2.4 %collective-permute-start.16 = (f32[32]{0:T(128)S(1)}, f32[32]{0:T(128)S(1)}, u32[]{:S(2)}, u32[]{:S(2)}) collective-permute-start(f32[32]{0:T(128)S(1)} %add.157), channel_id=1, source_target_pairs={{0,8},{1,9},{2,10},{3,11},{4,12},{5,13},{6,14},{7,15},{8,0},{9,1},... | collective-permute-start | bytes 392 | tf_op jit(solution)/shard_map/ppermute | solution.py:63
  102.2 3.4 %collective-permute-start.6 = (f32[4,512]{1,0:T(4,128)S(1)}, f32[4,512]{1,0:T(4,128)S(1)}, u32[]{:S(2)}, u32[]{:S(2)}) collective-permute-start(f32[4,512]{1,0:T(4,128)S(1)} %slice_select_fusion.2), channel_id=1, source_target_pairs={{0,4},{1,5},{2,6},{3,7},{4,0},{5,1},{6,2},{7,3},{8,12},{9,13},{10,... | collective-permute-start | bytes 24584 | tf_op jit(solution)/shard_map/ppermute | solution.py:79
  106.1 1.9 %collective-permute-start.17 = (f32[32]{0:T(128)S(1)}, f32[32]{0:T(128)S(1)}, u32[]{:S(2)}, u32[]{:S(2)}) collective-permute-start(f32[32]{0:T(128)S(1)} %add.158), channel_id=1, source_target_pairs={{0,16},{1,17},{2,18},{3,19},{4,20},{5,21},{6,22},{7,23},{8,24},{9,... | collective-permute-start | bytes 392 | tf_op jit(solution)/shard_map/ppermute | solution.py:63
  108.0 2.4 %collective-permute-start.7 = (f32[4,256]{1,0:T(4,128)S(1)}, f32[4,256]{1,0:T(4,128)S(1)}, u32[]{:S(2)}, u32[]{:S(2)}) collective-permute-start(f32[4,256]{1,0:T(4,128)S(1)} %slice_select_fusion.3), channel_id=1, source_target_pairs={{0,2},{1,3},{2,0},{3,1},{4,6},{5,7},{6,4},{7,5},{8,10},{9,11},{10,... | collective-permute-start | bytes 12296 | tf_op jit(solution)/shard_map/ppermute | solution.py:79
  110.5 5.0 %collective-permute-done.17 = f32[32]{0:T(128)S(1)} collective-permute-done((f32[32]{0:T(128)S(1)}, f32[32]{0:T(128)S(1)}, u32[]{:S(2)}, u32[]{:S(2)}) %collective-permute-start.17) | collective-permute-done | bytes 160 | tf_op jit(solution)/shard_map/ppermute | solution.py:63
  115.4 3.1 %collective-permute-start.8 = (f32[4,128]{1,0:T(4,128)S(1)}, f32[4,128]{1,0:T(4,128)S(1)}, u32[]{:S(2)}, u32[]{:S(2)}) collective-permute-start(f32[4,128]{1,0:T(4,128)S(1)} %slice_select_fusion.4), channel_id=1, source_target_pairs={{0,1},{1,0},{2,3},{3,2},{4,5},{5,4},{6,7},{7,6},{8,9},{9,8},{10,11... | collective-permute-start | bytes 6152 | tf_op jit(solution)/shard_map/ppermute | solution.py:79
  (56 shorter events, 10.0 us)
Async XLA Ops:
  0.6 36.8 %copy-start = (f32[32,4,4096]{2,1,0:T(4,128)S(1)}, f32[32,4,4096]{2,1,0:T(4,128)}, u32[]{:S(2)}) copy-start(f32[32,4,4096]{2,1,0:T(4,128)} %param.10) | copy-start | bytes 6291460
  0.6 2.0 %copy-start.3 = (f32[4,4096]{1,0:T(4,128)S(1)}, f32[4,4096]{1,0:T(4,128)}, u32[]{:S(2)}) copy-start(f32[4,4096]{1,0:T(4,128)} %param.6) | copy-start | bytes 196612
  0.7 6.5 %copy-start.4 = (s32[4,4096]{1,0:T(4,128)S(1)}, s32[4,4096]{1,0:T(4,128)}, u32[]{:S(2)}) copy-start(s32[4,4096]{1,0:T(4,128)} %param.8) | copy-start | bytes 196612
  0.7 6.5 %copy-start.5 = (f32[8]{0:T(128)S(1)}, f32[8]{0:T(128)}, u32[]{:S(2)}) copy-start(f32[8]{0:T(128)} %param.9) | copy-start | bytes 100
  2.8 7.2 %collective-permute-start = (f32[17,1,4096]{2,0,1:T(8,128)S(1)}, f32[17,1,4096]{2,0,1:T(8,128)S(1)}, u32[]{:S(2)}, u32[]{:S(2)}) collective-permute-start(f32[17,1,4096]{2,0,1:T(8,128)S(1)} %get-tuple-element.7), channel_id=1, source_target_pairs={{32,0},{64,32},{96,64},{128,96},{160,128},{192,160},{224,192},{256... | collective-permute-start | bytes 835592 | tf_op jit(solution)/shard_map/ppermute | solution.py:21
  4.7 10.3 %collective-permute-start.1 = (f32[17,1,4096]{2,0,1:T(8,128)S(1)}, f32[17,1,4096]{2,0,1:T(8,128)S(1)}, u32[]{:S(2)}, u32[]{:S(2)}) collective-permute-start(f32[17,1,4096]{2,0,1:T(8,128)S(1)} %get-tuple-element.8), channel_id=1, source_target_pairs={{0,32},{32,64},{64,96},{96,128},{128,160},{160,192},{192,224},{224... | collective-permute-start | bytes 835592 | tf_op jit(solution)/shard_map/ppermute | solution.py:20
  16.8 1.2 copy-start.2
  18.0 7.2 %collective-permute-start.2 = (f32[17,1,4096]{2,0,1:T(8,128)S(1)}, f32[17,1,4096]{2,0,1:T(8,128)S(1)}, u32[]{:S(2)}, u32[]{:S(2)}) collective-permute-start(f32[17,1,4096]{2,0,1:T(8,128)S(1)} %get-tuple-element.5), channel_id=1, source_target_pairs={{32,0},{64,32},{96,64},{128,96},{160,128},{192,160},{224,192},{256... | collective-permute-start | bytes 835592 | tf_op jit(solution)/shard_map/ppermute | solution.py:21
  19.9 10.4 %collective-permute-start.3 = (f32[17,1,4096]{2,0,1:T(8,128)S(1)}, f32[17,1,4096]{2,0,1:T(8,128)}, u32[]{:S(2)}, u32[]{:S(2)}) collective-permute-start(f32[17,1,4096]{2,0,1:T(8,128)S(1)} %get-tuple-element.6), channel_id=1, source_target_pairs={{0,32},{32,64},{64,96},{96,128},{128,160},{160,192},{192,224},{224... | collective-permute-start | bytes 835592 | tf_op jit(solution)/shard_map/ppermute | solution.py:20
  37.5 5.4 %copy-start.1 = (f32[17,4,4096]{2,0,1:T(8,128)}, f32[17,4,4096]{2,0,1:T(8,128)S(1)}, u32[]{:S(2)}) copy-start(f32[17,4,4096]{2,0,1:T(8,128)S(1)} %fusion.8) | copy-start | bytes 3342340
  42.8 75.7 %copy-start.6 = (s32[128]{0:T(128)S(1)}, s32[128]{0:T(128)}, u32[]{:S(2)}) copy-start(s32[128]{0:T(128)} %param.11) | copy-start | bytes 1540
  43.1 12.9 %collective-permute-start.9 = (f32[32,17]{0,1:T(8,128)S(1)}, f32[32,17]{0,1:T(8,128)S(1)}, u32[]{:S(2)}, u32[]{:S(2)}) collective-permute-start(f32[32,17]{0,1:T(8,128)S(1)} %pad_maximum_fusion.7), channel_id=1, source_target_pairs={{0,32},{32,0},{64,96},{96,64},{128,160},{160,128},{192,224},{224,1... | collective-permute-start | bytes 6536 | tf_op jit(solution)/shard_map/ppermute | solution.py:63
  45.1 32.5 %collective-permute-start.4 = (f32[4,2048]{1,0:T(4,128)S(1)}, f32[4,2048]{1,0:T(4,128)S(1)}, u32[]{:S(2)}, u32[]{:S(2)}) collective-permute-start(f32[4,2048]{1,0:T(4,128)S(1)} %slice_select_fusion), channel_id=1, source_target_pairs={{0,16},{1,17},{2,18},{3,19},{4,20},{5,21},{6,22},{7,23},{8,24},{9,... | collective-permute-start | bytes 98312 | tf_op jit(solution)/shard_map/ppermute | solution.py:79
  56.0 5.6 %collective-permute-start.10 = (f32[32,17]{0,1:T(8,128)S(1)}, f32[32,17]{0,1:T(8,128)S(1)}, u32[]{:S(2)}, u32[]{:S(2)}) collective-permute-start(f32[32,17]{0,1:T(8,128)S(1)} %fusion.33), channel_id=1, source_target_pairs={{0,64},{32,96},{64,0},{96,32},{128,192},{160,224},{192,128},{224,1... | collective-permute-start | bytes 6536 | tf_op jit(solution)/shard_map/ppermute | solution.py:63
  61.6 6.5 %collective-permute-start.11 = (f32[32,17]{0,1:T(8,128)S(1)}, f32[32,17]{0,1:T(8,128)S(1)}, u32[]{:S(2)}, u32[]{:S(2)}) collective-permute-start(f32[32,17]{0,1:T(8,128)S(1)} %add.152), channel_id=1, source_target_pairs={{0,128},{32,160},{64,192},{96,224},{128,0},{160,32},{192,64},{224,... | collective-permute-start | bytes 6536 | tf_op jit(solution)/shard_map/ppermute | solution.py:63
  68.1 9.5 %collective-permute-start.12 = (f32[32,17]{0,1:T(8,128)S(1)}, f32[32,17]{0,1:T(8,128)S(1)}, u32[]{:S(2)}, u32[]{:S(2)}) collective-permute-start(f32[32,17]{0,1:T(8,128)S(1)} %add.153), channel_id=1, source_target_pairs={{0,256},{32,288},{64,320},{96,352},{128,384},{160,416},{192,448},{... | collective-permute-start | bytes 6536 | tf_op jit(solution)/shard_map/ppermute | solution.py:63
  77.6 24.6 %collective-permute-start.5 = (f32[4,1024]{1,0:T(4,128)S(1)}, f32[4,1024]{1,0:T(4,128)S(1)}, u32[]{:S(2)}, u32[]{:S(2)}) collective-permute-start(f32[4,1024]{1,0:T(4,128)S(1)} %slice_select_fusion.1), channel_id=1, source_target_pairs={{0,8},{1,9},{2,10},{3,11},{4,12},{5,13},{6,14},{7,15},{8,0},{9,1},... | collective-permute-start | bytes 49160 | tf_op jit(solution)/shard_map/ppermute | solution.py:79
  82.0 5.4 %collective-permute-start.13 = (f32[32]{0:T(128)S(1)}, f32[32]{0:T(128)S(1)}, u32[]{:S(2)}, u32[]{:S(2)}) collective-permute-start(f32[32]{0:T(128)S(1)} %fusion.31), channel_id=1, source_target_pairs={{0,1},{1,0},{2,3},{3,2},{4,5},{5,4},{6,7},{7,6},{8,9},{9,8},{10,11... | collective-permute-start | bytes 392 | tf_op jit(solution)/shard_map/ppermute | solution.py:63
  87.4 6.9 %collective-permute-start.14 = (f32[32]{0:T(128)S(1)}, f32[32]{0:T(128)S(1)}, u32[]{:S(2)}, u32[]{:S(2)}) collective-permute-start(f32[32]{0:T(128)S(1)} %add.155), channel_id=1, source_target_pairs={{0,2},{1,3},{2,0},{3,1},{4,6},{5,7},{6,4},{7,5},{8,10},{9,11},{10,... | collective-permute-start | bytes 392 | tf_op jit(solution)/shard_map/ppermute | solution.py:63
  94.3 5.4 %collective-permute-start.15 = (f32[32]{0:T(128)S(1)}, f32[32]{0:T(128)S(1)}, u32[]{:S(2)}, u32[]{:S(2)}) collective-permute-start(f32[32]{0:T(128)S(1)} %add.156), channel_id=1, source_target_pairs={{0,4},{1,5},{2,6},{3,7},{4,0},{5,1},{6,2},{7,3},{8,12},{9,13},{10,... | collective-permute-start | bytes 392 | tf_op jit(solution)/shard_map/ppermute | solution.py:63
  99.8 6.3 %collective-permute-start.16 = (f32[32]{0:T(128)S(1)}, f32[32]{0:T(128)S(1)}, u32[]{:S(2)}, u32[]{:S(2)}) collective-permute-start(f32[32]{0:T(128)S(1)} %add.157), channel_id=1, source_target_pairs={{0,8},{1,9},{2,10},{3,11},{4,12},{5,13},{6,14},{7,15},{8,0},{9,1},... | collective-permute-start | bytes 392 | tf_op jit(solution)/shard_map/ppermute | solution.py:63
  102.2 5.8 %collective-permute-start.6 = (f32[4,512]{1,0:T(4,128)S(1)}, f32[4,512]{1,0:T(4,128)S(1)}, u32[]{:S(2)}, u32[]{:S(2)}) collective-permute-start(f32[4,512]{1,0:T(4,128)S(1)} %slice_select_fusion.2), channel_id=1, source_target_pairs={{0,4},{1,5},{2,6},{3,7},{4,0},{5,1},{6,2},{7,3},{8,12},{9,13},{10,... | collective-permute-start | bytes 24584 | tf_op jit(solution)/shard_map/ppermute | solution.py:79
  106.1 9.3 %collective-permute-start.17 = (f32[32]{0:T(128)S(1)}, f32[32]{0:T(128)S(1)}, u32[]{:S(2)}, u32[]{:S(2)}) collective-permute-start(f32[32]{0:T(128)S(1)} %add.158), channel_id=1, source_target_pairs={{0,16},{1,17},{2,18},{3,19},{4,20},{5,21},{6,22},{7,23},{8,24},{9,... | collective-permute-start | bytes 392 | tf_op jit(solution)/shard_map/ppermute | solution.py:63
  108.0 7.4 %collective-permute-start.7 = (f32[4,256]{1,0:T(4,128)S(1)}, f32[4,256]{1,0:T(4,128)S(1)}, u32[]{:S(2)}, u32[]{:S(2)}) collective-permute-start(f32[4,256]{1,0:T(4,128)S(1)} %slice_select_fusion.3), channel_id=1, source_target_pairs={{0,2},{1,3},{2,0},{3,1},{4,6},{5,7},{6,4},{7,5},{8,10},{9,11},{10,... | collective-permute-start | bytes 12296 | tf_op jit(solution)/shard_map/ppermute | solution.py:79
  115.4 5.5 %collective-permute-start.8 = (f32[4,128]{1,0:T(4,128)S(1)}, f32[4,128]{1,0:T(4,128)S(1)}, u32[]{:S(2)}, u32[]{:S(2)}) collective-permute-start(f32[4,128]{1,0:T(4,128)S(1)} %slice_select_fusion.4), channel_id=1, source_target_pairs={{0,1},{1,0},{2,3},{3,2},{4,5},{5,4},{6,7},{7,6},{8,9},{9,8},{10,11... | collective-permute-start | bytes 6152 | tf_op jit(solution)/shard_map/ppermute | solution.py:79

commit v2 on v1

--- a/solution.py
+++ b/solution.py
@@ -65,7 +65,7 @@
     return x
 
 
-def butterfly_scatter(x, axis):
+def butterfly_scatter(x, extra, axis):
     size = lax.axis_size(axis)
     me = lax.axis_index(axis)
     bit = size // 2
@@ -76,37 +76,37 @@
         keep = jnp.where(upper, hi, lo)
         send = jnp.where(upper, lo, hi)
         pairs = [(i, i ^ bit) for i in range(size)]
-        x = keep + lax.ppermute(send, axis, pairs)
+        message = jnp.concatenate([send.reshape(-1), extra])
+        got = lax.ppermute(message, axis, pairs)
+        x = keep + got[: send.size].reshape(send.shape)
+        extra = extra + got[send.size :]
         bit //= 2
-    return x
+    return x, extra
 
 
 def per_device(center, generators, conductivity, cond_table, direction_bank, selection):
     rate_field = lookup_rate(conductivity, cond_table)
-    fields = jnp.concatenate([center[None], generators], axis=0)
-    for turn in range(2):
-        extended = padded_2(fields, (("slab", 1),), 1)
-        fields = update(extended, rate_field)
+    packed = jnp.concatenate([center[None], generators, rate_field[None]], axis=0)
+    extended = padded_2(packed, (("slab", 1),), 2)
+    fields, rate_ext = extended[:-1], extended[-1]
+    fields = update(fields, rate_ext[1:-1])
+    fields = update(fields, rate_field)
     centre_moved = fields[0]
     gens_moved = fields[1:]
     radius_local = jnp.sum(jnp.abs(gens_moved), axis=0)
-    radius = butterfly_scatter(radius_local, "gen")
+    all_proj = jnp.einsum(
+        "bzc,gzc->bg", direction_bank, fields, precision=lax.Precision.HIGHEST
+    )
+    summed = butterfly_sum(all_proj, "slab")
+    summed_centre, summed_proj = summed[:, 0], summed[:, 1:]
+    partial_value = jnp.sum(jnp.abs(summed_proj), axis=1)
+    radius, magnitude = butterfly_scatter(radius_local, partial_value, "gen")
     columns = radius.shape[1]
     centre_cols = lax.dynamic_slice_in_dim(
         centre_moved, lax.axis_index("gen") * columns, columns, 1
     )
     hull_lo = centre_cols - radius
     hull_hi = centre_cols + radius
-    bank_proj = jnp.einsum(
-        "bzc,gzc->bg", direction_bank, gens_moved, precision=lax.Precision.HIGHEST
-    )
-    centre_proj = jnp.einsum(
-        "bzc,zc->b", direction_bank, centre_moved, precision=lax.Precision.HIGHEST
-    )
-    both = butterfly_sum(jnp.concatenate([bank_proj, centre_proj[:, None]], axis=1), "slab")
-    summed_proj, summed_centre = both[:, :-1], both[:, -1]
-    partial_value = jnp.sum(jnp.abs(summed_proj), axis=1)
-    magnitude = butterfly_sum(partial_value, "gen")
     bank_support = summed_centre + magnitude
     supports = select_rows(selection, bank_support)
     return (hull_lo, hull_hi, supports)

time: 123 us -> 96.8 us (0.79)
  the two profiles are of different devices: /device:TPU:36 before, /device:TPU:8 now
where the time goes in v2:
time: 96.8 us; the launch traced here: 96.4 us
  waiting for transfers between devices  46.7 us (48%)
  starting transfers between devices  31.1 us (32%)
  other arithmetic  11.1 us (11%)
  matrix products  3.45 us (4%)
  local copies, waits for them, and re-layouts  2.89 us (3%)
  between operations  1.14 us (1%)
    ppermute x5, starting transfers between devices, butterfly_scatter(): got = lax.ppermute(message, axis, pairs)  17.5 us
    ppermute x5, waiting for transfers between devices, butterfly_scatter(): got = lax.ppermute(message, axis, pairs)  17 us
    ppermute x4, waiting for transfers between devices, butterfly_sum(): x = x + lax.ppermute(x, axis, pairs)  15.1 us
    ppermute x4, starting transfers between devices, butterfly_sum(): x = x + lax.ppermute(x, axis, pairs)  9.14 us
    ppermute x1, waiting for transfers between devices, padded_2(): before = lax.ppermute(last, axis, up)  7.92 us
    ppermute x1, waiting for transfers between devices, padded_2(): after = lax.ppermute(leading, axis, down)  6.69 us
    add x2, other arithmetic, update(): return middle + rate_field * (zsum + lateral(middle) - 6.0 * middle)  5.2 us
    dot_general x1, matrix products, per_device(): jnp.einsum('bzc,gzc->bg', direction_bank, fields, precision=lax.Precision...  3.45 us
  transfers between devices with their start and end apart: 11, of which 11 were waited for; matrix products, arithmetic and copies ran while one was open for 1% of the time, Pallas kernels for 0%

profile of v2, /device:TPU:8, one launch (start us, length us, event | category | flops | bytes accessed | tf_op | source)
XLA Modules:
  0.0 96.4 jit_solution(15520903510901731771)
XLA Ops:
  0.6 1.3 %select_reduce_fusion = f32[4,4096]{1,0:T(4,128)S(1)} fusion(f32[8]{0:T(128)} %param.9, s32[4,4096]{1,0:T(4,128)} %param.8), kind=kLoop, calls=%fused_computation.30 | loop fusion | flops 376832 | bytes 131104 | tf_op jit(solution)/shard_map/reduce_sum | solution.py:31
  1.9 1.5 %pad_maximum_fusion.7 = f32[18,4,4096]{2,1,0:T(4,128)S(1)} fusion(f32[1,4,4096]{2,1,0:T(4,128)S(1)} %get-tuple-element.8, f32[16,4,4096]{2,1,0:T(4,128)} %param.7, f32[1,4,4096]{2,1,0:T(4,128)} %bitcast.35), kind=kLoop, calls=%fused_computation.18 | loop fusion | flops 589824 | bytes 2359296 | tf_op jit(solution)/shard_map/concatenate | solution.py:89
  3.5 0.6 fusion.28
  4.5 2.1 %collective-permute-start.1 = (f32[18,2,4096]{2,0,1:T(8,128)S(1)}, f32[18,2,4096]{2,0,1:T(8,128)S(1)}, u32[]{:S(2)}, u32[]{:S(2)}) collective-permute-start(f32[18,2,4096]{2,0,1:T(8,128)S(1)} %copy.22), channel_id=1, source_target_pairs={{32,0},{64,32},{96,64},{128,96},{160,128},{192,160},{224,192},{256... | collective-permute-start | bytes 1769480 | tf_op jit(solution)/shard_map/ppermute | solution.py:21
  6.9 2.4 %collective-permute-start = (f32[18,2,4096]{2,0,1:T(8,128)S(1)}, f32[18,2,4096]{2,0,1:T(8,128)S(1)}, u32[]{:S(2)}, u32[]{:S(2)}) collective-permute-start(f32[18,2,4096]{2,0,1:T(8,128)S(1)} %copy.21), channel_id=1, source_target_pairs={{0,32},{32,64},{64,96},{96,128},{128,160},{160,192},{192,224},{224... | collective-permute-start | bytes 1769480 | tf_op jit(solution)/shard_map/ppermute | solution.py:20
  9.3 6.7 %collective-permute-done.1 = f32[18,2,4096]{2,0,1:T(8,128)S(1)} collective-permute-done((f32[18,2,4096]{2,0,1:T(8,128)S(1)}, f32[18,2,4096]{2,0,1:T(8,128)S(1)}, u32[]{:S(2)}, u32[]{:S(2)}) %collective-permute-start.1) | collective-permute-done | bytes 589856 | tf_op jit(solution)/shard_map/ppermute | solution.py:21
  16.5 7.9 %collective-permute-done = f32[18,2,4096]{2,0,1:T(8,128)S(1)} collective-permute-done((f32[18,2,4096]{2,0,1:T(8,128)S(1)}, f32[18,2,4096]{2,0,1:T(8,128)S(1)}, u32[]{:S(2)}, u32[]{:S(2)}) %collective-permute-start) | collective-permute-done | bytes 589856 | tf_op jit(solution)/shard_map/ppermute | solution.py:20
  24.9 0.8 pad_maximum_fusion
  26.0 2.7 %fusion.4 = f32[17,6,4096]{2,1,0:T(8,128)S(1)} fusion(f32[17,6,4096]{2,1,0:T(8,128)S(1)} %slice.175, f32[18,2,4096]{2,1,0:T(2,128)S(1)} %copy.23, f32[1,4,4096]{2,1,0:T(4,128)S(1)} %get-tuple-element.8, f32[16,4,4096]{2,1,0:T(4,128)S(1)} %copy-done.1, f32[1,4,4096]{2,1,0:T(4,128)S(1)} %bitcast.38, f32[18,2,4096]{2,1,0:T(2,128)S(1)} %copy.24, ...), kind=kLoop, calls=%fused_computation.6 | loop fusion | flops 7102464 | bytes 5808128 | tf_op jit(solution)/shard_map/add | solution.py:48
  29.0 2.5 %fusion.12 = f32[17,4,4096]{2,1,0:T(4,128)S(1)} fusion(f32[17,4,4096]{2,1,0:T(4,128)S(1)} %slice.176, f32[17,6,4096]{2,1,0:T(8,128)S(1)} %fusion.4, f32[4,4096]{1,0:T(4,128)S(1)} %get-tuple-element.7, pred[4096]{0:T(1024)(128)(4,1)S(1)} %get-tuple-element.9, pred[4096]{0:T(1024)(128)(4,1)S(1)} %get-tuple-element.10), kind=kLoop, calls=%fused_computation.23 | loop fusion | flops 3063808 | bytes 4530176 | tf_op jit(solution)/shard_map/add | solution.py:48
  31.5 3.4 %fusion.14 = f32[32,17]{0,1:T(8,128)S(1)} fusion(f32[32,4,4096]{2,1,0:T(4,128)S(1)} %copy-done, f32[17,4,4096]{2,1,0:T(4,128)S(1)} %fusion.12), kind=kOutput, calls=%fused_computation.27 | convolution fusion | flops 106954752 | bytes 3213440 | tf_op jit(solution)/shard_map/bzc,gzc->bg/dot_general | solution.py:97
  35.0 1.9 %collective-permute-start.2 = (f32[32,17]{0,1:T(8,128)S(1)}, f32[32,17]{0,1:T(8,128)S(1)}, u32[]{:S(2)}, u32[]{:S(2)}) collective-permute-start(f32[32,17]{0,1:T(8,128)S(1)} %fusion.14), channel_id=1, source_target_pairs={{0,32},{32,0},{64,96},{96,64},{128,160},{160,128},{192,224},{224,1... | collective-permute-start | bytes 6536 | tf_op jit(solution)/shard_map/ppermute | solution.py:63
  36.9 1.1 %collective-permute-done.2 = f32[32,17]{0,1:T(8,128)S(1)} collective-permute-done((f32[32,17]{0,1:T(8,128)S(1)}, f32[32,17]{0,1:T(8,128)S(1)}, u32[]{:S(2)}, u32[]{:S(2)}) %collective-permute-start.2) | collective-permute-done | bytes 2208 | tf_op jit(solution)/shard_map/ppermute | solution.py:63
  38.0 1.9 %collective-permute-start.3 = (f32[32,17]{0,1:T(8,128)S(1)}, f32[32,17]{0,1:T(8,128)S(1)}, u32[]{:S(2)}, u32[]{:S(2)}) collective-permute-start(f32[32,17]{0,1:T(8,128)S(1)} %add.145), channel_id=1, source_target_pairs={{0,64},{32,96},{64,0},{96,32},{128,192},{160,224},{192,128},{224,1... | collective-permute-start | bytes 6536 | tf_op jit(solution)/shard_map/ppermute | solution.py:63
  40.0 3.6 %collective-permute-done.3 = f32[32,17]{0,1:T(8,128)S(1)} collective-permute-done((f32[32,17]{0,1:T(8,128)S(1)}, f32[32,17]{0,1:T(8,128)S(1)}, u32[]{:S(2)}, u32[]{:S(2)}) %collective-permute-start.3) | collective-permute-done | bytes 2208 | tf_op jit(solution)/shard_map/ppermute | solution.py:63
  43.6 1.9 %collective-permute-start.4 = (f32[32,17]{0,1:T(8,128)S(1)}, f32[32,17]{0,1:T(8,128)S(1)}, u32[]{:S(2)}, u32[]{:S(2)}) collective-permute-start(f32[32,17]{0,1:T(8,128)S(1)} %add.146), channel_id=1, source_target_pairs={{0,128},{32,160},{64,192},{96,224},{128,0},{160,32},{192,64},{224,... | collective-permute-start | bytes 6536 | tf_op jit(solution)/shard_map/ppermute | solution.py:63
  45.8 4.3 %collective-permute-done.4 = f32[32,17]{0,1:T(8,128)S(1)} collective-permute-done((f32[32,17]{0,1:T(8,128)S(1)}, f32[32,17]{0,1:T(8,128)S(1)}, u32[]{:S(2)}, u32[]{:S(2)}) %collective-permute-start.4) | collective-permute-done | bytes 2208 | tf_op jit(solution)/shard_map/ppermute | solution.py:63
  50.1 3.4 %collective-permute-start.5 = (f32[32,17]{0,1:T(8,128)S(1)}, f32[32,17]{0,1:T(8,128)S(1)}, u32[]{:S(2)}, u32[]{:S(2)}) collective-permute-start(f32[32,17]{0,1:T(8,128)S(1)} %add.147), channel_id=1, source_target_pairs={{0,256},{32,288},{64,320},{96,352},{128,384},{160,416},{192,448},{... | collective-permute-start | bytes 6536 | tf_op jit(solution)/shard_map/ppermute | solution.py:63
  53.5 6.0 %collective-permute-done.5 = f32[32,17]{0,1:T(8,128)S(1)} collective-permute-done((f32[32,17]{0,1:T(8,128)S(1)}, f32[32,17]{0,1:T(8,128)S(1)}, u32[]{:S(2)}, u32[]{:S(2)}) %collective-permute-start.5) | collective-permute-done | bytes 2208 | tf_op jit(solution)/shard_map/ppermute | solution.py:63
  59.6 6.7 %collective-permute-start.6 = (f32[8224]{0:T(1024)S(1)}, f32[8224]{0:T(1024)S(1)}, u32[]{:S(2)}, u32[]{:S(2)}) collective-permute-start(f32[8224]{0:T(1024)S(1)} %pad_maximum_fusion.8), channel_id=1, source_target_pairs={{0,16},{1,17},{2,18},{3,19},{4,20},{5,21},{6,22},{7,23},{8,24},{9,... | collective-permute-start | bytes 98696 | tf_op jit(solution)/shard_map/ppermute | solution.py:80
  66.4 3.2 %collective-permute-done.6 = f32[8224]{0:T(1024)S(1)} collective-permute-done((f32[8224]{0:T(1024)S(1)}, f32[8224]{0:T(1024)S(1)}, u32[]{:S(2)}, u32[]{:S(2)}) %collective-permute-start.6) | collective-permute-done | bytes 32928 | tf_op jit(solution)/shard_map/ppermute | solution.py:80
  69.7 3.0 %collective-permute-start.7 = (f32[4128]{0:T(1024)S(1)}, f32[4128]{0:T(1024)S(1)}, u32[]{:S(2)}, u32[]{:S(2)}) collective-permute-start(f32[4128]{0:T(1024)S(1)} %pad_maximum_fusion.9), channel_id=1, source_target_pairs={{0,8},{1,9},{2,10},{3,11},{4,12},{5,13},{6,14},{7,15},{8,0},{9,1},... | collective-permute-start | bytes 49544 | tf_op jit(solution)/shard_map/ppermute | solution.py:80
  72.7 3.6 %collective-permute-done.7 = f32[4128]{0:T(1024)S(1)} collective-permute-done((f32[4128]{0:T(1024)S(1)}, f32[4128]{0:T(1024)S(1)}, u32[]{:S(2)}, u32[]{:S(2)}) %collective-permute-start.7) | collective-permute-done | bytes 16544 | tf_op jit(solution)/shard_map/ppermute | solution.py:80
  76.3 2.1 %collective-permute-start.8 = (f32[2080]{0:T(1024)S(1)}, f32[2080]{0:T(1024)S(1)}, u32[]{:S(2)}, u32[]{:S(2)}) collective-permute-start(f32[2080]{0:T(1024)S(1)} %pad_maximum_fusion.10), channel_id=1, source_target_pairs={{0,4},{1,5},{2,6},{3,7},{4,0},{5,1},{6,2},{7,3},{8,12},{9,13},{10,... | collective-permute-start | bytes 24968 | tf_op jit(solution)/shard_map/ppermute | solution.py:80
  78.4 3.5 %collective-permute-done.8 = f32[2080]{0:T(1024)S(1)} collective-permute-done((f32[2080]{0:T(1024)S(1)}, f32[2080]{0:T(1024)S(1)}, u32[]{:S(2)}, u32[]{:S(2)}) %collective-permute-start.8) | collective-permute-done | bytes 8352 | tf_op jit(solution)/shard_map/ppermute | solution.py:80
  82.0 3.7 %collective-permute-start.9 = (f32[1056]{0:T(1024)S(1)}, f32[1056]{0:T(1024)S(1)}, u32[]{:S(2)}, u32[]{:S(2)}) collective-permute-start(f32[1056]{0:T(1024)S(1)} %pad_maximum_fusion.11), channel_id=1, source_target_pairs={{0,2},{1,3},{2,0},{3,1},{4,6},{5,7},{6,4},{7,5},{8,10},{9,11},{10,... | collective-permute-start | bytes 12680 | tf_op jit(solution)/shard_map/ppermute | solution.py:80
  85.7 3.4 %collective-permute-done.9 = f32[1056]{0:T(1024)S(1)} collective-permute-done((f32[1056]{0:T(1024)S(1)}, f32[1056]{0:T(1024)S(1)}, u32[]{:S(2)}, u32[]{:S(2)}) %collective-permute-start.9) | collective-permute-done | bytes 4256 | tf_op jit(solution)/shard_map/ppermute | solution.py:80
  89.1 2.1 %collective-permute-start.10 = (f32[544]{0:T(1024)S(1)}, f32[544]{0:T(1024)S(1)}, u32[]{:S(2)}, u32[]{:S(2)}) collective-permute-start(f32[544]{0:T(1024)S(1)} %pad_maximum_fusion.12), channel_id=1, source_target_pairs={{0,1},{1,0},{2,3},{3,2},{4,5},{5,4},{6,7},{7,6},{8,9},{9,8},{10,11... | collective-permute-start | bytes 6536 | tf_op jit(solution)/shard_map/ppermute | solution.py:80
  91.3 3.4 %collective-permute-done.10 = f32[544]{0:T(1024)S(1)} collective-permute-done((f32[544]{0:T(1024)S(1)}, f32[544]{0:T(1024)S(1)}, u32[]{:S(2)}, u32[]{:S(2)}) %collective-permute-start.10) | collective-permute-done | bytes 2208 | tf_op jit(solution)/shard_map/ppermute | solution.py:80
  94.6 0.6 bitcast_add_fusion.1
  95.2 0.6 bitcast_subtract_fusion
  95.8 0.6 select_reduce_fusion.1
  (55 shorter events, 2.8 us)
Async XLA Ops:
  0.6 30.9 %copy-start = (f32[32,4,4096]{2,1,0:T(4,128)S(1)}, f32[32,4,4096]{2,1,0:T(4,128)}, u32[]{:S(2)}) copy-start(f32[32,4,4096]{2,1,0:T(4,128)} %param.10) | copy-start | bytes 6291460
  4.5 20.4 %copy-start.1 = (f32[16,4,4096]{2,1,0:T(4,128)S(1)}, f32[16,4,4096]{2,1,0:T(4,128)}, u32[]{:S(2)}) copy-start(f32[16,4,4096]{2,1,0:T(4,128)} %param.7) | copy-start | bytes 3145732
  4.5 20.4 %copy-start.2 = (f32[4,4096]{1,0:T(4,128)S(1)}, f32[4,4096]{1,0:T(4,128)}, u32[]{:S(2)}) copy-start(f32[4,4096]{1,0:T(4,128)} %param.6) | copy-start | bytes 196612
  4.5 11.5 %collective-permute-start.1 = (f32[18,2,4096]{2,0,1:T(8,128)S(1)}, f32[18,2,4096]{2,0,1:T(8,128)S(1)}, u32[]{:S(2)}, u32[]{:S(2)}) collective-permute-start(f32[18,2,4096]{2,0,1:T(8,128)S(1)} %copy.22), channel_id=1, source_target_pairs={{32,0},{64,32},{96,64},{128,96},{160,128},{192,160},{224,192},{256... | collective-permute-start | bytes 1769480 | tf_op jit(solution)/shard_map/ppermute | solution.py:21
  6.9 17.5 %collective-permute-start = (f32[18,2,4096]{2,0,1:T(8,128)S(1)}, f32[18,2,4096]{2,0,1:T(8,128)S(1)}, u32[]{:S(2)}, u32[]{:S(2)}) collective-permute-start(f32[18,2,4096]{2,0,1:T(8,128)S(1)} %copy.21), channel_id=1, source_target_pairs={{0,32},{32,64},{64,96},{96,128},{128,160},{160,192},{192,224},{224... | collective-permute-start | bytes 1769480 | tf_op jit(solution)/shard_map/ppermute | solution.py:20
  31.5 64.3 %copy-start.3 = (s32[128]{0:T(128)S(1)}, s32[128]{0:T(128)}, u32[]{:S(2)}) copy-start(s32[128]{0:T(128)} %param.11) | copy-start | bytes 1540
  35.0 3.1 %collective-permute-start.2 = (f32[32,17]{0,1:T(8,128)S(1)}, f32[32,17]{0,1:T(8,128)S(1)}, u32[]{:S(2)}, u32[]{:S(2)}) collective-permute-start(f32[32,17]{0,1:T(8,128)S(1)} %fusion.14), channel_id=1, source_target_pairs={{0,32},{32,0},{64,96},{96,64},{128,160},{160,128},{192,224},{224,1... | collective-permute-start | bytes 6536 | tf_op jit(solution)/shard_map/ppermute | solution.py:63
  38.0 5.6 %collective-permute-start.3 = (f32[32,17]{0,1:T(8,128)S(1)}, f32[32,17]{0,1:T(8,128)S(1)}, u32[]{:S(2)}, u32[]{:S(2)}) collective-permute-start(f32[32,17]{0,1:T(8,128)S(1)} %add.145), channel_id=1, source_target_pairs={{0,64},{32,96},{64,0},{96,32},{128,192},{160,224},{192,128},{224,1... | collective-permute-start | bytes 6536 | tf_op jit(solution)/shard_map/ppermute | solution.py:63
  43.6 6.5 %collective-permute-start.4 = (f32[32,17]{0,1:T(8,128)S(1)}, f32[32,17]{0,1:T(8,128)S(1)}, u32[]{:S(2)}, u32[]{:S(2)}) collective-permute-start(f32[32,17]{0,1:T(8,128)S(1)} %add.146), channel_id=1, source_target_pairs={{0,128},{32,160},{64,192},{96,224},{128,0},{160,32},{192,64},{224,... | collective-permute-start | bytes 6536 | tf_op jit(solution)/shard_map/ppermute | solution.py:63
  50.1 9.5 %collective-permute-start.5 = (f32[32,17]{0,1:T(8,128)S(1)}, f32[32,17]{0,1:T(8,128)S(1)}, u32[]{:S(2)}, u32[]{:S(2)}) collective-permute-start(f32[32,17]{0,1:T(8,128)S(1)} %add.147), channel_id=1, source_target_pairs={{0,256},{32,288},{64,320},{96,352},{128,384},{160,416},{192,448},{... | collective-permute-start | bytes 6536 | tf_op jit(solution)/shard_map/ppermute | solution.py:63
  59.6 10.0 %collective-permute-start.6 = (f32[8224]{0:T(1024)S(1)}, f32[8224]{0:T(1024)S(1)}, u32[]{:S(2)}, u32[]{:S(2)}) collective-permute-start(f32[8224]{0:T(1024)S(1)} %pad_maximum_fusion.8), channel_id=1, source_target_pairs={{0,16},{1,17},{2,18},{3,19},{4,20},{5,21},{6,22},{7,23},{8,24},{9,... | collective-permute-start | bytes 98696 | tf_op jit(solution)/shard_map/ppermute | solution.py:80
  69.7 6.6 %collective-permute-start.7 = (f32[4128]{0:T(1024)S(1)}, f32[4128]{0:T(1024)S(1)}, u32[]{:S(2)}, u32[]{:S(2)}) collective-permute-start(f32[4128]{0:T(1024)S(1)} %pad_maximum_fusion.9), channel_id=1, source_target_pairs={{0,8},{1,9},{2,10},{3,11},{4,12},{5,13},{6,14},{7,15},{8,0},{9,1},... | collective-permute-start | bytes 49544 | tf_op jit(solution)/shard_map/ppermute | solution.py:80
  76.3 5.6 %collective-permute-start.8 = (f32[2080]{0:T(1024)S(1)}, f32[2080]{0:T(1024)S(1)}, u32[]{:S(2)}, u32[]{:S(2)}) collective-permute-start(f32[2080]{0:T(1024)S(1)} %pad_maximum_fusion.10), channel_id=1, source_target_pairs={{0,4},{1,5},{2,6},{3,7},{4,0},{5,1},{6,2},{7,3},{8,12},{9,13},{10,... | collective-permute-start | bytes 24968 | tf_op jit(solution)/shard_map/ppermute | solution.py:80
  82.0 7.0 %collective-permute-start.9 = (f32[1056]{0:T(1024)S(1)}, f32[1056]{0:T(1024)S(1)}, u32[]{:S(2)}, u32[]{:S(2)}) collective-permute-start(f32[1056]{0:T(1024)S(1)} %pad_maximum_fusion.11), channel_id=1, source_target_pairs={{0,2},{1,3},{2,0},{3,1},{4,6},{5,7},{6,4},{7,5},{8,10},{9,11},{10,... | collective-permute-start | bytes 12680 | tf_op jit(solution)/shard_map/ppermute | solution.py:80
  89.1 5.5 %collective-permute-start.10 = (f32[544]{0:T(1024)S(1)}, f32[544]{0:T(1024)S(1)}, u32[]{:S(2)}, u32[]{:S(2)}) collective-permute-start(f32[544]{0:T(1024)S(1)} %pad_maximum_fusion.12), channel_id=1, source_target_pairs={{0,1},{1,0},{2,3},{3,2},{4,5},{5,4},{6,7},{7,6},{8,9},{9,8},{10,11... | collective-permute-start | bytes 6536 | tf_op jit(solution)/shard_map/ppermute | solution.py:80

commit v3 on v2

--- a/solution.py
+++ b/solution.py
@@ -55,33 +55,22 @@
     )
 
 
-def butterfly_sum(x, axis):
+def exchange_sum(x, axis):
     size = lax.axis_size(axis)
-    bit = 1
-    while bit < size:
-        pairs = [(i, i ^ bit) for i in range(size)]
-        x = x + lax.ppermute(x, axis, pairs)
-        bit *= 2
-    return x
+    copies = jnp.broadcast_to(x[None], (size,) + x.shape)
+    received = lax.all_to_all(copies, axis, 0, 0, tiled=False)
+    return jnp.sum(received, axis=0)
 
 
-def butterfly_scatter(x, extra, axis):
+def exchange_scatter(x, extra, axis):
     size = lax.axis_size(axis)
-    me = lax.axis_index(axis)
-    bit = size // 2
-    while bit >= 1:
-        half = x.shape[1] // 2
-        lo, hi = x[:, :half], x[:, half:]
-        upper = (me // bit) % 2 == 1
-        keep = jnp.where(upper, hi, lo)
-        send = jnp.where(upper, lo, hi)
-        pairs = [(i, i ^ bit) for i in range(size)]
-        message = jnp.concatenate([send.reshape(-1), extra])
-        got = lax.ppermute(message, axis, pairs)
-        x = keep + got[: send.size].reshape(send.shape)
-        extra = extra + got[send.size :]
-        bit //= 2
-    return x, extra
+    rows, cols = x.shape
+    width = cols // size
+    blocks = x.reshape(rows, size, width).transpose(1, 0, 2).reshape(size, rows * width)
+    extras = jnp.broadcast_to(extra[None], (size, extra.shape[0]))
+    message = jnp.concatenate([blocks, extras], axis=1)
+    received = jnp.sum(lax.all_to_all(message, axis, 0, 0, tiled=True), axis=0)
+    return received[: rows * width].reshape(rows, width), received[rows * width :]
 
 
 def per_device(center, generators, conductivity, cond_table, direction_bank, selection):
@@ -97,10 +86,10 @@
     all_proj = jnp.einsum(
         "bzc,gzc->bg", direction_bank, fields, precision=lax.Precision.HIGHEST
     )
-    summed = butterfly_sum(all_proj, "slab")
+    summed = exchange_sum(all_proj, "slab")
     summed_centre, summed_proj = summed[:, 0], summed[:, 1:]
     partial_value = jnp.sum(jnp.abs(summed_proj), axis=1)
-    radius, magnitude = butterfly_scatter(radius_local, partial_value, "gen")
+    radius, magnitude = exchange_scatter(radius_local, partial_value, "gen")
     columns = radius.shape[1]
     centre_cols = lax.dynamic_slice_in_dim(
         centre_moved, lax.axis_index("gen") * columns, columns, 1

time: 96.8 us -> 74.6 us (0.77)
  the two profiles are of different devices: /device:TPU:8 before, /device:TPU:1 now
where the time goes in v3:
time: 74.6 us; the launch traced here: 74.3 us
  starting transfers between devices  30.6 us (41%)
  waiting for transfers between devices  23.4 us (31%)
  other arithmetic  11.2 us (15%)
  local copies, waits for them, and re-layouts  4.89 us (7%)
  matrix products  3.45 us (5%)
  between operations  0.87 us (1%)
    all_to_all x1, starting transfers between devices, exchange_scatter(): received = jnp.sum(lax.all_to_all(message, axis, 0, 0, tiled=True), axis=0)  12.9 us
    all_to_all x1, waiting for transfers between devices, exchange_scatter(): received = jnp.sum(lax.all_to_all(message, axis, 0, 0, tiled=True), axis=0)  8.94 us
    all_to_all x1, starting transfers between devices, exchange_sum(): received = lax.all_to_all(copies, axis, 0, 0, tiled=False)  7.43 us
    all_to_all x1, waiting for transfers between devices, exchange_sum(): received = lax.all_to_all(copies, axis, 0, 0, tiled=False)  7.13 us
    ppermute x1, starting transfers between devices, padded_2(): after = lax.ppermute(leading, axis, down)  5.53 us
    add x2, other arithmetic, update(): return middle + rate_field * (zsum + lateral(middle) - 6.0 * middle)  5.2 us
    ppermute x1, starting transfers between devices, padded_2(): before = lax.ppermute(last, axis, up)  4.73 us
    ppermute x1, waiting for transfers between devices, padded_2(): after = lax.ppermute(leading, axis, down)  4.3 us
  transfers between devices with their start and end apart: 4, of which 4 were waited for; matrix products, arithmetic and copies ran while one was open for 1% of the time, Pallas kernels for 0%

profile of v3, /device:TPU:1, one launch (start us, length us, event | category | flops | bytes accessed | tf_op | source)
XLA Modules:
  0.0 74.3 jit_solution(8261318318384641906)
XLA Ops:
  0.6 0.0 copy-start
  0.6 1.3 %select_reduce_fusion = f32[4,4096]{1,0:T(4,128)S(1)} fusion(f32[8]{0:T(128)} %param.9, s32[4,4096]{1,0:T(4,128)} %param.8), kind=kLoop, calls=%fused_computation.30 | loop fusion | flops 376832 | bytes 131104 | tf_op jit(solution)/shard_map/reduce_sum | solution.py:31
  1.9 1.5 %pad_maximum_fusion.7 = f32[18,4,4096]{2,1,0:T(4,128)S(1)} fusion(f32[1,4,4096]{2,1,0:T(4,128)S(1)} %get-tuple-element.8, f32[16,4,4096]{2,1,0:T(4,128)} %param.7, f32[1,4,4096]{2,1,0:T(4,128)} %bitcast.32), kind=kLoop, calls=%fused_computation.18 | loop fusion | flops 589824 | bytes 2359296 | tf_op jit(solution)/shard_map/concatenate | solution.py:78
  3.5 0.6 fusion.28
  4.1 0.4 copy.27
  4.5 4.7 %collective-permute-start = (f32[18,2,4096]{2,0,1:T(8,128)S(1)}, f32[18,2,4096]{2,0,1:T(8,128)S(1)}, u32[]{:S(2)}, u32[]{:S(2)}) collective-permute-start(f32[18,2,4096]{2,0,1:T(8,128)S(1)} %copy.27), channel_id=1, source_target_pairs={{0,32},{32,64},{64,96},{96,128},{128,160},{160,192},{192,224},{224... | collective-permute-start | bytes 1769480 | tf_op jit(solution)/shard_map/ppermute | solution.py:20
  9.2 0.4 copy.28
  9.6 5.5 %collective-permute-start.1 = (f32[18,2,4096]{2,0,1:T(8,128)S(1)}, f32[18,2,4096]{2,0,1:T(8,128)S(1)}, u32[]{:S(2)}, u32[]{:S(2)}) collective-permute-start(f32[18,2,4096]{2,0,1:T(8,128)S(1)} %copy.28), channel_id=1, source_target_pairs={{32,0},{64,32},{96,64},{128,96},{160,128},{192,160},{224,192},{256... | collective-permute-start | bytes 1769480 | tf_op jit(solution)/shard_map/ppermute | solution.py:21
  15.1 3.0 %collective-permute-done = f32[18,2,4096]{2,0,1:T(8,128)S(1)} collective-permute-done((f32[18,2,4096]{2,0,1:T(8,128)S(1)}, f32[18,2,4096]{2,0,1:T(8,128)S(1)}, u32[]{:S(2)}, u32[]{:S(2)}) %collective-permute-start) | collective-permute-done | bytes 589856 | tf_op jit(solution)/shard_map/ppermute | solution.py:20
  18.1 0.5 copy.29
  18.6 4.3 %collective-permute-done.1 = f32[18,2,4096]{2,0,1:T(8,128)S(1)} collective-permute-done((f32[18,2,4096]{2,0,1:T(8,128)S(1)}, f32[18,2,4096]{2,0,1:T(8,128)S(1)}, u32[]{:S(2)}, u32[]{:S(2)}) %collective-permute-start.1) | collective-permute-done | bytes 589856 | tf_op jit(solution)/shard_map/ppermute | solution.py:21
  22.9 0.5 copy.30
  23.4 0.8 %pad_maximum_fusion = f32[18,8,4096]{2,1,0:T(8,128)S(1)} fusion(f32[18,2,4096]{2,1,0:T(2,128)S(1)} %copy.30, f32[1,4,4096]{2,1,0:T(4,128)S(1)} %get-tuple-element.8, f32[16,4,4096]{2,1,0:T(4,128)S(1)} %copy-done.1, f32[1,4,4096]{2,1,0:T(4,128)S(1)} %bitcast.33, f32[18,2,4096]{2,1,0:T(2,128)S(1)} %copy.29), kind=kLoop, calls=%fused_computation | loop fusion | flops 2359296 | bytes 4718592 | tf_op jit(solution)/shard_map/concatenate | solution.py:22
  24.2 0.1 maximum_bitcast_fusion
  24.2 0.2 slice.103
  24.4 2.7 %fusion.4 = f32[17,6,4096]{2,1,0:T(8,128)S(1)} fusion(f32[17,6,4096]{2,1,0:T(8,128)S(1)} %slice.103, f32[18,2,4096]{2,1,0:T(2,128)S(1)} %copy.29, f32[1,4,4096]{2,1,0:T(4,128)S(1)} %get-tuple-element.8, f32[16,4,4096]{2,1,0:T(4,128)S(1)} %copy-done.1, f32[1,4,4096]{2,1,0:T(4,128)S(1)} %bitcast.35, f32[18,2,4096]{2,1,0:T(2,128)S(1)} %copy.30, ...), kind=kLoop, calls=%fused_computation.6 | loop fusion | flops 7102464 | bytes 5808128 | tf_op jit(solution)/shard_map/add | solution.py:48
  27.1 0.3 slice.104
  27.4 2.5 %fusion.12 = f32[17,4,4096]{2,1,0:T(4,128)S(1)} fusion(f32[17,4,4096]{2,1,0:T(4,128)S(1)} %slice.104, f32[17,6,4096]{2,1,0:T(8,128)S(1)} %fusion.4, f32[4,4096]{1,0:T(4,128)S(1)} %get-tuple-element.7, pred[4096]{0:T(1024)(128)(4,1)S(1)} %get-tuple-element.9, pred[4096]{0:T(1024)(128)(4,1)S(1)} %get-tuple-element.10), kind=kLoop, calls=%fused_computation.23 | loop fusion | flops 3063808 | bytes 4530176 | tf_op jit(solution)/shard_map/add | solution.py:48
  30.0 3.4 %fusion.14 = f32[32,17]{0,1:T(8,128)S(1)} fusion(f32[32,4,4096]{2,1,0:T(4,128)S(1)} %copy-done, f32[17,4,4096]{2,1,0:T(4,128)S(1)} %fusion.12), kind=kOutput, calls=%fused_computation.27 | convolution fusion | flops 106954752 | bytes 3213440 | tf_op jit(solution)/shard_map/bzc,gzc->bg/dot_general | solution.py:86
  33.5 0.7 reshape.40
  34.2 7.4 %all-to-all-start = ((f32[16,1,544]{2,1,0:T(1,128)}), f32[16,1,544]{2,1,0:T(1,128)S(1)}, u32[]{:S(2)}, u32[]{:S(2)}) async-start(f32[16,1,544]{2,1,0:T(1,128)} %reshape.40), calls=%async_computation | async-start | bytes 81920 | tf_op jit(solution)/shard_map/all_to_all | solution.py:61
  41.6 0.3 fusion.19
  41.9 7.1 %all-to-all-done = f32[16,1,544]{2,1,0:T(1,128)S(1)} async-done(((f32[16,1,544]{2,1,0:T(1,128)}), f32[16,1,544]{2,1,0:T(1,128)S(1)}, u32[]{:S(2)}, u32[]{:S(2)}) %all-to-all-start) | async-done | bytes 34848 | tf_op jit(solution)/shard_map/all_to_all | solution.py:61
  49.0 0.5 broadcast.30
  49.6 0.7 reduce.1
  50.3 0.1 reshape.41
  50.5 0.7 copy.35
  51.2 12.9 %all-to-all-start.1 = ((f32[32,1,544]{2,1,0:T(1,128)}), f32[32,1,544]{2,1,0:T(1,128)S(1)}, u32[]{:S(2)}, u32[]{:S(2)}) async-start(f32[32,1,544]{2,1,0:T(1,128)} %copy.35), calls=%async_computation.1 | async-start | bytes 163840 | tf_op jit(solution)/shard_map/all_to_all | solution.py:72
  64.1 8.9 %all-to-all-done.1 = f32[32,1,544]{2,1,0:T(1,128)S(1)} async-done(((f32[32,1,544]{2,1,0:T(1,128)}), f32[32,1,544]{2,1,0:T(1,128)S(1)}, u32[]{:S(2)}, u32[]{:S(2)}) %all-to-all-start.1) | async-done | bytes 69664 | tf_op jit(solution)/shard_map/all_to_all | solution.py:72
  73.0 0.1 reduce_sum.58
  73.1 0.6 select_reduce_fusion.1
  73.7 0.6 bitcast_add_fusion
  (17 shorter events, 0.2 us)
Async XLA Ops:
  0.6 29.3 %copy-start = (f32[32,4,4096]{2,1,0:T(4,128)S(1)}, f32[32,4,4096]{2,1,0:T(4,128)}, u32[]{:S(2)}) copy-start(f32[32,4,4096]{2,1,0:T(4,128)} %param.10) | copy-start | bytes 6291460
  4.5 18.9 %copy-start.1 = (f32[16,4,4096]{2,1,0:T(4,128)S(1)}, f32[16,4,4096]{2,1,0:T(4,128)}, u32[]{:S(2)}) copy-start(f32[16,4,4096]{2,1,0:T(4,128)} %param.7) | copy-start | bytes 3145732
  4.5 18.9 %copy-start.2 = (f32[4,4096]{1,0:T(4,128)S(1)}, f32[4,4096]{1,0:T(4,128)}, u32[]{:S(2)}) copy-start(f32[4,4096]{1,0:T(4,128)} %param.6) | copy-start | bytes 196612
  4.5 13.6 %collective-permute-start = (f32[18,2,4096]{2,0,1:T(8,128)S(1)}, f32[18,2,4096]{2,0,1:T(8,128)S(1)}, u32[]{:S(2)}, u32[]{:S(2)}) collective-permute-start(f32[18,2,4096]{2,0,1:T(8,128)S(1)} %copy.27), channel_id=1, source_target_pairs={{0,32},{32,64},{64,96},{96,128},{128,160},{160,192},{192,224},{224... | collective-permute-start | bytes 1769480 | tf_op jit(solution)/shard_map/ppermute | solution.py:20
  9.6 13.3 %collective-permute-start.1 = (f32[18,2,4096]{2,0,1:T(8,128)S(1)}, f32[18,2,4096]{2,0,1:T(8,128)S(1)}, u32[]{:S(2)}, u32[]{:S(2)}) collective-permute-start(f32[18,2,4096]{2,0,1:T(8,128)S(1)} %copy.28), channel_id=1, source_target_pairs={{32,0},{64,32},{96,64},{128,96},{160,128},{192,160},{224,192},{256... | collective-permute-start | bytes 1769480 | tf_op jit(solution)/shard_map/ppermute | solution.py:21
  33.4 39.7 %copy-start.3 = (s32[128]{0:T(128)S(1)}, s32[128]{0:T(128)}, u32[]{:S(2)}) copy-start(s32[128]{0:T(128)} %param.11) | copy-start | bytes 1540
  34.2 14.8 %all-to-all-start = ((f32[16,1,544]{2,1,0:T(1,128)}), f32[16,1,544]{2,1,0:T(1,128)S(1)}, u32[]{:S(2)}, u32[]{:S(2)}) async-start(f32[16,1,544]{2,1,0:T(1,128)} %reshape.40), calls=%async_computation | async-start | bytes 81920 | tf_op jit(solution)/shard_map/all_to_all | solution.py:61
  51.2 21.8 %all-to-all-start.1 = ((f32[32,1,544]{2,1,0:T(1,128)}), f32[32,1,544]{2,1,0:T(1,128)S(1)}, u32[]{:S(2)}, u32[]{:S(2)}) async-start(f32[32,1,544]{2,1,0:T(1,128)} %copy.35), calls=%async_computation.1 | async-start | bytes 163840 | tf_op jit(solution)/shard_map/all_to_all | solution.py:72

commit v4 on v3

--- a/solution.py
+++ b/solution.py
@@ -75,16 +75,24 @@
 
 def per_device(center, generators, conductivity, cond_table, direction_bank, selection):
     rate_field = lookup_rate(conductivity, cond_table)
-    packed = jnp.concatenate([center[None], generators, rate_field[None]], axis=0)
-    extended = padded_2(packed, (("slab", 1),), 2)
-    fields, rate_ext = extended[:-1], extended[-1]
-    fields = update(fields, rate_ext[1:-1])
+    body = jnp.concatenate([center[None], generators], axis=0)
+    size = lax.axis_size("slab")
+    up = [(i, i + 1) for i in range(size - 1)]
+    down = [(j, i) for i, j in up]
+    planes = body.shape[1]
+    lower = jnp.concatenate([body[:, :2], rate_field[None, :2]], axis=0)
+    upper = jnp.concatenate([body[:, planes - 2 :], rate_field[None, planes - 2 :]], axis=0)
+    before = lax.ppermute(upper, "slab", up)
+    after = lax.ppermute(lower, "slab", down)
+    fields = jnp.concatenate([before[:-1], body, after[:-1]], axis=1)
+    rate_ext = jnp.concatenate([before[-1, 1:], rate_field, after[-1, :1]], axis=0)
+    fields = update(fields, rate_ext)
     fields = update(fields, rate_field)
     centre_moved = fields[0]
     gens_moved = fields[1:]
     radius_local = jnp.sum(jnp.abs(gens_moved), axis=0)
     all_proj = jnp.einsum(
-        "bzc,gzc->bg", direction_bank, fields, precision=lax.Precision.HIGHEST
+        "bzc,gzc->bg", direction_bank, fields, precision=lax.Precision.HIGH
     )
     summed = exchange_sum(all_proj, "slab")
     summed_centre, summed_proj = summed[:, 0], summed[:, 1:]

time: 74.6 us -> 72.6 us (0.973)
  local copies, waits for them, and re-layouts: 4.89 us -> 7.48 us
  waiting for transfers between devices: 23.4 us -> 21.3 us
  matrix products: 3.45 us -> 2.13 us
  other arithmetic: 11.2 us -> 9.92 us
    unnamed x12 -> x11, local copies, waits for them, and re-layouts: 0.88 us -> 4.01 us
    concatenate x2 -> x5, other arithmetic: 2.31 us -> 0.57 us  [the longest x1 0.25 us: per_device(): fields = jnp.concatenate([before[:-1], body, after[:-1]], axis=1)]
    all_to_all x1, waiting for transfers between devices: 7.13 us -> 5.72 us  [exchange_sum(): received = lax.all_to_all(copies, axis, 0, 0, tiled=False)]
    reduce_sum x1, other arithmetic: 0.27 us -> 1.68 us  [per_device(): radius_local = jnp.sum(jnp.abs(gens_moved), axis=0)]
    slice x3 -> x0, local copies, waits for them, and re-layouts: 1.34 us -> none  [the longest x2 0.98 us: padded_2(): last = lax.slice_in_dim(x, length - width, length, axis=dim)]
    dot_general x1, matrix products: 3.45 us -> 2.13 us  [per_device(): jnp.einsum('bzc,gzc->bg', direction_bank, fields, precision=lax.Precision...]
    all_to_all x1, waiting for transfers between devices: 8.94 us -> 7.85 us  [exchange_scatter(): received = jnp.sum(lax.all_to_all(message, axis, 0, 0, tiled=True), axis=0)]
    slice x1, local copies, waits for them, and re-layouts: 0.01 us -> 1.08 us  [per_device(): centre_moved = fields[0]]
  transfers between devices with their start and end apart: 4 -> 4, of which waited for: 4 -> 4; matrix products, arithmetic and copies ran while one was open for 1% -> 4% of each run, Pallas kernels for 0% -> 0%
where the time goes in v4:
time: 72.6 us; the launch traced here: 72.2 us
  starting transfers between devices  30.4 us (42%)
  waiting for transfers between devices  21.3 us (29%)
  other arithmetic  9.92 us (14%)
  local copies, waits for them, and re-layouts  7.48 us (10%)
  matrix products  2.13 us (3%)
  between operations  0.87 us (1%)
    all_to_all x1, starting transfers between devices, exchange_scatter(): received = jnp.sum(lax.all_to_all(message, axis, 0, 0, tiled=True), axis=0)  12.9 us
    all_to_all x1, waiting for transfers between devices, exchange_scatter(): received = jnp.sum(lax.all_to_all(message, axis, 0, 0, tiled=True), axis=0)  7.85 us
    all_to_all x1, starting transfers between devices, exchange_sum(): received = lax.all_to_all(copies, axis, 0, 0, tiled=False)  7.43 us
    all_to_all x1, waiting for transfers between devices, exchange_sum(): received = lax.all_to_all(copies, axis, 0, 0, tiled=False)  5.72 us
    ppermute x1, starting transfers between devices, per_device(): after = lax.ppermute(lower, 'slab', down)  5.53 us
    ppermute x1, starting transfers between devices, per_device(): before = lax.ppermute(upper, 'slab', up)  4.59 us
    ppermute x1, waiting for transfers between devices, per_device(): after = lax.ppermute(lower, 'slab', down)  4.56 us
    add x2, other arithmetic, update(): return middle + rate_field * (zsum + lateral(middle) - 6.0 * middle)  4.48 us
  transfers between devices with their start and end apart: 4, of which 4 were waited for; matrix products, arithmetic and copies ran while one was open for 4% of the time, Pallas kernels for 0%

profile of v4, /device:TPU:1, one launch (start us, length us, event | category | flops | bytes accessed | tf_op | source)
XLA Modules:
  0.0 72.2 jit_solution(10778145080812645770)
XLA Ops:
  0.6 0.0 copy-start
  0.6 2.0 %copy.31 = f32[16,4,4096]{2,0,1:T(8,128)S(1)} copy(f32[16,4,4096]{2,1,0:T(4,128)} %param.7) | data formatting | bytes 2097152 | tf_op args[1]
  2.6 0.9 %copy.30 = f32[1,4,4096]{2,0,1:T(1,128)S(1)} copy(f32[1,4,4096]{2,1,0:T(4,128)} %bitcast.43) | data formatting | bytes 131072 | tf_op jit(solution)/shard_map/broadcast_in_dim | solution.py:78
  3.5 1.1 %select_reduce_fusion = f32[4,4096]{1,0:T(4,128)S(1)} fusion(f32[8]{0:T(128)} %param.9, s32[4,4096]{1,0:T(4,128)} %param.8), kind=kLoop, calls=%fused_computation.30 | loop fusion | flops 376832 | bytes 131104 | tf_op jit(solution)/shard_map/reduce_sum | solution.py:31
  4.8 0.1 fusion.16
  4.8 0.1 pad_maximum_fusion.4
  4.9 4.6 %collective-permute-start = (f32[18,2,4096]{2,0,1:T(8,128)S(1)}, f32[18,2,4096]{2,0,1:T(8,128)S(1)}, u32[]{:S(2)}, u32[]{:S(2)}) collective-permute-start(f32[18,2,4096]{2,0,1:T(8,128)S(1)} %pad_maximum_fusion.4), channel_id=1, source_target_pairs={{0,32},{32,64},{64,96},{96,128},{128,160},{160,192},{192,224},{224... | collective-permute-start | bytes 1769480 | tf_op jit(solution)/shard_map/ppermute | solution.py:85
  9.6 0.1 fusion.17
  9.7 5.5 %collective-permute-start.1 = (f32[18,2,4096]{2,0,1:T(8,128)S(1)}, f32[18,2,4096]{2,0,1:T(8,128)S(1)}, u32[]{:S(2)}, u32[]{:S(2)}) collective-permute-start(f32[18,2,4096]{2,0,1:T(8,128)S(1)} %fusion.17), channel_id=1, source_target_pairs={{32,0},{64,32},{96,64},{128,96},{160,128},{192,160},{224,192},{256... | collective-permute-start | bytes 1769480 | tf_op jit(solution)/shard_map/ppermute | solution.py:86
  15.3 3.2 %collective-permute-done = f32[18,2,4096]{2,0,1:T(8,128)S(1)} collective-permute-done((f32[18,2,4096]{2,0,1:T(8,128)S(1)}, f32[18,2,4096]{2,0,1:T(8,128)S(1)}, u32[]{:S(2)}, u32[]{:S(2)}) %collective-permute-start) | collective-permute-done | bytes 589856 | tf_op jit(solution)/shard_map/ppermute | solution.py:85
  18.4 4.6 %collective-permute-done.1 = f32[18,2,4096]{2,0,1:T(8,128)S(1)} collective-permute-done((f32[18,2,4096]{2,0,1:T(8,128)S(1)}, f32[18,2,4096]{2,0,1:T(8,128)S(1)}, u32[]{:S(2)}, u32[]{:S(2)}) %collective-permute-start.1) | collective-permute-done | bytes 589856 | tf_op jit(solution)/shard_map/ppermute | solution.py:86
  23.0 0.3 pad_maximum_fusion
  23.4 2.8 %fusion.3 = f32[17,6,4096]{2,0,1:T(8,128)S(1)} fusion(f32[17,6,4096]{2,0,1:T(8,128)S(1)} %pad_maximum_fusion, f32[17,2,4096]{2,0,1:T(8,128)S(1)} %bitcast.40, f32[16,4,4096]{2,0,1:T(8,128)S(1)} %copy.31, f32[1,4,4096]{2,0,1:T(1,128)S(1)} %copy.30, f32[17,2,4096]{2,0,1:T(8,128)S(1)} %bitcast.38, f32[6,4096]{1,0:T(8,128)S(1)} %pad_maximum_fusion.5, ...), kind=kLoop, calls=%fused_computation.7 | loop fusion | flops 6266880 | bytes 5677056 | tf_op jit(solution)/shard_map/add | solution.py:48
  26.2 0.1 slice.116
  26.3 1.7 %fusion.10 = f32[17,4,4096]{2,0,1:T(8,128)S(1)} fusion(f32[17,4,4096]{2,0,1:T(8,128)S(1)} %slice.116, f32[17,6,4096]{2,0,1:T(8,128)S(1)} %fusion.3, f32[4,4096]{1,0:T(4,128)S(1)} %broadcast_multiply_fusion, pred[4096]{0:T(1024)(128)(4,1)S(1)} %get-tuple-element.7, pred[4096]{0:T(1024)(128)(4,1)S(1)} %get-tuple-element.8), kind=kLoop, calls=%fused_computation.17 | loop fusion | flops 3063808 | bytes 4530176 | tf_op jit(solution)/shard_map/add | solution.py:48
  28.0 1.1 %copy-done.1 = f32[17,4,4096]{2,0,1:T(8,128)} copy-done((f32[17,4,4096]{2,0,1:T(8,128)}, f32[17,4,4096]{2,0,1:T(8,128)S(1)}, u32[]{:S(2)}) %copy-start.1) | copy-done | bytes 1114136
  29.1 2.1 %fusion.12 = f32[32,17]{0,1:T(8,128)S(1)} fusion(f32[17,4,4096]{2,0,1:T(8,128)S(1)} %fusion.10, f32[32,4,4096]{2,1,0:T(4,128)S(1)} %copy-done), kind=kOutput, calls=%fused_computation.23 | convolution fusion | flops 53477376 | bytes 3213440 | tf_op jit(solution)/shard_map/bzc,gzc->bg/dot_general | solution.py:94
  31.3 0.0 copy-start.2
  31.3 0.7 %reshape.33 = f32[16,1,544]{2,1,0:T(1,128)} reshape(f32[16,17,32]{2,1,0:T(8,128)S(1)} %broadcast_bitcast_fusion) | data formatting | bytes 69632
  32.1 7.4 %all-to-all-start = ((f32[16,1,544]{2,1,0:T(1,128)}), f32[16,1,544]{2,1,0:T(1,128)S(1)}, u32[]{:S(2)}, u32[]{:S(2)}) async-start(f32[16,1,544]{2,1,0:T(1,128)} %reshape.33), calls=%async_computation | async-start | bytes 81920 | tf_op jit(solution)/shard_map/all_to_all | solution.py:61
  39.5 1.7 %fusion.15 = f32[4,4096]{1,0:T(4,128)S(1)} fusion(f32[17,4,4096]{2,0,1:T(8,128)} %copy-done.1), kind=kLoop, calls=%fused_computation.25 | loop fusion | flops 507904 | bytes 1114112 | tf_op jit(solution)/shard_map/reduce_sum | solution.py:93
  41.2 5.7 %all-to-all-done = f32[16,1,544]{2,1,0:T(1,128)S(1)} async-done(((f32[16,1,544]{2,1,0:T(1,128)}), f32[16,1,544]{2,1,0:T(1,128)S(1)}, u32[]{:S(2)}, u32[]{:S(2)}) %all-to-all-start) | async-done | bytes 34848 | tf_op jit(solution)/shard_map/all_to_all | solution.py:61
  46.9 0.5 broadcast.25
  47.4 0.7 %reduce.1 = f32[16,544]{1,0:T(8,128)S(1)} reduce(f32[16,1,544]{2,1,0:T(1,128)S(1)} %all-to-all-done, f32[]{:T(128)} %broadcast.25), dimensions={1}, to_apply=%all_to_all.9.reduce_sub_computation | reduce | bytes 69636 | tf_op jit(solution)/shard_map/all_to_all | solution.py:61
  48.2 0.1 reshape.34
  48.3 0.7 copy.35
  49.1 12.9 %all-to-all-start.1 = ((f32[32,1,544]{2,1,0:T(1,128)}), f32[32,1,544]{2,1,0:T(1,128)S(1)}, u32[]{:S(2)}, u32[]{:S(2)}) async-start(f32[32,1,544]{2,1,0:T(1,128)} %copy.35), calls=%async_computation.1 | async-start | bytes 163840 | tf_op jit(solution)/shard_map/all_to_all | solution.py:72
  61.9 1.1 %slice.119 = f32[1,4,4096]{2,0,1:T(1,128)S(1)} slice(f32[17,4,4096]{2,0,1:T(8,128)} %copy-done.1), slice={[0:1], [0:4], [0:4096]} | slice | bytes 131072 | tf_op jit(solution)/shard_map/slice | solution.py:91
  63.1 7.8 %all-to-all-done.1 = f32[32,1,544]{2,1,0:T(1,128)S(1)} async-done(((f32[32,1,544]{2,1,0:T(1,128)}), f32[32,1,544]{2,1,0:T(1,128)S(1)}, u32[]{:S(2)}, u32[]{:S(2)}) %all-to-all-start.1) | async-done | bytes 69664 | tf_op jit(solution)/shard_map/all_to_all | solution.py:72
  70.9 0.1 reduce_sum.58
  71.0 0.6 bitcast_add_fusion
  71.6 0.6 select_reduce_fusion.1
  (19 shorter events, 0.3 us)
Async XLA Ops:
  0.6 28.5 %copy-start = (f32[32,4,4096]{2,1,0:T(4,128)S(1)}, f32[32,4,4096]{2,1,0:T(4,128)}, u32[]{:S(2)}) copy-start(f32[32,4,4096]{2,1,0:T(4,128)} %param.10) | copy-start | bytes 6291460
  4.9 13.5 %collective-permute-start = (f32[18,2,4096]{2,0,1:T(8,128)S(1)}, f32[18,2,4096]{2,0,1:T(8,128)S(1)}, u32[]{:S(2)}, u32[]{:S(2)}) collective-permute-start(f32[18,2,4096]{2,0,1:T(8,128)S(1)} %pad_maximum_fusion.4), channel_id=1, source_target_pairs={{0,32},{32,64},{64,96},{96,128},{128,160},{160,192},{192,224},{224... | collective-permute-start | bytes 1769480 | tf_op jit(solution)/shard_map/ppermute | solution.py:85
  9.7 13.3 %collective-permute-start.1 = (f32[18,2,4096]{2,0,1:T(8,128)S(1)}, f32[18,2,4096]{2,0,1:T(8,128)S(1)}, u32[]{:S(2)}, u32[]{:S(2)}) collective-permute-start(f32[18,2,4096]{2,0,1:T(8,128)S(1)} %fusion.17), channel_id=1, source_target_pairs={{32,0},{64,32},{96,64},{128,96},{160,128},{192,160},{224,192},{256... | collective-permute-start | bytes 1769480 | tf_op jit(solution)/shard_map/ppermute | solution.py:86
  28.0 1.2 %copy-start.1 = (f32[17,4,4096]{2,0,1:T(8,128)}, f32[17,4,4096]{2,0,1:T(8,128)S(1)}, u32[]{:S(2)}) copy-start(f32[17,4,4096]{2,0,1:T(8,128)S(1)} %fusion.10) | copy-start | bytes 3342340
  31.3 40.3 %copy-start.2 = (s32[128]{0:T(128)S(1)}, s32[128]{0:T(128)}, u32[]{:S(2)}) copy-start(s32[128]{0:T(128)} %param.11) | copy-start | bytes 1540
  32.1 14.8 %all-to-all-start = ((f32[16,1,544]{2,1,0:T(1,128)}), f32[16,1,544]{2,1,0:T(1,128)S(1)}, u32[]{:S(2)}, u32[]{:S(2)}) async-start(f32[16,1,544]{2,1,0:T(1,128)} %reshape.33), calls=%async_computation | async-start | bytes 81920 | tf_op jit(solution)/shard_map/all_to_all | solution.py:61
  49.1 21.8 %all-to-all-start.1 = ((f32[32,1,544]{2,1,0:T(1,128)}), f32[32,1,544]{2,1,0:T(1,128)S(1)}, u32[]{:S(2)}, u32[]{:S(2)}) async-start(f32[32,1,544]{2,1,0:T(1,128)} %copy.35), calls=%async_computation.1 | async-start | bytes 163840 | tf_op jit(solution)/shard_map/all_to_all | solution.py:72

commit v5 on v4

--- a/solution.py
+++ b/solution.py
@@ -75,15 +75,20 @@
 
 def per_device(center, generators, conductivity, cond_table, direction_bank, selection):
     rate_field = lookup_rate(conductivity, cond_table)
-    body = jnp.concatenate([center[None], generators], axis=0)
     size = lax.axis_size("slab")
     up = [(i, i + 1) for i in range(size - 1)]
     down = [(j, i) for i, j in up]
-    planes = body.shape[1]
-    lower = jnp.concatenate([body[:, :2], rate_field[None, :2]], axis=0)
-    upper = jnp.concatenate([body[:, planes - 2 :], rate_field[None, planes - 2 :]], axis=0)
+    planes = center.shape[0]
+    lower = jnp.concatenate(
+        [center[None, :2], generators[:, :2], rate_field[None, :2]], axis=0
+    )
+    upper = jnp.concatenate(
+        [center[None, planes - 2 :], generators[:, planes - 2 :], rate_field[None, planes - 2 :]],
+        axis=0,
+    )
     before = lax.ppermute(upper, "slab", up)
     after = lax.ppermute(lower, "slab", down)
+    body = jnp.concatenate(lax.optimization_barrier([center[None], generators]), axis=0)
     fields = jnp.concatenate([before[:-1], body, after[:-1]], axis=1)
     rate_ext = jnp.concatenate([before[-1, 1:], rate_field, after[-1, :1]], axis=0)
     fields = update(fields, rate_ext)

time: 72.6 us -> 74 us (1.019)
  waiting for transfers between devices: 21.3 us -> 23.2 us
  local copies, waits for them, and re-layouts: 7.48 us -> 6.37 us
    slice x0 -> x3, local copies, waits for them, and re-layouts: none -> 2.97 us  [the longest x1 2.11 us: per_device(): generators[:, planes - 2:]]
    unnamed x11 -> x15, local copies, waits for them, and re-layouts: 4.01 us -> 1.5 us
    all_to_all x1, waiting for transfers between devices: 5.72 us -> 7.13 us  [exchange_sum(): received = lax.all_to_all(copies, axis, 0, 0, tiled=False)]
    reduce_sum x1, other arithmetic: 1.68 us -> 0.27 us  [per_device(): radius_local = jnp.sum(jnp.abs(gens_moved), axis=0)]
    all_to_all x1, waiting for transfers between devices: 7.85 us -> 8.94 us  [exchange_scatter(): received = jnp.sum(lax.all_to_all(message, axis, 0, 0, tiled=True), axis=0)]
    slice x1, local copies, waits for them, and re-layouts: 1.08 us -> 0.01 us  [per_device(): centre_moved = fields[0]]
    broadcast_in_dim x2 -> x4, local copies, waits for them, and re-layouts: 0.95 us -> 0.13 us  [the longest x2 0.06 us: per_device(): center[None, planes - 2:]]
    add x2, other arithmetic: 4.48 us -> 5.23 us  [update(): return middle + rate_field * (zsum + lateral(middle) - 6.0 * middle)]
  transfers between devices with their start and end apart: 4 -> 4, of which waited for: 4 -> 4; matrix products, arithmetic and copies ran while one was open for 4% -> 2% of each run, Pallas kernels for 0% -> 0%
where the time goes in v5:
time: 74 us; the launch traced here: 73.7 us
  starting transfers between devices  30.6 us (41%)
  waiting for transfers between devices  23.2 us (31%)
  other arithmetic  9.94 us (13%)
  local copies, waits for them, and re-layouts  6.37 us (9%)
  matrix products  2.66 us (4%)
  between operations  0.96 us (1%)
    all_to_all x1, starting transfers between devices, exchange_scatter(): received = jnp.sum(lax.all_to_all(message, axis, 0, 0, tiled=True), axis=0)  12.9 us
    all_to_all x1, waiting for transfers between devices, exchange_scatter(): received = jnp.sum(lax.all_to_all(message, axis, 0, 0, tiled=True), axis=0)  8.94 us
    all_to_all x1, starting transfers between devices, exchange_sum(): received = lax.all_to_all(copies, axis, 0, 0, tiled=False)  7.43 us
    all_to_all x1, waiting for transfers between devices, exchange_sum(): received = lax.all_to_all(copies, axis, 0, 0, tiled=False)  7.13 us
    ppermute x1, starting transfers between devices, per_device(): after = lax.ppermute(lower, 'slab', down)  5.53 us
    add x2, other arithmetic, update(): return middle + rate_field * (zsum + lateral(middle) - 6.0 * middle)  5.23 us
    ppermute x1, starting transfers between devices, per_device(): before = lax.ppermute(upper, 'slab', up)  4.73 us
    ppermute x1, waiting for transfers between devices, per_device(): after = lax.ppermute(lower, 'slab', down)  4.48 us
  transfers between devices with their start and end apart: 4, of which 4 were waited for; matrix products, arithmetic and copies ran while one was open for 2% of the time, Pallas kernels for 0%

profile of v5, /device:TPU:1, one launch (start us, length us, event | category | flops | bytes accessed | tf_op | source)
XLA Modules:
  0.0 73.7 jit_solution(6903896568183021547)
XLA Ops:
  0.6 0.0 copy-start
  0.7 1.3 %select_reduce_fusion = f32[4,4096]{1,0:T(4,128)S(1)} fusion(f32[8]{0:T(128)} %param.9, s32[4,4096]{1,0:T(4,128)} %param.8), kind=kLoop, calls=%fused_computation.26 | loop fusion | flops 376832 | bytes 131104 | tf_op jit(solution)/shard_map/reduce_sum | solution.py:31
  2.0 2.1 %fusion.26 = (f32[16,2,4096]{2,1,0:T(2,128)S(1)}, f32[16,2,4096]{2,1,0:T(2,128)S(1)}) fusion(f32[16,4,4096]{2,1,0:T(4,128)} %param.7), kind=kLoop, calls=%fused_computation.55 | loop fusion | bytes 2097152 | tf_op jit(solution)/shard_map/slice | solution.py:86
  4.1 0.3 copy.63
  4.6 0.1 pad_maximum_fusion.2
  4.7 4.7 %collective-permute-start = (f32[18,2,4096]{2,0,1:T(8,128)S(1)}, f32[18,2,4096]{2,0,1:T(8,128)S(1)}, u32[]{:S(2)}, u32[]{:S(2)}) collective-permute-start(f32[18,2,4096]{2,0,1:T(8,128)S(1)} %pad_maximum_fusion.2), channel_id=1, source_target_pairs={{0,32},{32,64},{64,96},{96,128},{128,160},{160,192},{192,224},{224... | collective-permute-start | bytes 1769480 | tf_op jit(solution)/shard_map/ppermute | solution.py:89
  9.5 0.3 copy.64
  9.8 0.1 pad_maximum_fusion.3
  9.9 5.5 %collective-permute-start.1 = (f32[18,2,4096]{2,0,1:T(8,128)S(1)}, f32[18,2,4096]{2,0,1:T(8,128)S(1)}, u32[]{:S(2)}, u32[]{:S(2)}) collective-permute-start(f32[18,2,4096]{2,0,1:T(8,128)S(1)} %pad_maximum_fusion.3), channel_id=1, source_target_pairs={{32,0},{64,32},{96,64},{128,96},{160,128},{192,160},{224,192},{256... | collective-permute-start | bytes 1769480 | tf_op jit(solution)/shard_map/ppermute | solution.py:90
  15.5 0.1 constant_dynamic-update-slice_fusion
  15.7 2.7 %collective-permute-done = f32[18,2,4096]{2,0,1:T(8,128)S(1)} collective-permute-done((f32[18,2,4096]{2,0,1:T(8,128)S(1)}, f32[18,2,4096]{2,0,1:T(8,128)S(1)}, u32[]{:S(2)}, u32[]{:S(2)}) %collective-permute-start) | collective-permute-done | bytes 589856 | tf_op jit(solution)/shard_map/ppermute | solution.py:89
  18.3 0.4 copy.56
  18.8 4.5 %collective-permute-done.1 = f32[18,2,4096]{2,0,1:T(8,128)S(1)} collective-permute-done((f32[18,2,4096]{2,0,1:T(8,128)S(1)}, f32[18,2,4096]{2,0,1:T(8,128)S(1)}, u32[]{:S(2)}, u32[]{:S(2)}) %collective-permute-start.1) | collective-permute-done | bytes 589856 | tf_op jit(solution)/shard_map/ppermute | solution.py:90
  23.2 0.4 copy.57
  23.8 0.8 %pad_maximum_fusion = f32[17,6,4096]{2,1,0:T(8,128)S(1)} fusion(f32[17,2,4096]{2,1,0:T(2,128)S(1)} %copy.57, f32[17,4,4096]{2,1,0:T(4,128)S(1)} %constant_dynamic-update-slice_fusion, f32[17,2,4096]{2,1,0:T(2,128)S(1)} %copy.56), kind=kLoop, calls=%fused_computation | loop fusion | flops 835584 | bytes 3899392 | tf_op jit(solution)/shard_map/concatenate | solution.py:92
  24.6 2.7 %fusion.3 = f32[17,6,4096]{2,1,0:T(8,128)S(1)} fusion(f32[17,6,4096]{2,1,0:T(8,128)S(1)} %pad_maximum_fusion, f32[17,2,4096]{2,1,0:T(2,128)S(1)} %copy.57, f32[17,4,4096]{2,1,0:T(4,128)S(1)} %constant_dynamic-update-slice_fusion, f32[17,2,4096]{2,1,0:T(2,128)S(1)} %copy.56, f32[6,4096]{1,0:T(8,128)S(1)} %pad_maximum_fusion.4, ...), kind=kLoop, calls=%fused_computation.6 | loop fusion | flops 5431296 | bytes 5677056 | tf_op jit(solution)/shard_map/add | solution.py:48
  27.3 0.3 slice.122
  27.6 2.5 %fusion.11 = f32[17,4,4096]{2,1,0:T(4,128)S(1)} fusion(f32[17,4,4096]{2,1,0:T(4,128)S(1)} %slice.122, f32[17,6,4096]{2,1,0:T(8,128)S(1)} %fusion.3, f32[4,4096]{1,0:T(4,128)S(1)} %broadcast_multiply_fusion, pred[4096]{0:T(1024)(128)(4,1)S(1)} %get-tuple-element.15, pred[4096]{0:T(1024)(128)(4,1)S(1)} %get-tuple-element.16), kind=kLoop, calls=%fused_computation.17 | loop fusion | flops 3063808 | bytes 4530176 | tf_op jit(solution)/shard_map/add | solution.py:48
  30.2 2.7 %fusion.13 = f32[32,17]{0,1:T(8,128)S(1)} fusion(f32[32,4,4096]{2,1,0:T(4,128)S(1)} %copy-done, f32[17,4,4096]{2,1,0:T(4,128)S(1)} %fusion.11), kind=kOutput, calls=%fused_computation.21 | convolution fusion | flops 53477376 | bytes 3213440 | tf_op jit(solution)/shard_map/bzc,gzc->bg/dot_general | solution.py:99
  32.9 0.7 %reshape.33 = f32[16,1,544]{2,1,0:T(1,128)} reshape(f32[16,17,32]{2,1,0:T(8,128)S(1)} %broadcast_bitcast_fusion) | data formatting | bytes 69632
  33.6 7.4 %all-to-all-start = ((f32[16,1,544]{2,1,0:T(1,128)}), f32[16,1,544]{2,1,0:T(1,128)S(1)}, u32[]{:S(2)}, u32[]{:S(2)}) async-start(f32[16,1,544]{2,1,0:T(1,128)} %reshape.33), calls=%async_computation | async-start | bytes 81920 | tf_op jit(solution)/shard_map/all_to_all | solution.py:61
  41.0 0.3 fusion.18
  41.3 7.1 %all-to-all-done = f32[16,1,544]{2,1,0:T(1,128)S(1)} async-done(((f32[16,1,544]{2,1,0:T(1,128)}), f32[16,1,544]{2,1,0:T(1,128)S(1)}, u32[]{:S(2)}, u32[]{:S(2)}) %all-to-all-start) | async-done | bytes 34848 | tf_op jit(solution)/shard_map/all_to_all | solution.py:61
  48.5 0.5 broadcast.25
  49.0 0.7 %reduce.1 = f32[16,544]{1,0:T(8,128)S(1)} reduce(f32[16,1,544]{2,1,0:T(1,128)S(1)} %all-to-all-done, f32[]{:T(128)} %broadcast.25), dimensions={1}, to_apply=%all_to_all.9.reduce_sub_computation | reduce | bytes 69636 | tf_op jit(solution)/shard_map/all_to_all | solution.py:61
  49.7 0.1 reshape.34
  49.9 0.7 copy.62
  50.6 12.9 %all-to-all-start.1 = ((f32[32,1,544]{2,1,0:T(1,128)}), f32[32,1,544]{2,1,0:T(1,128)S(1)}, u32[]{:S(2)}, u32[]{:S(2)}) async-start(f32[32,1,544]{2,1,0:T(1,128)} %copy.62), calls=%async_computation.1 | async-start | bytes 163840 | tf_op jit(solution)/shard_map/all_to_all | solution.py:72
  63.5 8.9 %all-to-all-done.1 = f32[32,1,544]{2,1,0:T(1,128)S(1)} async-done(((f32[32,1,544]{2,1,0:T(1,128)}), f32[32,1,544]{2,1,0:T(1,128)S(1)}, u32[]{:S(2)}, u32[]{:S(2)}) %all-to-all-start.1) | async-done | bytes 69664 | tf_op jit(solution)/shard_map/all_to_all | solution.py:72
  72.5 0.1 reduce_sum.58
  72.5 0.6 select_reduce_fusion.1
  73.1 0.6 bitcast_add_fusion
  (27 shorter events, 0.4 us)
Async XLA Ops:
  0.6 29.5 %copy-start = (f32[32,4,4096]{2,1,0:T(4,128)S(1)}, f32[32,4,4096]{2,1,0:T(4,128)}, u32[]{:S(2)}) copy-start(f32[32,4,4096]{2,1,0:T(4,128)} %param.10) | copy-start | bytes 6291460
  0.6 3.8 %copy-start.2 = (f32[4,4096]{1,0:T(4,128)S(1)}, f32[4,4096]{1,0:T(4,128)}, u32[]{:S(2)}) copy-start(f32[4,4096]{1,0:T(4,128)} %param.6) | copy-start | bytes 196612
  4.5 11.0 %copy-start.1 = (f32[16,4,4096]{2,1,0:T(4,128)S(1)}, f32[16,4,4096]{2,1,0:T(4,128)}, u32[]{:S(2)}) copy-start(f32[16,4,4096]{2,1,0:T(4,128)} %param.7) | copy-start | bytes 3145732
  4.7 13.6 %collective-permute-start = (f32[18,2,4096]{2,0,1:T(8,128)S(1)}, f32[18,2,4096]{2,0,1:T(8,128)S(1)}, u32[]{:S(2)}, u32[]{:S(2)}) collective-permute-start(f32[18,2,4096]{2,0,1:T(8,128)S(1)} %pad_maximum_fusion.2), channel_id=1, source_target_pairs={{0,32},{32,64},{64,96},{96,128},{128,160},{160,192},{192,224},{224... | collective-permute-start | bytes 1769480 | tf_op jit(solution)/shard_map/ppermute | solution.py:89
  9.9 13.3 %collective-permute-start.1 = (f32[18,2,4096]{2,0,1:T(8,128)S(1)}, f32[18,2,4096]{2,0,1:T(8,128)S(1)}, u32[]{:S(2)}, u32[]{:S(2)}) collective-permute-start(f32[18,2,4096]{2,0,1:T(8,128)S(1)} %pad_maximum_fusion.3), channel_id=1, source_target_pairs={{32,0},{64,32},{96,64},{128,96},{160,128},{192,160},{224,192},{256... | collective-permute-start | bytes 1769480 | tf_op jit(solution)/shard_map/ppermute | solution.py:90
  32.8 39.7 %copy-start.3 = (s32[128]{0:T(128)S(1)}, s32[128]{0:T(128)}, u32[]{:S(2)}) copy-start(s32[128]{0:T(128)} %param.11) | copy-start | bytes 1540
  33.6 14.8 %all-to-all-start = ((f32[16,1,544]{2,1,0:T(1,128)}), f32[16,1,544]{2,1,0:T(1,128)S(1)}, u32[]{:S(2)}, u32[]{:S(2)}) async-start(f32[16,1,544]{2,1,0:T(1,128)} %reshape.33), calls=%async_computation | async-start | bytes 81920 | tf_op jit(solution)/shard_map/all_to_all | solution.py:61
  50.6 21.8 %all-to-all-start.1 = ((f32[32,1,544]{2,1,0:T(1,128)}), f32[32,1,544]{2,1,0:T(1,128)S(1)}, u32[]{:S(2)}, u32[]{:S(2)}) async-start(f32[32,1,544]{2,1,0:T(1,128)} %copy.62), calls=%async_computation.1 | async-start | bytes 163840 | tf_op jit(solution)/shard_map/all_to_all | solution.py:72

commit v6 on v4

--- a/solution.py
+++ b/solution.py
@@ -2,6 +2,8 @@
 import jax.numpy as jnp
 from jax import lax
 from jax.sharding import PartitionSpec as P
+from jax.experimental import pallas as pl
+from jax.experimental.pallas import tpu as pltpu
 
 NX = 64
 NY = 64
@@ -73,6 +75,61 @@
     return received[: rows * width].reshape(rows, width), received[rows * width :]
 
 
+def stencil_kernel(ext_ref, rate_ref, bank_ref, centre_ref, radius_ref, prod_ref, moved_ref):
+    rate = rate_ref[...]
+    rows, cells = rate.shape
+    lane = lax.broadcasted_iota(jnp.int32, (rows, cells), 1)
+    column = lane % NY
+    has_next = lane < cells - NY
+    has_prev = lane >= NY
+    has_plus = column < NY - 1
+    has_minus = column > 0
+    zero = jnp.float32(0.0)
+
+    def step(u):
+        zsum = pltpu.roll(u, rows - 1, 0) + pltpu.roll(u, 1, 0)
+        total = jnp.where(has_next, pltpu.roll(u, cells - NY, 1), zero) + jnp.where(
+            has_prev, pltpu.roll(u, NY, 1), zero
+        )
+        plus = jnp.where(has_plus, pltpu.roll(u, cells - 1, 1), zero)
+        minus = jnp.where(has_minus, pltpu.roll(u, 1, 1), zero)
+        side = total + plus + minus
+        return u + rate * (zsum + side - 6.0 * u)
+
+    radius = jnp.zeros((rows, cells), jnp.float32)
+    for f in range(ext_ref.shape[0]):
+        moved = step(step(ext_ref[f]))
+        if f == 0:
+            centre_ref[...] = moved
+        else:
+            radius = radius + jnp.abs(moved)
+        moved_ref[pl.ds(f * rows, rows), :] = moved
+    radius_ref[...] = radius
+    prod_ref[...] = lax.dot_general(
+        bank_ref[...],
+        moved_ref[...],
+        (((1,), (1,)), ((), ())),
+        precision=lax.Precision.HIGHEST,
+        preferred_element_type=jnp.float32,
+    )
+
+
+def fused_stencil(ext, rate_ext, bank):
+    count, rows, cells = ext.shape
+    vmem = pl.BlockSpec(memory_space=pltpu.VMEM)
+    return pl.pallas_call(
+        stencil_kernel,
+        out_shape=(
+            jax.ShapeDtypeStruct((rows, cells), jnp.float32),
+            jax.ShapeDtypeStruct((rows, cells), jnp.float32),
+            jax.ShapeDtypeStruct((bank.shape[0], count * rows), jnp.float32),
+        ),
+        in_specs=[vmem, vmem, vmem],
+        out_specs=(vmem, vmem, vmem),
+        scratch_shapes=[pltpu.VMEM((count * rows, cells), jnp.float32)],
+    )(ext, rate_ext, bank)
+
+
 def per_device(center, generators, conductivity, cond_table, direction_bank, selection):
     rate_field = lookup_rate(conductivity, cond_table)
     body = jnp.concatenate([center[None], generators], axis=0)
@@ -85,15 +142,15 @@
     before = lax.ppermute(upper, "slab", up)
     after = lax.ppermute(lower, "slab", down)
     fields = jnp.concatenate([before[:-1], body, after[:-1]], axis=1)
-    rate_ext = jnp.concatenate([before[-1, 1:], rate_field, after[-1, :1]], axis=0)
-    fields = update(fields, rate_ext)
-    fields = update(fields, rate_field)
-    centre_moved = fields[0]
-    gens_moved = fields[1:]
-    radius_local = jnp.sum(jnp.abs(gens_moved), axis=0)
-    all_proj = jnp.einsum(
-        "bzc,gzc->bg", direction_bank, fields, precision=lax.Precision.HIGH
-    )
+    rate_ext = jnp.concatenate([before[-1], rate_field, after[-1]], axis=0)
+    bank_rows = direction_bank.reshape(-1, direction_bank.shape[2])
+    centre_ext, radius_ext, prod = fused_stencil(fields, rate_ext, bank_rows)
+    centre_moved = centre_ext[2 : 2 + planes]
+    radius_local = radius_ext[2 : 2 + planes]
+    prod = prod.reshape(direction_bank.shape[0], planes, fields.shape[0], fields.shape[1])
+    all_proj = prod[:, 0, :, 2]
+    for z in range(1, planes):
+        all_proj = all_proj + prod[:, z, :, 2 + z]
     summed = exchange_sum(all_proj, "slab")
     summed_centre, summed_proj = summed[:, 0], summed[:, 1:]
     partial_value = jnp.sum(jnp.abs(summed_proj), axis=1)

time: 72.6 us -> 79.3 us (1.092)
  Pallas kernels: 0 us -> 8.44 us
  waiting for transfers between devices: 21.3 us -> 18.7 us
  matrix products: 2.13 us -> 0 us
  local copies, waits for them, and re-layouts: 7.48 us -> 9.14 us
  starting transfers between devices: 30.4 us -> 31.2 us
    pallas_call x0 -> x1, Pallas kernels: none -> 8.44 us  [fused_stencil(): pl.pallas_call(stencil_kernel, out_shape=(jax.ShapeDtypeStruct((rows, cel...]
    add x2 -> x1, other arithmetic: 4.48 us -> 0.47 us  [per_device(): all_proj = all_proj + prod[:, z, :, 2 + z]]
    ppermute x1, waiting for transfers between devices: 3.2 us -> 0.01 us  [per_device(): before = lax.ppermute(upper, 'slab', up)]
    unnamed x11 -> x16, local copies, waits for them, and re-layouts: 4.01 us -> 0.89 us
    reshape x0 -> x2, local copies, waits for them, and re-layouts: none -> 3.03 us  [the longest x1 1.74 us: per_device(): bank_rows = direction_bank.reshape(-1, direction_bank.shape[2])]
    ppermute x1, waiting for transfers between devices: 4.56 us -> 2.38 us  [per_device(): after = lax.ppermute(lower, 'slab', down)]
    dot_general x1 -> x0, matrix products: 2.13 us -> none  [per_device(): jnp.einsum('bzc,gzc->bg', direction_bank, fields, precision=lax.Precision...]
    concatenate x1, other arithmetic: 0.25 us -> 2.15 us  [per_device(): fields = jnp.concatenate([before[:-1], body, after[:-1]], axis=1)]
  transfers between devices with their start and end apart: 4 -> 4, of which waited for: 4 -> 3; matrix products, arithmetic and copies ran while one was open for 4% -> 5% of each run, Pallas kernels for 0% -> 0%
where the time goes in v6:
time: 79.3 us; the launch traced here: 78.8 us
  starting transfers between devices  31.2 us (39%)
  waiting for transfers between devices  18.7 us (24%)
  other arithmetic  10.5 us (13%)
  local copies, waits for them, and re-layouts  9.14 us (12%)
  Pallas kernels  8.44 us (11%)
  between operations  0.85 us (1%)
    all_to_all x1, starting transfers between devices, exchange_scatter(): received = jnp.sum(lax.all_to_all(message, axis, 0, 0, tiled=True), axis=0)  12.9 us
    all_to_all x1, waiting for transfers between devices, exchange_scatter(): received = jnp.sum(lax.all_to_all(message, axis, 0, 0, tiled=True), axis=0)  8.92 us
    pallas_call x1, Pallas kernels, fused_stencil(): pl.pallas_call(stencil_kernel, out_shape=(jax.ShapeDtypeStruct((rows, cel...  8.44 us
    all_to_all x1, starting transfers between devices, exchange_sum(): received = lax.all_to_all(copies, axis, 0, 0, tiled=False)  7.42 us
    all_to_all x1, waiting for transfers between devices, exchange_sum(): received = lax.all_to_all(copies, axis, 0, 0, tiled=False)  7.37 us
    ppermute x1, starting transfers between devices, per_device(): after = lax.ppermute(lower, 'slab', down)  6.28 us
    ppermute x1, starting transfers between devices, per_device(): before = lax.ppermute(upper, 'slab', up)  4.58 us
    ppermute x1, waiting for transfers between devices, per_device(): after = lax.ppermute(lower, 'slab', down)  2.38 us
  transfers between devices with their start and end apart: 4, of which 3 were waited for; matrix products, arithmetic and copies ran while one was open for 5% of the time, Pallas kernels for 0%

profile of v6, /device:TPU:1, one launch (start us, length us, event | category | flops | bytes accessed | tf_op | source)
XLA Modules:
  0.0 78.8 jit_solution(8655664094716314850)
XLA Ops:
  0.6 0.0 copy-start.2
  0.6 0.0 copy-start
  0.7 1.2 %select_reduce_fusion = f32[4,4096]{1,0:T(4,128)S(1)} fusion(f32[8]{0:T(128)} %param.9, s32[4,4096]{1,0:T(4,128)} %param.8), kind=kLoop, calls=%fused_computation.7 | loop fusion | flops 376832 | bytes 131104 | tf_op jit(solution)/shard_map/reduce_sum | solution.py:33
  1.9 1.8 %fusion.1 = f32[17,2,4096]{2,1,0:T(2,128)S(1)} fusion(f32[1,4,4096]{2,1,0:T(4,128)} %bitcast.30, f32[16,4,4096]{2,1,0:T(4,128)} %param.7), kind=kLoop, calls=%fused_computation.6 | loop fusion | flops 139264 | bytes 1671168 | tf_op jit(solution)/shard_map/concatenate | solution.py:135
  3.7 1.1 %pad_maximum_fusion.2 = f32[18,2,4096]{2,1,0:T(2,128)} fusion(f32[1,2,4096]{2,1,0:T(2,128)S(1)} %get-tuple-element.11, f32[17,2,4096]{2,1,0:T(2,128)S(1)} %fusion.1), kind=kLoop, calls=%fused_computation.5 | loop fusion | flops 147456 | bytes 1179648 | tf_op jit(solution)/shard_map/concatenate | solution.py:141
  4.8 4.6 %collective-permute-start = (f32[18,2,4096]{2,1,0:T(2,128)}, f32[18,2,4096]{2,1,0:T(2,128)}, u32[]{:S(2)}, u32[]{:S(2)}) collective-permute-start(f32[18,2,4096]{2,1,0:T(2,128)} %pad_maximum_fusion.2), channel_id=1, source_target_pairs={{0,32},{32,64},{64,96},{96,128},{128,160},{160,192},{192,224},{224... | collective-permute-start | bytes 1769480 | tf_op jit(solution)/shard_map/ppermute | solution.py:142
  9.4 1.1 %fusion = f32[18,2,4096]{2,1,0:T(2,128)} fusion(f32[16,4,4096]{2,1,0:T(4,128)S(1)} %copy-done, f32[1,4,4096]{2,1,0:T(4,128)S(1)} %bitcast.31, f32[1,2,4096]{2,1,0:T(2,128)S(1)} %get-tuple-element.12), kind=kLoop, calls=%fused_computation.4 | loop fusion | flops 294912 | bytes 1736704 | tf_op jit(solution)/shard_map/concatenate | solution.py:140
  10.5 6.3 %collective-permute-start.1 = (f32[18,2,4096]{2,1,0:T(2,128)}, f32[18,2,4096]{2,1,0:T(2,128)}, u32[]{:S(2)}, u32[]{:S(2)}) collective-permute-start(f32[18,2,4096]{2,1,0:T(2,128)} %fusion), channel_id=1, source_target_pairs={{32,0},{64,32},{96,64},{128,96},{160,128},{192,160},{224,192},{256... | collective-permute-start | bytes 1769480 | tf_op jit(solution)/shard_map/ppermute | solution.py:143
  16.8 1.7 %reshape.50.bank_ref = f32[128,4096]{1,0:T(8,128)} reshape(f32[32,4,4096]{2,1,0:T(4,128)S(1)} %copy-done.1) | data formatting | bytes 4194304 | tf_op jit(solution)/shard_map/reshape | solution.py:146
  18.5 1.1 %slice.75 = f32[17,2,4096]{2,1,0:T(2,128)S(1)} slice(f32[18,2,4096]{2,1,0:T(2,128)} %collective-permute-done), slice={[0:17], [0:2], [0:4096]} | slice | bytes 1114112 | tf_op jit(solution)/shard_map/slice | solution.py:144
  19.6 2.4 %collective-permute-done.1 = f32[18,2,4096]{2,1,0:T(2,128)} collective-permute-done((f32[18,2,4096]{2,1,0:T(2,128)}, f32[18,2,4096]{2,1,0:T(2,128)}, u32[]{:S(2)}, u32[]{:S(2)}) %collective-permute-start.1) | collective-permute-done | bytes 589856 | tf_op jit(solution)/shard_map/ppermute | solution.py:143
  22.0 1.1 %slice.77 = f32[17,2,4096]{2,1,0:T(2,128)S(1)} slice(f32[18,2,4096]{2,1,0:T(2,128)} %collective-permute-done.1), slice={[0:17], [0:2], [0:4096]} | slice | bytes 1114112 | tf_op jit(solution)/shard_map/slice | solution.py:144
  23.1 2.1 %pad_maximum_fusion.ext_ref = f32[17,8,4096]{2,1,0:T(8,128)} fusion(f32[17,2,4096]{2,1,0:T(2,128)S(1)} %slice.77, f32[16,4,4096]{2,1,0:T(4,128)S(1)} %copy-done, f32[1,4,4096]{2,1,0:T(4,128)S(1)} %bitcast.32, f32[17,2,4096]{2,1,0:T(2,128)S(1)} %slice.75), kind=kLoop, calls=%fused_computation | loop fusion | flops 1671168 | bytes 4456448 | tf_op jit(solution)/shard_map/concatenate | solution.py:144
  25.2 0.8 slice_bitcast_fusion.1
  26.0 0.8 slice_bitcast_fusion
  26.7 0.7 pad_maximum_fusion.3.rate_ref
  27.5 8.4 %shard_map.85 = (f32[8,4096]{1,0:T(8,128)}, f32[8,4096]{1,0:T(8,128)}, f32[128,136]{1,0:T(8,128)}) custom-call(f32[17,8,4096]{2,1,0:T(8,128)} %pad_maximum_fusion.ext_ref, f32[8,4096]{1,0:T(8,128)} %pad_maximum_fusion.3.rate_ref, f32[128,4096]{1,0:T(8,128)} %reshape.50.bank_ref), custom_call_target="tpu_custom_call" | custom-call | tf_op jit(solution)/shard_map/pallas_call | solution.py:120
  35.9 1.3 %reshape.53 = f32[32,4,17,8]{3,2,1,0:T(8,128)S(1)} reshape(f32[128,136]{1,0:T(8,128)} %get-tuple-element.8) | data formatting | bytes 139264 | tf_op jit(solution)/shard_map/reshape | solution.py:150
  37.2 0.5 slice_add_fusion
  37.7 0.2 copy.16
  37.9 0.7 reshape.56
  38.7 7.4 %all-to-all-start = ((f32[16,1,544]{2,1,0:T(1,128)}), f32[16,1,544]{2,1,0:T(1,128)S(1)}, u32[]{:S(2)}, u32[]{:S(2)}) async-start(f32[16,1,544]{2,1,0:T(1,128)} %reshape.56), calls=%async_computation | async-start | bytes 81920 | tf_op jit(solution)/shard_map/all_to_all | solution.py:63
  46.2 7.4 %all-to-all-done = f32[16,1,544]{2,1,0:T(1,128)S(1)} async-done(((f32[16,1,544]{2,1,0:T(1,128)}), f32[16,1,544]{2,1,0:T(1,128)S(1)}, u32[]{:S(2)}, u32[]{:S(2)}) %all-to-all-start) | async-done | bytes 34848 | tf_op jit(solution)/shard_map/all_to_all | solution.py:63
  53.5 0.5 broadcast.7
  54.0 0.7 reduce.1
  54.8 0.1 reshape.57
  55.0 0.7 copy.17
  55.7 12.9 %all-to-all-start.1 = ((f32[32,1,544]{2,1,0:T(1,128)}), f32[32,1,544]{2,1,0:T(1,128)S(1)}, u32[]{:S(2)}, u32[]{:S(2)}) async-start(f32[32,1,544]{2,1,0:T(1,128)} %copy.17), calls=%async_computation.1 | async-start | bytes 163840 | tf_op jit(solution)/shard_map/all_to_all | solution.py:74
  68.6 8.9 %all-to-all-done.1 = f32[32,1,544]{2,1,0:T(1,128)S(1)} async-done(((f32[32,1,544]{2,1,0:T(1,128)}), f32[32,1,544]{2,1,0:T(1,128)S(1)}, u32[]{:S(2)}, u32[]{:S(2)}) %all-to-all-start.1) | async-done | bytes 69664 | tf_op jit(solution)/shard_map/all_to_all | solution.py:74
  77.5 0.1 reduce_sum.48
  77.6 0.6 select_reduce_fusion.1
  78.2 0.6 bitcast_add_fusion
  (22 shorter events, 0.2 us)
Async XLA Ops:
  0.6 8.7 %copy-start.2 = (f32[4,4096]{1,0:T(4,128)S(1)}, f32[4,4096]{1,0:T(4,128)}, u32[]{:S(2)}) copy-start(f32[4,4096]{1,0:T(4,128)} %param.6) | copy-start | bytes 196612
  0.6 8.7 %copy-start = (f32[16,4,4096]{2,1,0:T(4,128)S(1)}, f32[16,4,4096]{2,1,0:T(4,128)}, u32[]{:S(2)}) copy-start(f32[16,4,4096]{2,1,0:T(4,128)} %param.7) | copy-start | bytes 3145732
  1.9 14.8 %copy-start.1 = (f32[32,4,4096]{2,1,0:T(4,128)S(1)}, f32[32,4,4096]{2,1,0:T(4,128)}, u32[]{:S(2)}) copy-start(f32[32,4,4096]{2,1,0:T(4,128)} %param.10) | copy-start | bytes 6291460
  4.8 13.7 %collective-permute-start = (f32[18,2,4096]{2,1,0:T(2,128)}, f32[18,2,4096]{2,1,0:T(2,128)}, u32[]{:S(2)}, u32[]{:S(2)}) collective-permute-start(f32[18,2,4096]{2,1,0:T(2,128)} %pad_maximum_fusion.2), channel_id=1, source_target_pairs={{0,32},{32,64},{64,96},{96,128},{128,160},{160,192},{192,224},{224... | collective-permute-start | bytes 1769480 | tf_op jit(solution)/shard_map/ppermute | solution.py:142
  10.5 11.5 %collective-permute-start.1 = (f32[18,2,4096]{2,1,0:T(2,128)}, f32[18,2,4096]{2,1,0:T(2,128)}, u32[]{:S(2)}, u32[]{:S(2)}) collective-permute-start(f32[18,2,4096]{2,1,0:T(2,128)} %fusion), channel_id=1, source_target_pairs={{32,0},{64,32},{96,64},{128,96},{160,128},{192,160},{224,192},{256... | collective-permute-start | bytes 1769480 | tf_op jit(solution)/shard_map/ppermute | solution.py:143
  35.9 10.2 %copy-start.4 = (f32[8,4096]{1,0:T(8,128)S(1)}, f32[8,4096]{1,0:T(8,128)}, u32[]{:S(2)}) copy-start(f32[8,4096]{1,0:T(8,128)} %get-tuple-element.7) | copy-start | bytes 393220
  37.2 31.4 %copy-start.3 = (f32[8,4096]{1,0:T(8,128)S(1)}, f32[8,4096]{1,0:T(8,128)}, u32[]{:S(2)}) copy-start(f32[8,4096]{1,0:T(8,128)} %get-tuple-element.6) | copy-start | bytes 393220
  37.2 40.4 %copy-start.5 = (s32[128]{0:T(128)S(1)}, s32[128]{0:T(128)}, u32[]{:S(2)}) copy-start(s32[128]{0:T(128)} %param.11) | copy-start | bytes 1540
  38.7 14.8 %all-to-all-start = ((f32[16,1,544]{2,1,0:T(1,128)}), f32[16,1,544]{2,1,0:T(1,128)S(1)}, u32[]{:S(2)}, u32[]{:S(2)}) async-start(f32[16,1,544]{2,1,0:T(1,128)} %reshape.56), calls=%async_computation | async-start | bytes 81920 | tf_op jit(solution)/shard_map/all_to_all | solution.py:63
  55.7 21.8 %all-to-all-start.1 = ((f32[32,1,544]{2,1,0:T(1,128)}), f32[32,1,544]{2,1,0:T(1,128)S(1)}, u32[]{:S(2)}, u32[]{:S(2)}) async-start(f32[32,1,544]{2,1,0:T(1,128)} %copy.17), calls=%async_computation.1 | async-start | bytes 163840 | tf_op jit(solution)/shard_map/all_to_all | solution.py:74

commit v7 on v4

--- a/solution.py
+++ b/solution.py
@@ -57,20 +57,22 @@
 
 def exchange_sum(x, axis):
     size = lax.axis_size(axis)
-    copies = jnp.broadcast_to(x[None], (size,) + x.shape)
-    received = lax.all_to_all(copies, axis, 0, 0, tiled=False)
-    return jnp.sum(received, axis=0)
+    flat = x.reshape(-1)
+    copies = jnp.broadcast_to(flat[None], (size, flat.shape[0]))
+    received = lax.all_to_all(copies, axis, 0, 0, tiled=True)
+    return jnp.sum(received, axis=0).reshape(x.shape)
 
 
 def exchange_scatter(x, extra, axis):
     size = lax.axis_size(axis)
     rows, cols = x.shape
     width = cols // size
-    blocks = x.reshape(rows, size, width).transpose(1, 0, 2).reshape(size, rows * width)
-    extras = jnp.broadcast_to(extra[None], (size, extra.shape[0]))
-    message = jnp.concatenate([blocks, extras], axis=1)
-    received = jnp.sum(lax.all_to_all(message, axis, 0, 0, tiled=True), axis=0)
-    return received[: rows * width].reshape(rows, width), received[rows * width :]
+    blocks = x.reshape(rows, size, width)
+    padded = jnp.pad(extra, (0, width - extra.shape[0]))
+    extras = jnp.broadcast_to(padded[None, None], (1, size, width))
+    message = jnp.concatenate([blocks, extras], axis=0)
+    received = jnp.sum(lax.all_to_all(message, axis, 1, 1, tiled=True), axis=1)
+    return received[:rows], received[rows, : extra.shape[0]]
 
 
 def per_device(center, generators, conductivity, cond_table, direction_bank, selection):

time: 72.6 us -> 78.1 us (1.076)
  other arithmetic: 9.92 us -> 14 us
  starting transfers between devices: 30.4 us -> 31.2 us
    ppermute x1, waiting for transfers between devices: 3.2 us -> 1.81 us  [per_device(): before = lax.ppermute(upper, 'slab', up)]
    all_to_all x2 -> x0, local copies, waits for them, and re-layouts: 1.22 us -> none  [the longest x1 0.71 us: exchange_scatter(): received = jnp.sum(lax.all_to_all(message, axis, 0, 0, tiled=True), axis=0)]
    add x2, other arithmetic: 4.48 us -> 5.61 us  [update(): return middle + rate_field * (zsum + lateral(middle) - 6.0 * middle)]
    concatenate x1, other arithmetic: 0.25 us -> 1.36 us  [per_device(): fields = jnp.concatenate([before[:-1], body, after[:-1]], axis=1)]
    squeeze x1, local copies, waits for them, and re-layouts: 0.02 us -> 0.92 us  [per_device(): after[-1, :1]]
    squeeze x1, local copies, waits for them, and re-layouts: 0.02 us -> 0.92 us  [per_device(): before[-1, 1:]]
    concatenate x1, other arithmetic: 0.11 us -> 1 us  [per_device(): lower = jnp.concatenate([body[:, :2], rate_field[None, :2]], axis=0)]
    concatenate x1, other arithmetic: 0.09 us -> 0.96 us  [per_device(): jnp.concatenate([body[:, planes - 2:], rate_field[None, planes - 2:]], ax...]
  transfers between devices with their start and end apart: 4 -> 4, of which waited for: 4 -> 4; matrix products, arithmetic and copies ran while one was open for 4% -> 5% of each run, Pallas kernels for 0% -> 0%
where the time goes in v7:
time: 78.1 us; the launch traced here: 77.6 us
  starting transfers between devices  31.2 us (40%)
  waiting for transfers between devices  21.1 us (27%)
  other arithmetic  14 us (18%)
  local copies, waits for them, and re-layouts  8.25 us (11%)
  matrix products  2.13 us (3%)
  between operations  0.83 us (1%)
    all_to_all x1, starting transfers between devices, exchange_scatter(): received = jnp.sum(lax.all_to_all(message, axis, 1, 1, tiled=True), axis=1)  12.9 us
    all_to_all x1, waiting for transfers between devices, exchange_scatter(): received = jnp.sum(lax.all_to_all(message, axis, 1, 1, tiled=True), axis=1)  9.22 us
    all_to_all x1, starting transfers between devices, exchange_sum(): received = lax.all_to_all(copies, axis, 0, 0, tiled=True)  7.43 us
    ppermute x1, starting transfers between devices, per_device(): after = lax.ppermute(lower, 'slab', down)  6.34 us
    add x2, other arithmetic, update(): return middle + rate_field * (zsum + lateral(middle) - 6.0 * middle)  5.61 us
    ppermute x1, waiting for transfers between devices, per_device(): after = lax.ppermute(lower, 'slab', down)  5.43 us
    all_to_all x1, waiting for transfers between devices, exchange_sum(): received = lax.all_to_all(copies, axis, 0, 0, tiled=True)  4.66 us
    ppermute x1, starting transfers between devices, per_device(): before = lax.ppermute(upper, 'slab', up)  4.58 us
  transfers between devices with their start and end apart: 4, of which 4 were waited for; matrix products, arithmetic and copies ran while one was open for 5% of the time, Pallas kernels for 0%

profile of v7, /device:TPU:1, one launch (start us, length us, event | category | flops | bytes accessed | tf_op | source)
XLA Modules:
  0.0 77.6 jit_solution(2493966162546588759)
XLA Ops:
  0.6 2.0 %copy.39 = f32[16,4,4096]{2,0,1:T(8,128)S(1)} copy(f32[16,4,4096]{2,1,0:T(4,128)} %param.7) | data formatting | bytes 2097152 | tf_op args[1]
  2.6 0.9 %copy.38 = f32[1,4,4096]{2,0,1:T(1,128)S(1)} copy(f32[1,4,4096]{2,1,0:T(4,128)} %bitcast.25) | data formatting | bytes 131072 | tf_op jit(solution)/shard_map/broadcast_in_dim | solution.py:80
  3.5 1.1 %select_reduce_fusion = f32[4,4096]{1,0:T(4,128)S(1)} fusion(f32[8]{0:T(128)} %param.9, s32[4,4096]{1,0:T(4,128)} %param.8), kind=kLoop, calls=%fused_computation.30 | loop fusion | flops 376832 | bytes 131104 | tf_op jit(solution)/shard_map/reduce_sum | solution.py:31
  4.8 1.0 %pad_maximum_fusion.4 = f32[18,2,4096]{2,0,1:T(8,128)} fusion(f32[1,2,4096]{2,0,1:T(1,128)S(1)} %copy.40, f32[17,2,4096]{2,0,1:T(8,128)S(1)} %fusion.16), kind=kLoop, calls=%fused_computation.29 | loop fusion | flops 147456 | bytes 1179648 | tf_op jit(solution)/shard_map/concatenate | solution.py:86
  5.8 4.6 %collective-permute-start = (f32[18,2,4096]{2,0,1:T(8,128)}, f32[18,2,4096]{2,0,1:T(8,128)}, u32[]{:S(2)}, u32[]{:S(2)}) collective-permute-start(f32[18,2,4096]{2,0,1:T(8,128)} %pad_maximum_fusion.4), channel_id=1, source_target_pairs={{0,32},{32,64},{64,96},{96,128},{128,160},{160,192},{192,224},{224... | collective-permute-start | bytes 1769480 | tf_op jit(solution)/shard_map/ppermute | solution.py:87
  10.4 1.0 %fusion.17 = f32[18,2,4096]{2,0,1:T(8,128)} fusion(f32[16,4,4096]{2,0,1:T(8,128)S(1)} %copy.39, f32[1,4,4096]{2,0,1:T(1,128)S(1)} %copy.38, f32[1,2,4096]{2,0,1:T(1,128)S(1)} %copy.41), kind=kLoop, calls=%fused_computation.28 | loop fusion | flops 294912 | bytes 1736704 | tf_op jit(solution)/shard_map/concatenate | solution.py:85
  11.4 6.3 %collective-permute-start.1 = (f32[18,2,4096]{2,0,1:T(8,128)}, f32[18,2,4096]{2,0,1:T(8,128)}, u32[]{:S(2)}, u32[]{:S(2)}) collective-permute-start(f32[18,2,4096]{2,0,1:T(8,128)} %fusion.17), channel_id=1, source_target_pairs={{32,0},{64,32},{96,64},{128,96},{160,128},{192,160},{224,192},{256... | collective-permute-start | bytes 1769480 | tf_op jit(solution)/shard_map/ppermute | solution.py:88
  17.8 1.8 %collective-permute-done = f32[18,2,4096]{2,0,1:T(8,128)} collective-permute-done((f32[18,2,4096]{2,0,1:T(8,128)}, f32[18,2,4096]{2,0,1:T(8,128)}, u32[]{:S(2)}, u32[]{:S(2)}) %collective-permute-start) | collective-permute-done | bytes 589856 | tf_op jit(solution)/shard_map/ppermute | solution.py:87
  19.6 5.4 %collective-permute-done.1 = f32[18,2,4096]{2,0,1:T(8,128)} collective-permute-done((f32[18,2,4096]{2,0,1:T(8,128)}, f32[18,2,4096]{2,0,1:T(8,128)}, u32[]{:S(2)}, u32[]{:S(2)}) %collective-permute-start.1) | collective-permute-done | bytes 589856 | tf_op jit(solution)/shard_map/ppermute | solution.py:88
  25.1 1.4 %pad_maximum_fusion = f32[17,6,4096]{2,0,1:T(8,128)S(1)} fusion(f32[17,2,4096]{2,0,1:T(8,128)} %bitcast.22, f32[17,2,4096]{2,0,1:T(8,128)} %bitcast.23, f32[16,4,4096]{2,0,1:T(8,128)S(1)} %copy.39, f32[1,4,4096]{2,0,1:T(1,128)S(1)} %copy.38), kind=kLoop, calls=%fused_computation | loop fusion | flops 1253376 | bytes 3899392 | tf_op jit(solution)/shard_map/concatenate | solution.py:89
  26.4 0.9 %slice_bitcast_fusion.3 = f32[1,4096]{1,0:T(1,128)S(1)} fusion(f32[18,2,4096]{2,0,1:T(8,128)} %collective-permute-done), kind=kLoop, calls=%fused_computation.42 | loop fusion | bytes 32768 | tf_op jit(solution)/shard_map/squeeze | solution.py:90
  27.4 0.9 %slice_bitcast_fusion.2 = f32[1,4096]{1,0:T(1,128)S(1)} fusion(f32[18,2,4096]{2,0,1:T(8,128)} %collective-permute-done.1), kind=kLoop, calls=%fused_computation.41 | loop fusion | bytes 32768 | tf_op jit(solution)/shard_map/squeeze | solution.py:90
  28.3 3.9 %fusion.3 = f32[17,6,4096]{2,0,1:T(8,128)S(1)} fusion(f32[17,6,4096]{2,0,1:T(8,128)S(1)} %pad_maximum_fusion, f32[17,2,4096]{2,0,1:T(8,128)} %bitcast.22, f32[16,4,4096]{2,0,1:T(8,128)S(1)} %copy.39, f32[1,4,4096]{2,0,1:T(1,128)S(1)} %copy.38, f32[17,2,4096]{2,0,1:T(8,128)} %bitcast.23, f32[6,4096]{1,0:T(8,128)S(1)} %pad_maximum_fusion.5, ...), kind=kLoop, calls=%fused_computation.7 | loop fusion | flops 6266880 | bytes 5677056 | tf_op jit(solution)/shard_map/add | solution.py:48
  32.3 0.1 slice.116
  32.4 1.7 %fusion.10 = f32[17,4,4096]{2,0,1:T(8,128)S(1)} fusion(f32[17,4,4096]{2,0,1:T(8,128)S(1)} %slice.116, f32[17,6,4096]{2,0,1:T(8,128)S(1)} %fusion.3, f32[4,4096]{1,0:T(4,128)S(1)} %broadcast_multiply_fusion, pred[4096]{0:T(1024)(128)(4,1)S(1)} %get-tuple-element.7, pred[4096]{0:T(1024)(128)(4,1)S(1)} %get-tuple-element.8), kind=kLoop, calls=%fused_computation.17 | loop fusion | flops 3063808 | bytes 4530176 | tf_op jit(solution)/shard_map/add | solution.py:48
  34.1 1.1 %copy-done.1 = f32[17,4,4096]{2,0,1:T(8,128)} copy-done((f32[17,4,4096]{2,0,1:T(8,128)}, f32[17,4,4096]{2,0,1:T(8,128)S(1)}, u32[]{:S(2)}) %copy-start.1) | copy-done | bytes 1114136
  35.2 2.1 %fusion.12 = f32[32,17]{0,1:T(8,128)S(1)} fusion(f32[17,4,4096]{2,0,1:T(8,128)S(1)} %fusion.10, f32[32,4,4096]{2,1,0:T(4,128)S(1)} %copy-done), kind=kOutput, calls=%fused_computation.23 | convolution fusion | flops 53477376 | bytes 3213440 | tf_op jit(solution)/shard_map/bzc,gzc->bg/dot_general | solution.py:96
  37.4 0.1 copy.43
  37.5 0.1 broadcast_in_dim.91
  37.6 0.6 broadcast_in_dim.92
  38.2 7.4 %all-to-all-start = ((f32[16,1,544]{2,1,0:T(1,128)}), f32[16,1,544]{2,1,0:T(1,128)S(1)}, u32[]{:S(2)}, u32[]{:S(2)}) async-start(f32[16,1,544]{2,1,0:T(1,128)} %broadcast_in_dim.92), calls=%async_computation | async-start | bytes 81920 | tf_op jit(solution)/shard_map/all_to_all | solution.py:62
  45.6 1.7 %fusion.15 = f32[4,4096]{1,0:T(4,128)S(1)} fusion(f32[17,4,4096]{2,0,1:T(8,128)} %copy-done.1), kind=kLoop, calls=%fused_computation.25 | loop fusion | flops 507904 | bytes 1114112 | tf_op jit(solution)/shard_map/reduce_sum | solution.py:95
  47.3 1.1 %slice.119 = f32[1,4,4096]{2,0,1:T(1,128)S(1)} slice(f32[17,4,4096]{2,0,1:T(8,128)} %copy-done.1), slice={[0:1], [0:4], [0:4096]} | slice | bytes 131072 | tf_op jit(solution)/shard_map/slice | solution.py:93
  48.4 4.7 %all-to-all-done = f32[16,1,544]{2,1,0:T(1,128)S(1)} async-done(((f32[16,1,544]{2,1,0:T(1,128)}), f32[16,1,544]{2,1,0:T(1,128)S(1)}, u32[]{:S(2)}, u32[]{:S(2)}) %all-to-all-start) | async-done | bytes 34848 | tf_op jit(solution)/shard_map/all_to_all | solution.py:62
  53.1 0.1 reshape.33
  53.2 0.2 fusion.18
  53.4 0.7 pad_maximum_fusion.6
  54.1 12.9 %all-to-all-start.1 = ((f32[5,32,128]{2,0,1:T(8,128)}), f32[5,32,128]{2,0,1:T(8,128)S(1)}, u32[]{:S(2)}, u32[]{:S(2)}) async-start(f32[5,32,128]{2,0,1:T(8,128)} %pad_maximum_fusion.6), calls=%async_computation.1 | async-start | bytes 262144 | tf_op jit(solution)/shard_map/all_to_all | solution.py:74
  67.0 0.1 slice_reduce_fusion
  67.1 9.2 %all-to-all-done.1 = f32[5,32,128]{2,0,1:T(8,128)S(1)} async-done(((f32[5,32,128]{2,0,1:T(8,128)}), f32[5,32,128]{2,0,1:T(8,128)S(1)}, u32[]{:S(2)}, u32[]{:S(2)}) %all-to-all-start.1) | async-done | bytes 81952 | tf_op jit(solution)/shard_map/all_to_all | solution.py:74
  76.4 0.6 slice_add_fusion.1
  77.0 0.6 select_reduce_fusion.1
  (18 shorter events, 0.4 us)
Async XLA Ops:
  0.6 34.6 %copy-start = (f32[32,4,4096]{2,1,0:T(4,128)S(1)}, f32[32,4,4096]{2,1,0:T(4,128)}, u32[]{:S(2)}) copy-start(f32[32,4,4096]{2,1,0:T(4,128)} %param.10) | copy-start | bytes 6291460
  5.8 13.8 %collective-permute-start = (f32[18,2,4096]{2,0,1:T(8,128)}, f32[18,2,4096]{2,0,1:T(8,128)}, u32[]{:S(2)}, u32[]{:S(2)}) collective-permute-start(f32[18,2,4096]{2,0,1:T(8,128)} %pad_maximum_fusion.4), channel_id=1, source_target_pairs={{0,32},{32,64},{64,96},{96,128},{128,160},{160,192},{192,224},{224... | collective-permute-start | bytes 1769480 | tf_op jit(solution)/shard_map/ppermute | solution.py:87
  11.4 13.6 %collective-permute-start.1 = (f32[18,2,4096]{2,0,1:T(8,128)}, f32[18,2,4096]{2,0,1:T(8,128)}, u32[]{:S(2)}, u32[]{:S(2)}) collective-permute-start(f32[18,2,4096]{2,0,1:T(8,128)} %fusion.17), channel_id=1, source_target_pairs={{32,0},{64,32},{96,64},{128,96},{160,128},{192,160},{224,192},{256... | collective-permute-start | bytes 1769480 | tf_op jit(solution)/shard_map/ppermute | solution.py:88
  34.1 1.2 %copy-start.1 = (f32[17,4,4096]{2,0,1:T(8,128)}, f32[17,4,4096]{2,0,1:T(8,128)S(1)}, u32[]{:S(2)}) copy-start(f32[17,4,4096]{2,0,1:T(8,128)S(1)} %fusion.10) | copy-start | bytes 3342340
  35.2 41.7 %copy-start.2 = (s32[128]{0:T(128)S(1)}, s32[128]{0:T(128)}, u32[]{:S(2)}) copy-start(s32[128]{0:T(128)} %param.11) | copy-start | bytes 1540
  38.2 14.8 %all-to-all-start = ((f32[16,1,544]{2,1,0:T(1,128)}), f32[16,1,544]{2,1,0:T(1,128)S(1)}, u32[]{:S(2)}, u32[]{:S(2)}) async-start(f32[16,1,544]{2,1,0:T(1,128)} %broadcast_in_dim.92), calls=%async_computation | async-start | bytes 81920 | tf_op jit(solution)/shard_map/all_to_all | solution.py:62
  54.1 22.2 %all-to-all-start.1 = ((f32[5,32,128]{2,0,1:T(8,128)}), f32[5,32,128]{2,0,1:T(8,128)S(1)}, u32[]{:S(2)}, u32[]{:S(2)}) async-start(f32[5,32,128]{2,0,1:T(8,128)} %pad_maximum_fusion.6), calls=%async_computation.1 | async-start | bytes 262144 | tf_op jit(solution)/shard_map/all_to_all | solution.py:74

commit v8 on v4

--- a/solution.py
+++ b/solution.py
@@ -57,9 +57,10 @@
 
 def exchange_sum(x, axis):
     size = lax.axis_size(axis)
-    copies = jnp.broadcast_to(x[None], (size,) + x.shape)
-    received = lax.all_to_all(copies, axis, 0, 0, tiled=False)
-    return jnp.sum(received, axis=0)
+    flat = x.reshape(-1)
+    copies = jnp.broadcast_to(flat[None], (size, flat.shape[0]))
+    received = lax.all_to_all(copies, axis, 0, 0, tiled=True)
+    return jnp.sum(received, axis=0).reshape(x.shape)
 
 
 def exchange_scatter(x, extra, axis):

time: 72.6 us -> 77.7 us (1.070)
  other arithmetic: 9.92 us -> 13.4 us
  local copies, waits for them, and re-layouts: 7.48 us -> 8.96 us
  starting transfers between devices: 30.4 us -> 31.2 us
    ppermute x1, waiting for transfers between devices: 3.2 us -> 1.81 us  [per_device(): before = lax.ppermute(upper, 'slab', up)]
    add x2, other arithmetic: 4.48 us -> 5.61 us  [update(): return middle + rate_field * (zsum + lateral(middle) - 6.0 * middle)]
    concatenate x1, other arithmetic: 0.25 us -> 1.36 us  [per_device(): fields = jnp.concatenate([before[:-1], body, after[:-1]], axis=1)]
    all_to_all x1, waiting for transfers between devices: 5.72 us -> 4.64 us  [exchange_sum(): received = lax.all_to_all(copies, axis, 0, 0, tiled=True)]
    all_to_all x1, waiting for transfers between devices: 7.85 us -> 8.82 us  [exchange_scatter(): received = jnp.sum(lax.all_to_all(message, axis, 0, 0, tiled=True), axis=0)]
    squeeze x1, local copies, waits for them, and re-layouts: 0.02 us -> 0.92 us  [per_device(): after[-1, :1]]
    squeeze x1, local copies, waits for them, and re-layouts: 0.02 us -> 0.92 us  [per_device(): before[-1, 1:]]
    concatenate x1, other arithmetic: 0.11 us -> 1 us  [per_device(): lower = jnp.concatenate([body[:, :2], rate_field[None, :2]], axis=0)]
  transfers between devices with their start and end apart: 4 -> 4, of which waited for: 4 -> 4; matrix products, arithmetic and copies ran while one was open for 4% -> 5% of each run, Pallas kernels for 0% -> 0%
where the time goes in v8:
time: 77.7 us; the launch traced here: 77.2 us
  starting transfers between devices  31.2 us (40%)
  waiting for transfers between devices  20.7 us (27%)
  other arithmetic  13.4 us (17%)
  local copies, waits for them, and re-layouts  8.96 us (12%)
  matrix products  2.13 us (3%)
  between operations  0.83 us (1%)
    all_to_all x1, starting transfers between devices, exchange_scatter(): received = jnp.sum(lax.all_to_all(message, axis, 0, 0, tiled=True), axis=0)  12.9 us
    all_to_all x1, waiting for transfers between devices, exchange_scatter(): received = jnp.sum(lax.all_to_all(message, axis, 0, 0, tiled=True), axis=0)  8.82 us
    all_to_all x1, starting transfers between devices, exchange_sum(): received = lax.all_to_all(copies, axis, 0, 0, tiled=True)  7.43 us
    ppermute x1, starting transfers between devices, per_device(): after = lax.ppermute(lower, 'slab', down)  6.34 us
    add x2, other arithmetic, update(): return middle + rate_field * (zsum + lateral(middle) - 6.0 * middle)  5.61 us
    ppermute x1, waiting for transfers between devices, per_device(): after = lax.ppermute(lower, 'slab', down)  5.43 us
    all_to_all x1, waiting for transfers between devices, exchange_sum(): received = lax.all_to_all(copies, axis, 0, 0, tiled=True)  4.64 us
    ppermute x1, starting transfers between devices, per_device(): before = lax.ppermute(upper, 'slab', up)  4.58 us
  transfers between devices with their start and end apart: 4, of which 4 were waited for; matrix products, arithmetic and copies ran while one was open for 5% of the time, Pallas kernels for 0%

profile of v8, /device:TPU:1, one launch (start us, length us, event | category | flops | bytes accessed | tf_op | source)
XLA Modules:
  0.0 77.2 jit_solution(6979337872806764251)
XLA Ops:
  0.6 2.0 %copy.43 = f32[16,4,4096]{2,0,1:T(8,128)S(1)} copy(f32[16,4,4096]{2,1,0:T(4,128)} %param.7) | data formatting | bytes 2097152 | tf_op args[1]
  2.6 0.9 %copy.42 = f32[1,4,4096]{2,0,1:T(1,128)S(1)} copy(f32[1,4,4096]{2,1,0:T(4,128)} %bitcast.31) | data formatting | bytes 131072 | tf_op jit(solution)/shard_map/broadcast_in_dim | solution.py:79
  3.5 1.1 %select_reduce_fusion = f32[4,4096]{1,0:T(4,128)S(1)} fusion(f32[8]{0:T(128)} %param.9, s32[4,4096]{1,0:T(4,128)} %param.8), kind=kLoop, calls=%fused_computation.30 | loop fusion | flops 376832 | bytes 131104 | tf_op jit(solution)/shard_map/reduce_sum | solution.py:31
  4.8 1.0 %pad_maximum_fusion.4 = f32[18,2,4096]{2,0,1:T(8,128)} fusion(f32[1,2,4096]{2,0,1:T(1,128)S(1)} %copy.44, f32[17,2,4096]{2,0,1:T(8,128)S(1)} %fusion.16), kind=kLoop, calls=%fused_computation.29 | loop fusion | flops 147456 | bytes 1179648 | tf_op jit(solution)/shard_map/concatenate | solution.py:85
  5.8 4.6 %collective-permute-start = (f32[18,2,4096]{2,0,1:T(8,128)}, f32[18,2,4096]{2,0,1:T(8,128)}, u32[]{:S(2)}, u32[]{:S(2)}) collective-permute-start(f32[18,2,4096]{2,0,1:T(8,128)} %pad_maximum_fusion.4), channel_id=1, source_target_pairs={{0,32},{32,64},{64,96},{96,128},{128,160},{160,192},{192,224},{224... | collective-permute-start | bytes 1769480 | tf_op jit(solution)/shard_map/ppermute | solution.py:86
  10.4 1.0 %fusion.17 = f32[18,2,4096]{2,0,1:T(8,128)} fusion(f32[16,4,4096]{2,0,1:T(8,128)S(1)} %copy.43, f32[1,4,4096]{2,0,1:T(1,128)S(1)} %copy.42, f32[1,2,4096]{2,0,1:T(1,128)S(1)} %copy.45), kind=kLoop, calls=%fused_computation.28 | loop fusion | flops 294912 | bytes 1736704 | tf_op jit(solution)/shard_map/concatenate | solution.py:84
  11.4 6.3 %collective-permute-start.1 = (f32[18,2,4096]{2,0,1:T(8,128)}, f32[18,2,4096]{2,0,1:T(8,128)}, u32[]{:S(2)}, u32[]{:S(2)}) collective-permute-start(f32[18,2,4096]{2,0,1:T(8,128)} %fusion.17), channel_id=1, source_target_pairs={{32,0},{64,32},{96,64},{128,96},{160,128},{192,160},{224,192},{256... | collective-permute-start | bytes 1769480 | tf_op jit(solution)/shard_map/ppermute | solution.py:87
  17.8 1.8 %collective-permute-done = f32[18,2,4096]{2,0,1:T(8,128)} collective-permute-done((f32[18,2,4096]{2,0,1:T(8,128)}, f32[18,2,4096]{2,0,1:T(8,128)}, u32[]{:S(2)}, u32[]{:S(2)}) %collective-permute-start) | collective-permute-done | bytes 589856 | tf_op jit(solution)/shard_map/ppermute | solution.py:86
  19.6 5.4 %collective-permute-done.1 = f32[18,2,4096]{2,0,1:T(8,128)} collective-permute-done((f32[18,2,4096]{2,0,1:T(8,128)}, f32[18,2,4096]{2,0,1:T(8,128)}, u32[]{:S(2)}, u32[]{:S(2)}) %collective-permute-start.1) | collective-permute-done | bytes 589856 | tf_op jit(solution)/shard_map/ppermute | solution.py:87
  25.1 1.4 %pad_maximum_fusion = f32[17,6,4096]{2,0,1:T(8,128)S(1)} fusion(f32[17,2,4096]{2,0,1:T(8,128)} %bitcast.27, f32[17,2,4096]{2,0,1:T(8,128)} %bitcast.28, f32[16,4,4096]{2,0,1:T(8,128)S(1)} %copy.43, f32[1,4,4096]{2,0,1:T(1,128)S(1)} %copy.42), kind=kLoop, calls=%fused_computation | loop fusion | flops 1253376 | bytes 3899392 | tf_op jit(solution)/shard_map/concatenate | solution.py:88
  26.4 0.9 %slice_bitcast_fusion.3 = f32[1,4096]{1,0:T(1,128)S(1)} fusion(f32[18,2,4096]{2,0,1:T(8,128)} %collective-permute-done), kind=kLoop, calls=%fused_computation.43 | loop fusion | bytes 32768 | tf_op jit(solution)/shard_map/squeeze | solution.py:89
  27.4 0.9 %slice_bitcast_fusion.2 = f32[1,4096]{1,0:T(1,128)S(1)} fusion(f32[18,2,4096]{2,0,1:T(8,128)} %collective-permute-done.1), kind=kLoop, calls=%fused_computation.42 | loop fusion | bytes 32768 | tf_op jit(solution)/shard_map/squeeze | solution.py:89
  28.3 3.9 %fusion.3 = f32[17,6,4096]{2,0,1:T(8,128)S(1)} fusion(f32[17,6,4096]{2,0,1:T(8,128)S(1)} %pad_maximum_fusion, f32[17,2,4096]{2,0,1:T(8,128)} %bitcast.27, f32[16,4,4096]{2,0,1:T(8,128)S(1)} %copy.43, f32[1,4,4096]{2,0,1:T(1,128)S(1)} %copy.42, f32[17,2,4096]{2,0,1:T(8,128)} %bitcast.28, f32[6,4096]{1,0:T(8,128)S(1)} %pad_maximum_fusion.5, ...), kind=kLoop, calls=%fused_computation.7 | loop fusion | flops 6266880 | bytes 5677056 | tf_op jit(solution)/shard_map/add | solution.py:48
  32.3 0.1 slice.116
  32.4 1.7 %fusion.10 = f32[17,4,4096]{2,0,1:T(8,128)S(1)} fusion(f32[17,4,4096]{2,0,1:T(8,128)S(1)} %slice.116, f32[17,6,4096]{2,0,1:T(8,128)S(1)} %fusion.3, f32[4,4096]{1,0:T(4,128)S(1)} %broadcast_multiply_fusion, pred[4096]{0:T(1024)(128)(4,1)S(1)} %get-tuple-element.7, pred[4096]{0:T(1024)(128)(4,1)S(1)} %get-tuple-element.8), kind=kLoop, calls=%fused_computation.17 | loop fusion | flops 3063808 | bytes 4530176 | tf_op jit(solution)/shard_map/add | solution.py:48
  34.1 1.1 %copy-done.1 = f32[17,4,4096]{2,0,1:T(8,128)} copy-done((f32[17,4,4096]{2,0,1:T(8,128)}, f32[17,4,4096]{2,0,1:T(8,128)S(1)}, u32[]{:S(2)}) %copy-start.1) | copy-done | bytes 1114136
  35.2 2.1 %fusion.12 = f32[32,17]{0,1:T(8,128)S(1)} fusion(f32[17,4,4096]{2,0,1:T(8,128)S(1)} %fusion.10, f32[32,4,4096]{2,1,0:T(4,128)S(1)} %copy-done), kind=kOutput, calls=%fused_computation.23 | convolution fusion | flops 53477376 | bytes 3213440 | tf_op jit(solution)/shard_map/bzc,gzc->bg/dot_general | solution.py:95
  37.4 0.1 copy.47
  37.5 0.1 broadcast_in_dim.89
  37.6 0.6 broadcast_in_dim.90
  38.2 7.4 %all-to-all-start = ((f32[16,1,544]{2,1,0:T(1,128)}), f32[16,1,544]{2,1,0:T(1,128)S(1)}, u32[]{:S(2)}, u32[]{:S(2)}) async-start(f32[16,1,544]{2,1,0:T(1,128)} %broadcast_in_dim.90), calls=%async_computation | async-start | bytes 81920 | tf_op jit(solution)/shard_map/all_to_all | solution.py:62
  45.6 1.7 %fusion.15 = f32[4,4096]{1,0:T(4,128)S(1)} fusion(f32[17,4,4096]{2,0,1:T(8,128)} %copy-done.1), kind=kLoop, calls=%fused_computation.25 | loop fusion | flops 507904 | bytes 1114112 | tf_op jit(solution)/shard_map/reduce_sum | solution.py:94
  47.3 1.1 %slice.119 = f32[1,4,4096]{2,0,1:T(1,128)S(1)} slice(f32[17,4,4096]{2,0,1:T(8,128)} %copy-done.1), slice={[0:1], [0:4], [0:4096]} | slice | bytes 131072 | tf_op jit(solution)/shard_map/slice | solution.py:92
  48.4 4.6 %all-to-all-done = f32[16,1,544]{2,1,0:T(1,128)S(1)} async-done(((f32[16,1,544]{2,1,0:T(1,128)}), f32[16,1,544]{2,1,0:T(1,128)S(1)}, u32[]{:S(2)}, u32[]{:S(2)}) %all-to-all-start) | async-done | bytes 34848 | tf_op jit(solution)/shard_map/all_to_all | solution.py:62
  53.1 0.1 reshape.40
  53.2 0.2 fusion.18
  53.4 0.7 copy.49
  54.1 12.9 %all-to-all-start.1 = ((f32[32,1,544]{2,1,0:T(1,128)}), f32[32,1,544]{2,1,0:T(1,128)S(1)}, u32[]{:S(2)}, u32[]{:S(2)}) async-start(f32[32,1,544]{2,1,0:T(1,128)} %copy.49), calls=%async_computation.1 | async-start | bytes 163840 | tf_op jit(solution)/shard_map/all_to_all | solution.py:73
  67.0 0.1 slice_reduce_fusion
  67.2 8.8 %all-to-all-done.1 = f32[32,1,544]{2,1,0:T(1,128)S(1)} async-done(((f32[32,1,544]{2,1,0:T(1,128)}), f32[32,1,544]{2,1,0:T(1,128)S(1)}, u32[]{:S(2)}, u32[]{:S(2)}) %all-to-all-start.1) | async-done | bytes 69664 | tf_op jit(solution)/shard_map/all_to_all | solution.py:73
  76.1 0.6 bitcast_add_fusion
  76.6 0.6 select_reduce_fusion.1
  (19 shorter events, 0.4 us)
Async XLA Ops:
  0.6 34.6 %copy-start = (f32[32,4,4096]{2,1,0:T(4,128)S(1)}, f32[32,4,4096]{2,1,0:T(4,128)}, u32[]{:S(2)}) copy-start(f32[32,4,4096]{2,1,0:T(4,128)} %param.10) | copy-start | bytes 6291460
  5.8 13.8 %collective-permute-start = (f32[18,2,4096]{2,0,1:T(8,128)}, f32[18,2,4096]{2,0,1:T(8,128)}, u32[]{:S(2)}, u32[]{:S(2)}) collective-permute-start(f32[18,2,4096]{2,0,1:T(8,128)} %pad_maximum_fusion.4), channel_id=1, source_target_pairs={{0,32},{32,64},{64,96},{96,128},{128,160},{160,192},{192,224},{224... | collective-permute-start | bytes 1769480 | tf_op jit(solution)/shard_map/ppermute | solution.py:86
  11.4 13.6 %collective-permute-start.1 = (f32[18,2,4096]{2,0,1:T(8,128)}, f32[18,2,4096]{2,0,1:T(8,128)}, u32[]{:S(2)}, u32[]{:S(2)}) collective-permute-start(f32[18,2,4096]{2,0,1:T(8,128)} %fusion.17), channel_id=1, source_target_pairs={{32,0},{64,32},{96,64},{128,96},{160,128},{192,160},{224,192},{256... | collective-permute-start | bytes 1769480 | tf_op jit(solution)/shard_map/ppermute | solution.py:87
  34.1 1.2 %copy-start.1 = (f32[17,4,4096]{2,0,1:T(8,128)}, f32[17,4,4096]{2,0,1:T(8,128)S(1)}, u32[]{:S(2)}) copy-start(f32[17,4,4096]{2,0,1:T(8,128)S(1)} %fusion.10) | copy-start | bytes 3342340
  35.2 41.4 %copy-start.2 = (s32[128]{0:T(128)S(1)}, s32[128]{0:T(128)}, u32[]{:S(2)}) copy-start(s32[128]{0:T(128)} %param.11) | copy-start | bytes 1540
  38.2 14.8 %all-to-all-start = ((f32[16,1,544]{2,1,0:T(1,128)}), f32[16,1,544]{2,1,0:T(1,128)S(1)}, u32[]{:S(2)}, u32[]{:S(2)}) async-start(f32[16,1,544]{2,1,0:T(1,128)} %broadcast_in_dim.90), calls=%async_computation | async-start | bytes 81920 | tf_op jit(solution)/shard_map/all_to_all | solution.py:62
  54.1 21.8 %all-to-all-start.1 = ((f32[32,1,544]{2,1,0:T(1,128)}), f32[32,1,544]{2,1,0:T(1,128)S(1)}, u32[]{:S(2)}, u32[]{:S(2)}) async-start(f32[32,1,544]{2,1,0:T(1,128)} %copy.49), calls=%async_computation.1 | async-start | bytes 163840 | tf_op jit(solution)/shard_map/all_to_all | solution.py:73

commit v9 on v4

--- a/solution.py
+++ b/solution.py
@@ -80,12 +80,19 @@
     up = [(i, i + 1) for i in range(size - 1)]
     down = [(j, i) for i, j in up]
     planes = body.shape[1]
-    lower = jnp.concatenate([body[:, :2], rate_field[None, :2]], axis=0)
-    upper = jnp.concatenate([body[:, planes - 2 :], rate_field[None, planes - 2 :]], axis=0)
+    classes = conductivity.astype(jnp.float32)
+    lower = jnp.concatenate([body[:, :2], classes[None, :2]], axis=0)
+    upper = jnp.concatenate([body[:, planes - 2 :], classes[None, planes - 2 :]], axis=0)
     before = lax.ppermute(upper, "slab", up)
     after = lax.ppermute(lower, "slab", down)
     fields = jnp.concatenate([before[:-1], body, after[:-1]], axis=1)
-    rate_ext = jnp.concatenate([before[-1, 1:], rate_field, after[-1, :1]], axis=0)
+    edges = jnp.concatenate([before[-1, 1:], after[-1, :1]], axis=0).astype(jnp.int32)
+    edge_rate = lookup_rate(edges, cond_table)
+    valid = jnp.concatenate(
+        [(lax.axis_index("slab") > 0)[None], (lax.axis_index("slab") < size - 1)[None]]
+    )
+    edge_rate = jnp.where(valid[:, None], edge_rate, jnp.float32(0.0))
+    rate_ext = jnp.concatenate([edge_rate[:1], rate_field, edge_rate[1:]], axis=0)
     fields = update(fields, rate_ext)
     fields = update(fields, rate_field)
     centre_moved = fields[0]

time: 72.6 us -> 77.9 us (1.073)
  other arithmetic: 9.92 us -> 14.3 us
  local copies, waits for them, and re-layouts: 7.48 us -> 9.32 us
  waiting for transfers between devices: 21.3 us -> 19.5 us
  starting transfers between devices: 30.4 us -> 31.2 us
    concatenate x3 -> x4, other arithmetic: 0.24 us -> 2.09 us  [the longest x1 1 us: per_device(): lower = jnp.concatenate([body[:, :2], classes[None, :2]], axis=0)]
    concatenate x0 -> x2, local copies, waits for them, and re-layouts: none -> 1.84 us  [per_device(): jnp.concatenate([before[-1, 1:], after[-1, :1]], axis=0).astype(jnp.int32)]
    ppermute x1, waiting for transfers between devices: 3.2 us -> 1.43 us  [per_device(): before = lax.ppermute(upper, 'slab', up)]
    add x2, other arithmetic: 4.48 us -> 5.6 us  [update(): return middle + rate_field * (zsum + lateral(middle) - 6.0 * middle)]
    concatenate x1, other arithmetic: 0.25 us -> 1.37 us  [per_device(): fields = jnp.concatenate([before[:-1], body, after[:-1]], axis=1)]
    convert_element_type x0 -> x2, other arithmetic: none -> 0.89 us  [the longest x1 0.85 us: per_device(): classes = conductivity.astype(jnp.float32)]
    ppermute x1, starting transfers between devices: 5.53 us -> 6.34 us  [per_device(): after = lax.ppermute(lower, 'slab', down)]
    unnamed x11 -> x15, local copies, waits for them, and re-layouts: 4.01 us -> 4.02 us
  transfers between devices with their start and end apart: 4 -> 4, of which waited for: 4 -> 4; matrix products, arithmetic and copies ran while one was open for 4% -> 7% of each run, Pallas kernels for 0% -> 0%
where the time goes in v9:
time: 77.9 us; the launch traced here: 77.4 us
  starting transfers between devices  31.2 us (40%)
  waiting for transfers between devices  19.5 us (25%)
  other arithmetic  14.3 us (18%)
  local copies, waits for them, and re-layouts  9.32 us (12%)
  matrix products  2.13 us (3%)
  between operations  0.91 us (1%)
    all_to_all x1, starting transfers between devices, exchange_scatter(): received = jnp.sum(lax.all_to_all(message, axis, 0, 0, tiled=True), axis=0)  12.9 us
    all_to_all x1, waiting for transfers between devices, exchange_scatter(): received = jnp.sum(lax.all_to_all(message, axis, 0, 0, tiled=True), axis=0)  7.85 us
    all_to_all x1, starting transfers between devices, exchange_sum(): received = lax.all_to_all(copies, axis, 0, 0, tiled=False)  7.42 us
    ppermute x1, starting transfers between devices, per_device(): after = lax.ppermute(lower, 'slab', down)  6.34 us
    all_to_all x1, waiting for transfers between devices, exchange_sum(): received = lax.all_to_all(copies, axis, 0, 0, tiled=False)  5.72 us
    add x2, other arithmetic, update(): return middle + rate_field * (zsum + lateral(middle) - 6.0 * middle)  5.6 us
    ppermute x1, starting transfers between devices, per_device(): before = lax.ppermute(upper, 'slab', up)  4.58 us
    ppermute x1, waiting for transfers between devices, per_device(): after = lax.ppermute(lower, 'slab', down)  4.51 us
  transfers between devices with their start and end apart: 4, of which 4 were waited for; matrix products, arithmetic and copies ran while one was open for 7% of the time, Pallas kernels for 0%

profile of v9, /device:TPU:1, one launch (start us, length us, event | category | flops | bytes accessed | tf_op | source)
XLA Modules:
  0.0 77.4 jit_solution(4444121106267096087)
XLA Ops:
  0.6 2.0 %copy.31 = f32[16,4,4096]{2,0,1:T(8,128)S(1)} copy(f32[16,4,4096]{2,1,0:T(4,128)} %param.7) | data formatting | bytes 2097152 | tf_op args[1]
  2.6 0.9 %copy.30 = f32[1,4,4096]{2,0,1:T(1,128)S(1)} copy(f32[1,4,4096]{2,1,0:T(4,128)} %bitcast.41) | data formatting | bytes 131072 | tf_op jit(solution)/shard_map/broadcast_in_dim | solution.py:78
  3.5 0.9 %convert_element_type.14 = f32[4,4096]{1,0:T(4,128)S(1)} convert(s32[4,4096]{1,0:T(4,128)} %param.8) | non-fusion elementwise | flops 16384 | bytes 131072 | tf_op jit(solution)/shard_map/convert_element_type | solution.py:83
  4.6 1.0 %pad_maximum_fusion.4 = f32[18,2,4096]{2,0,1:T(8,128)} fusion(f32[1,2,4096]{2,0,1:T(1,128)S(1)} %copy.32, f32[17,2,4096]{2,0,1:T(8,128)S(1)} %fusion.16), kind=kLoop, calls=%fused_computation.29 | loop fusion | flops 147456 | bytes 1179648 | tf_op jit(solution)/shard_map/concatenate | solution.py:85
  5.6 4.6 %collective-permute-start = (f32[18,2,4096]{2,0,1:T(8,128)}, f32[18,2,4096]{2,0,1:T(8,128)}, u32[]{:S(2)}, u32[]{:S(2)}) collective-permute-start(f32[18,2,4096]{2,0,1:T(8,128)} %pad_maximum_fusion.4), channel_id=1, source_target_pairs={{0,32},{32,64},{64,96},{96,128},{128,160},{160,192},{192,224},{224... | collective-permute-start | bytes 1769480 | tf_op jit(solution)/shard_map/ppermute | solution.py:86
  10.2 1.0 %fusion.17 = f32[18,2,4096]{2,0,1:T(8,128)} fusion(f32[16,4,4096]{2,0,1:T(8,128)S(1)} %copy.31, f32[1,4,4096]{2,0,1:T(1,128)S(1)} %copy.30, f32[1,2,4096]{2,0,1:T(1,128)S(1)} %copy.33), kind=kLoop, calls=%fused_computation.28 | loop fusion | flops 294912 | bytes 1736704 | tf_op jit(solution)/shard_map/concatenate | solution.py:84
  11.2 6.3 %collective-permute-start.1 = (f32[18,2,4096]{2,0,1:T(8,128)}, f32[18,2,4096]{2,0,1:T(8,128)}, u32[]{:S(2)}, u32[]{:S(2)}) collective-permute-start(f32[18,2,4096]{2,0,1:T(8,128)} %fusion.17), channel_id=1, source_target_pairs={{32,0},{64,32},{96,64},{128,96},{160,128},{192,160},{224,192},{256... | collective-permute-start | bytes 1769480 | tf_op jit(solution)/shard_map/ppermute | solution.py:87
  17.6 0.2 select_reduce_fusion
  17.9 1.4 %collective-permute-done = f32[18,2,4096]{2,0,1:T(8,128)} collective-permute-done((f32[18,2,4096]{2,0,1:T(8,128)}, f32[18,2,4096]{2,0,1:T(8,128)}, u32[]{:S(2)}, u32[]{:S(2)}) %collective-permute-start) | collective-permute-done | bytes 589856 | tf_op jit(solution)/shard_map/ppermute | solution.py:86
  19.4 0.9 %slice_bitcast_fusion.3 = f32[1,4096]{1,0:T(1,128)S(1)} fusion(f32[18,2,4096]{2,0,1:T(8,128)} %collective-permute-done), kind=kLoop, calls=%fused_computation.44 | loop fusion | bytes 32768 | tf_op jit(solution)/shard_map/concatenate | solution.py:89
  20.3 4.5 %collective-permute-done.1 = f32[18,2,4096]{2,0,1:T(8,128)} collective-permute-done((f32[18,2,4096]{2,0,1:T(8,128)}, f32[18,2,4096]{2,0,1:T(8,128)}, u32[]{:S(2)}, u32[]{:S(2)}) %collective-permute-start.1) | collective-permute-done | bytes 589856 | tf_op jit(solution)/shard_map/ppermute | solution.py:87
  24.8 0.9 %slice_bitcast_fusion.2 = f32[1,4096]{1,0:T(1,128)S(1)} fusion(f32[18,2,4096]{2,0,1:T(8,128)} %collective-permute-done.1), kind=kLoop, calls=%fused_computation.43 | loop fusion | bytes 32768 | tf_op jit(solution)/shard_map/concatenate | solution.py:89
  25.8 0.2 select_reduce_fusion.1
  26.1 1.4 %pad_maximum_fusion = f32[17,6,4096]{2,0,1:T(8,128)S(1)} fusion(f32[17,2,4096]{2,0,1:T(8,128)} %bitcast.37, f32[17,2,4096]{2,0,1:T(8,128)} %bitcast.38, f32[16,4,4096]{2,0,1:T(8,128)S(1)} %copy.31, f32[1,4,4096]{2,0,1:T(1,128)S(1)} %copy.30), kind=kLoop, calls=%fused_computation | loop fusion | flops 1253376 | bytes 3899392 | tf_op jit(solution)/shard_map/concatenate | solution.py:88
  27.5 3.9 %fusion.3 = f32[17,6,4096]{2,0,1:T(8,128)S(1)} fusion(f32[17,6,4096]{2,0,1:T(8,128)S(1)} %pad_maximum_fusion, f32[17,2,4096]{2,0,1:T(8,128)} %bitcast.37, f32[16,4,4096]{2,0,1:T(8,128)S(1)} %copy.31, f32[1,4,4096]{2,0,1:T(1,128)S(1)} %copy.30, f32[17,2,4096]{2,0,1:T(8,128)} %bitcast.38, f32[6,4096]{1,0:T(8,128)S(1)} %pad_maximum_fusion.5, ...), kind=kLoop, calls=%fused_computation.7 | loop fusion | flops 6266880 | bytes 5677056 | tf_op jit(solution)/shard_map/add | solution.py:48
  31.4 0.1 slice.126
  31.5 1.7 %fusion.10 = f32[17,4,4096]{2,0,1:T(8,128)S(1)} fusion(f32[17,4,4096]{2,0,1:T(8,128)S(1)} %slice.126, f32[17,6,4096]{2,0,1:T(8,128)S(1)} %fusion.3, f32[4,4096]{1,0:T(4,128)S(1)} %broadcast_multiply_fusion, pred[4096]{0:T(1024)(128)(4,1)S(1)} %get-tuple-element.9, pred[4096]{0:T(1024)(128)(4,1)S(1)} %get-tuple-element.10), kind=kLoop, calls=%fused_computation.17 | loop fusion | flops 3063808 | bytes 4530176 | tf_op jit(solution)/shard_map/add | solution.py:48
  33.2 1.1 %copy-done.1 = f32[17,4,4096]{2,0,1:T(8,128)} copy-done((f32[17,4,4096]{2,0,1:T(8,128)}, f32[17,4,4096]{2,0,1:T(8,128)S(1)}, u32[]{:S(2)}) %copy-start.1) | copy-done | bytes 1114136
  34.4 2.1 %fusion.12 = f32[32,17]{0,1:T(8,128)S(1)} fusion(f32[17,4,4096]{2,0,1:T(8,128)S(1)} %fusion.10, f32[32,4,4096]{2,1,0:T(4,128)S(1)} %copy-done), kind=kOutput, calls=%fused_computation.23 | convolution fusion | flops 53477376 | bytes 3213440 | tf_op jit(solution)/shard_map/bzc,gzc->bg/dot_general | solution.py:101
  36.5 0.7 reshape.49
  37.3 7.4 %all-to-all-start = ((f32[16,1,544]{2,1,0:T(1,128)}), f32[16,1,544]{2,1,0:T(1,128)S(1)}, u32[]{:S(2)}, u32[]{:S(2)}) async-start(f32[16,1,544]{2,1,0:T(1,128)} %reshape.49), calls=%async_computation | async-start | bytes 81920 | tf_op jit(solution)/shard_map/all_to_all | solution.py:61
  44.7 1.7 %fusion.15 = f32[4,4096]{1,0:T(4,128)S(1)} fusion(f32[17,4,4096]{2,0,1:T(8,128)} %copy-done.1), kind=kLoop, calls=%fused_computation.25 | loop fusion | flops 507904 | bytes 1114112 | tf_op jit(solution)/shard_map/reduce_sum | solution.py:100
  46.4 5.7 %all-to-all-done = f32[16,1,544]{2,1,0:T(1,128)S(1)} async-done(((f32[16,1,544]{2,1,0:T(1,128)}), f32[16,1,544]{2,1,0:T(1,128)S(1)}, u32[]{:S(2)}, u32[]{:S(2)}) %all-to-all-start) | async-done | bytes 34848 | tf_op jit(solution)/shard_map/all_to_all | solution.py:61
  52.1 0.5 broadcast.26
  52.6 0.7 reduce.1
  53.4 0.1 reshape.50
  53.6 0.7 copy.35
  54.3 12.9 %all-to-all-start.1 = ((f32[32,1,544]{2,1,0:T(1,128)}), f32[32,1,544]{2,1,0:T(1,128)S(1)}, u32[]{:S(2)}, u32[]{:S(2)}) async-start(f32[32,1,544]{2,1,0:T(1,128)} %copy.35), calls=%async_computation.1 | async-start | bytes 163840 | tf_op jit(solution)/shard_map/all_to_all | solution.py:72
  67.2 1.1 %slice.129 = f32[1,4,4096]{2,0,1:T(1,128)S(1)} slice(f32[17,4,4096]{2,0,1:T(8,128)} %copy-done.1), slice={[0:1], [0:4], [0:4096]} | slice | bytes 131072 | tf_op jit(solution)/shard_map/slice | solution.py:98
  68.3 7.8 %all-to-all-done.1 = f32[32,1,544]{2,1,0:T(1,128)S(1)} async-done(((f32[32,1,544]{2,1,0:T(1,128)}), f32[32,1,544]{2,1,0:T(1,128)S(1)}, u32[]{:S(2)}, u32[]{:S(2)}) %all-to-all-start.1) | async-done | bytes 69664 | tf_op jit(solution)/shard_map/all_to_all | solution.py:72
  76.2 0.6 bitcast_add_fusion
  76.8 0.6 select_reduce_fusion.2
  (29 shorter events, 0.7 us)
Async XLA Ops:
  0.6 33.7 %copy-start = (f32[32,4,4096]{2,1,0:T(4,128)S(1)}, f32[32,4,4096]{2,1,0:T(4,128)}, u32[]{:S(2)}) copy-start(f32[32,4,4096]{2,1,0:T(4,128)} %param.10) | copy-start | bytes 6291460
  4.5 13.1 %copy-start.2 = (s32[4,4096]{1,0:T(4,128)S(1)}, s32[4,4096]{1,0:T(4,128)}, u32[]{:S(2)}) copy-start(s32[4,4096]{1,0:T(4,128)} %param.8) | copy-start | bytes 196612
  4.5 13.1 %copy-start.3 = (f32[8]{0:T(128)S(1)}, f32[8]{0:T(128)}, u32[]{:S(2)}) copy-start(f32[8]{0:T(128)} %param.9) | copy-start | bytes 100
  5.6 13.8 %collective-permute-start = (f32[18,2,4096]{2,0,1:T(8,128)}, f32[18,2,4096]{2,0,1:T(8,128)}, u32[]{:S(2)}, u32[]{:S(2)}) collective-permute-start(f32[18,2,4096]{2,0,1:T(8,128)} %pad_maximum_fusion.4), channel_id=1, source_target_pairs={{0,32},{32,64},{64,96},{96,128},{128,160},{160,192},{192,224},{224... | collective-permute-start | bytes 1769480 | tf_op jit(solution)/shard_map/ppermute | solution.py:86
  11.2 13.6 %collective-permute-start.1 = (f32[18,2,4096]{2,0,1:T(8,128)}, f32[18,2,4096]{2,0,1:T(8,128)}, u32[]{:S(2)}, u32[]{:S(2)}) collective-permute-start(f32[18,2,4096]{2,0,1:T(8,128)} %fusion.17), channel_id=1, source_target_pairs={{32,0},{64,32},{96,64},{128,96},{160,128},{192,160},{224,192},{256... | collective-permute-start | bytes 1769480 | tf_op jit(solution)/shard_map/ppermute | solution.py:87
  33.2 1.2 %copy-start.1 = (f32[17,4,4096]{2,0,1:T(8,128)}, f32[17,4,4096]{2,0,1:T(8,128)S(1)}, u32[]{:S(2)}) copy-start(f32[17,4,4096]{2,0,1:T(8,128)S(1)} %fusion.10) | copy-start | bytes 3342340
  36.5 40.3 %copy-start.4 = (s32[128]{0:T(128)S(1)}, s32[128]{0:T(128)}, u32[]{:S(2)}) copy-start(s32[128]{0:T(128)} %param.11) | copy-start | bytes 1540
  37.3 14.8 %all-to-all-start = ((f32[16,1,544]{2,1,0:T(1,128)}), f32[16,1,544]{2,1,0:T(1,128)S(1)}, u32[]{:S(2)}, u32[]{:S(2)}) async-start(f32[16,1,544]{2,1,0:T(1,128)} %reshape.49), calls=%async_computation | async-start | bytes 81920 | tf_op jit(solution)/shard_map/all_to_all | solution.py:61
  54.3 21.8 %all-to-all-start.1 = ((f32[32,1,544]{2,1,0:T(1,128)}), f32[32,1,544]{2,1,0:T(1,128)S(1)}, u32[]{:S(2)}, u32[]{:S(2)}) async-start(f32[32,1,544]{2,1,0:T(1,128)} %copy.35), calls=%async_computation.1 | async-start | bytes 163840 | tf_op jit(solution)/shard_map/all_to_all | solution.py:72

commit v10 on v4

--- a/solution.py
+++ b/solution.py
@@ -92,7 +92,7 @@
     gens_moved = fields[1:]
     radius_local = jnp.sum(jnp.abs(gens_moved), axis=0)
     all_proj = jnp.einsum(
-        "bzc,gzc->bg", direction_bank, fields, precision=lax.Precision.HIGH
+        "bzc,gzc->bg", direction_bank, fields, precision=lax.Precision.HIGHEST
     )
     summed = exchange_sum(all_proj, "slab")
     summed_centre, summed_proj = summed[:, 0], summed[:, 1:]

time: 72.6 us -> 73.3 us (level)
  no operation moved by 1% of the time
where the time goes in v10:
time: 73.3 us; the launch traced here: 72.8 us
  starting transfers between devices  30.4 us (41%)
  waiting for transfers between devices  21.3 us (29%)
  other arithmetic  9.92 us (14%)
  local copies, waits for them, and re-layouts  7.47 us (10%)
  matrix products  2.81 us (4%)
  between operations  0.87 us (1%)
    all_to_all x1, starting transfers between devices, exchange_scatter(): received = jnp.sum(lax.all_to_all(message, axis, 0, 0, tiled=True), axis=0)  12.9 us
    all_to_all x1, waiting for transfers between devices, exchange_scatter(): received = jnp.sum(lax.all_to_all(message, axis, 0, 0, tiled=True), axis=0)  7.85 us
    all_to_all x1, starting transfers between devices, exchange_sum(): received = lax.all_to_all(copies, axis, 0, 0, tiled=False)  7.43 us
    all_to_all x1, waiting for transfers between devices, exchange_sum(): received = lax.all_to_all(copies, axis, 0, 0, tiled=False)  5.72 us
    ppermute x1, starting transfers between devices, per_device(): after = lax.ppermute(lower, 'slab', down)  5.53 us
    ppermute x1, starting transfers between devices, per_device(): before = lax.ppermute(upper, 'slab', up)  4.59 us
    ppermute x1, waiting for transfers between devices, per_device(): after = lax.ppermute(lower, 'slab', down)  4.56 us
    add x2, other arithmetic, update(): return middle + rate_field * (zsum + lateral(middle) - 6.0 * middle)  4.48 us
  transfers between devices with their start and end apart: 4, of which 4 were waited for; matrix products, arithmetic and copies ran while one was open for 4% of the time, Pallas kernels for 0%

profile of v10, /device:TPU:1, one launch (start us, length us, event | category | flops | bytes accessed | tf_op | source)
XLA Modules:
  0.0 72.8 jit_solution(16013070698154751832)
XLA Ops:
  0.6 0.0 copy-start
  0.6 2.0 %copy.31 = f32[16,4,4096]{2,0,1:T(8,128)S(1)} copy(f32[16,4,4096]{2,1,0:T(4,128)} %param.7) | data formatting | bytes 2097152 | tf_op args[1]
  2.6 0.9 %copy.30 = f32[1,4,4096]{2,0,1:T(1,128)S(1)} copy(f32[1,4,4096]{2,1,0:T(4,128)} %bitcast.43) | data formatting | bytes 131072 | tf_op jit(solution)/shard_map/broadcast_in_dim | solution.py:78
  3.5 1.1 %select_reduce_fusion = f32[4,4096]{1,0:T(4,128)S(1)} fusion(f32[8]{0:T(128)} %param.9, s32[4,4096]{1,0:T(4,128)} %param.8), kind=kLoop, calls=%fused_computation.30 | loop fusion | flops 376832 | bytes 131104 | tf_op jit(solution)/shard_map/reduce_sum | solution.py:31
  4.8 0.1 fusion.16
  4.8 0.1 pad_maximum_fusion.4
  4.9 4.6 %collective-permute-start = (f32[18,2,4096]{2,0,1:T(8,128)S(1)}, f32[18,2,4096]{2,0,1:T(8,128)S(1)}, u32[]{:S(2)}, u32[]{:S(2)}) collective-permute-start(f32[18,2,4096]{2,0,1:T(8,128)S(1)} %pad_maximum_fusion.4), channel_id=1, source_target_pairs={{0,32},{32,64},{64,96},{96,128},{128,160},{160,192},{192,224},{224... | collective-permute-start | bytes 1769480 | tf_op jit(solution)/shard_map/ppermute | solution.py:85
  9.6 0.1 fusion.17
  9.7 5.5 %collective-permute-start.1 = (f32[18,2,4096]{2,0,1:T(8,128)S(1)}, f32[18,2,4096]{2,0,1:T(8,128)S(1)}, u32[]{:S(2)}, u32[]{:S(2)}) collective-permute-start(f32[18,2,4096]{2,0,1:T(8,128)S(1)} %fusion.17), channel_id=1, source_target_pairs={{32,0},{64,32},{96,64},{128,96},{160,128},{192,160},{224,192},{256... | collective-permute-start | bytes 1769480 | tf_op jit(solution)/shard_map/ppermute | solution.py:86
  15.3 3.2 %collective-permute-done = f32[18,2,4096]{2,0,1:T(8,128)S(1)} collective-permute-done((f32[18,2,4096]{2,0,1:T(8,128)S(1)}, f32[18,2,4096]{2,0,1:T(8,128)S(1)}, u32[]{:S(2)}, u32[]{:S(2)}) %collective-permute-start) | collective-permute-done | bytes 589856 | tf_op jit(solution)/shard_map/ppermute | solution.py:85
  18.4 4.6 %collective-permute-done.1 = f32[18,2,4096]{2,0,1:T(8,128)S(1)} collective-permute-done((f32[18,2,4096]{2,0,1:T(8,128)S(1)}, f32[18,2,4096]{2,0,1:T(8,128)S(1)}, u32[]{:S(2)}, u32[]{:S(2)}) %collective-permute-start.1) | collective-permute-done | bytes 589856 | tf_op jit(solution)/shard_map/ppermute | solution.py:86
  23.0 0.3 pad_maximum_fusion
  23.4 2.8 %fusion.3 = f32[17,6,4096]{2,0,1:T(8,128)S(1)} fusion(f32[17,6,4096]{2,0,1:T(8,128)S(1)} %pad_maximum_fusion, f32[17,2,4096]{2,0,1:T(8,128)S(1)} %bitcast.40, f32[16,4,4096]{2,0,1:T(8,128)S(1)} %copy.31, f32[1,4,4096]{2,0,1:T(1,128)S(1)} %copy.30, f32[17,2,4096]{2,0,1:T(8,128)S(1)} %bitcast.38, f32[6,4096]{1,0:T(8,128)S(1)} %pad_maximum_fusion.5, ...), kind=kLoop, calls=%fused_computation.7 | loop fusion | flops 6266880 | bytes 5677056 | tf_op jit(solution)/shard_map/add | solution.py:48
  26.2 0.1 slice.116
  26.3 1.7 %fusion.10 = f32[17,4,4096]{2,0,1:T(8,128)S(1)} fusion(f32[17,4,4096]{2,0,1:T(8,128)S(1)} %slice.116, f32[17,6,4096]{2,0,1:T(8,128)S(1)} %fusion.3, f32[4,4096]{1,0:T(4,128)S(1)} %broadcast_multiply_fusion, pred[4096]{0:T(1024)(128)(4,1)S(1)} %get-tuple-element.7, pred[4096]{0:T(1024)(128)(4,1)S(1)} %get-tuple-element.8), kind=kLoop, calls=%fused_computation.17 | loop fusion | flops 3063808 | bytes 4530176 | tf_op jit(solution)/shard_map/add | solution.py:48
  28.0 1.1 %copy-done.1 = f32[17,4,4096]{2,0,1:T(8,128)} copy-done((f32[17,4,4096]{2,0,1:T(8,128)}, f32[17,4,4096]{2,0,1:T(8,128)S(1)}, u32[]{:S(2)}) %copy-start.1) | copy-done | bytes 1114136
  29.1 2.8 %fusion.12 = f32[32,17]{0,1:T(8,128)S(1)} fusion(f32[17,4,4096]{2,0,1:T(8,128)S(1)} %fusion.10, f32[32,4,4096]{2,1,0:T(4,128)S(1)} %copy-done), kind=kOutput, calls=%fused_computation.23 | convolution fusion | flops 106954752 | bytes 3213440 | tf_op jit(solution)/shard_map/bzc,gzc->bg/dot_general | solution.py:94
  32.0 0.0 copy-start.2
  32.0 0.7 %reshape.33 = f32[16,1,544]{2,1,0:T(1,128)} reshape(f32[16,17,32]{2,1,0:T(8,128)S(1)} %broadcast_bitcast_fusion) | data formatting | bytes 69632
  32.7 7.4 %all-to-all-start = ((f32[16,1,544]{2,1,0:T(1,128)}), f32[16,1,544]{2,1,0:T(1,128)S(1)}, u32[]{:S(2)}, u32[]{:S(2)}) async-start(f32[16,1,544]{2,1,0:T(1,128)} %reshape.33), calls=%async_computation | async-start | bytes 81920 | tf_op jit(solution)/shard_map/all_to_all | solution.py:61
  40.2 1.7 %fusion.15 = f32[4,4096]{1,0:T(4,128)S(1)} fusion(f32[17,4,4096]{2,0,1:T(8,128)} %copy-done.1), kind=kLoop, calls=%fused_computation.25 | loop fusion | flops 507904 | bytes 1114112 | tf_op jit(solution)/shard_map/reduce_sum | solution.py:93
  41.9 5.7 %all-to-all-done = f32[16,1,544]{2,1,0:T(1,128)S(1)} async-done(((f32[16,1,544]{2,1,0:T(1,128)}), f32[16,1,544]{2,1,0:T(1,128)S(1)}, u32[]{:S(2)}, u32[]{:S(2)}) %all-to-all-start) | async-done | bytes 34848 | tf_op jit(solution)/shard_map/all_to_all | solution.py:61
  47.6 0.5 broadcast.25
  48.1 0.7 %reduce.1 = f32[16,544]{1,0:T(8,128)S(1)} reduce(f32[16,1,544]{2,1,0:T(1,128)S(1)} %all-to-all-done, f32[]{:T(128)} %broadcast.25), dimensions={1}, to_apply=%all_to_all.9.reduce_sub_computation | reduce | bytes 69636 | tf_op jit(solution)/shard_map/all_to_all | solution.py:61
  48.8 0.1 reshape.34
  49.0 0.7 copy.35
  49.7 12.9 %all-to-all-start.1 = ((f32[32,1,544]{2,1,0:T(1,128)}), f32[32,1,544]{2,1,0:T(1,128)S(1)}, u32[]{:S(2)}, u32[]{:S(2)}) async-start(f32[32,1,544]{2,1,0:T(1,128)} %copy.35), calls=%async_computation.1 | async-start | bytes 163840 | tf_op jit(solution)/shard_map/all_to_all | solution.py:72
  62.6 1.1 %slice.119 = f32[1,4,4096]{2,0,1:T(1,128)S(1)} slice(f32[17,4,4096]{2,0,1:T(8,128)} %copy-done.1), slice={[0:1], [0:4], [0:4096]} | slice | bytes 131072 | tf_op jit(solution)/shard_map/slice | solution.py:91
  63.7 7.8 %all-to-all-done.1 = f32[32,1,544]{2,1,0:T(1,128)S(1)} async-done(((f32[32,1,544]{2,1,0:T(1,128)}), f32[32,1,544]{2,1,0:T(1,128)S(1)}, u32[]{:S(2)}, u32[]{:S(2)}) %all-to-all-start.1) | async-done | bytes 69664 | tf_op jit(solution)/shard_map/all_to_all | solution.py:72
  71.6 0.1 reduce_sum.58
  71.7 0.6 bitcast_add_fusion
  72.2 0.6 select_reduce_fusion.1
  (19 shorter events, 0.3 us)
Async XLA Ops:
  0.6 28.5 %copy-start = (f32[32,4,4096]{2,1,0:T(4,128)S(1)}, f32[32,4,4096]{2,1,0:T(4,128)}, u32[]{:S(2)}) copy-start(f32[32,4,4096]{2,1,0:T(4,128)} %param.10) | copy-start | bytes 6291460
  4.9 13.5 %collective-permute-start = (f32[18,2,4096]{2,0,1:T(8,128)S(1)}, f32[18,2,4096]{2,0,1:T(8,128)S(1)}, u32[]{:S(2)}, u32[]{:S(2)}) collective-permute-start(f32[18,2,4096]{2,0,1:T(8,128)S(1)} %pad_maximum_fusion.4), channel_id=1, source_target_pairs={{0,32},{32,64},{64,96},{96,128},{128,160},{160,192},{192,224},{224... | collective-permute-start | bytes 1769480 | tf_op jit(solution)/shard_map/ppermute | solution.py:85
  9.7 13.3 %collective-permute-start.1 = (f32[18,2,4096]{2,0,1:T(8,128)S(1)}, f32[18,2,4096]{2,0,1:T(8,128)S(1)}, u32[]{:S(2)}, u32[]{:S(2)}) collective-permute-start(f32[18,2,4096]{2,0,1:T(8,128)S(1)} %fusion.17), channel_id=1, source_target_pairs={{32,0},{64,32},{96,64},{128,96},{160,128},{192,160},{224,192},{256... | collective-permute-start | bytes 1769480 | tf_op jit(solution)/shard_map/ppermute | solution.py:86
  28.0 1.2 %copy-start.1 = (f32[17,4,4096]{2,0,1:T(8,128)}, f32[17,4,4096]{2,0,1:T(8,128)S(1)}, u32[]{:S(2)}) copy-start(f32[17,4,4096]{2,0,1:T(8,128)S(1)} %fusion.10) | copy-start | bytes 3342340
  32.0 40.3 %copy-start.2 = (s32[128]{0:T(128)S(1)}, s32[128]{0:T(128)}, u32[]{:S(2)}) copy-start(s32[128]{0:T(128)} %param.11) | copy-start | bytes 1540
  32.7 14.8 %all-to-all-start = ((f32[16,1,544]{2,1,0:T(1,128)}), f32[16,1,544]{2,1,0:T(1,128)S(1)}, u32[]{:S(2)}, u32[]{:S(2)}) async-start(f32[16,1,544]{2,1,0:T(1,128)} %reshape.33), calls=%async_computation | async-start | bytes 81920 | tf_op jit(solution)/shard_map/all_to_all | solution.py:61
  49.7 21.8 %all-to-all-start.1 = ((f32[32,1,544]{2,1,0:T(1,128)}), f32[32,1,544]{2,1,0:T(1,128)S(1)}, u32[]{:S(2)}, u32[]{:S(2)}) async-start(f32[32,1,544]{2,1,0:T(1,128)} %copy.35), calls=%async_computation.1 | async-start | bytes 163840 | tf_op jit(solution)/shard_map/all_to_all | solution.py:72

commit v11 on v10

--- a/solution.py
+++ b/solution.py
@@ -82,8 +82,13 @@
     planes = body.shape[1]
     lower = jnp.concatenate([body[:, :2], rate_field[None, :2]], axis=0)
     upper = jnp.concatenate([body[:, planes - 2 :], rate_field[None, planes - 2 :]], axis=0)
-    before = lax.ppermute(upper, "slab", up)
-    after = lax.ppermute(lower, "slab", down)
+    even = lax.axis_index("slab") % 2 == 0
+    across = [(i, i + 1) for i in range(1, size - 1, 2)] + [(i, i - 1) for i in range(2, size, 2)]
+    within = [(i, i + 1) for i in range(0, size, 2)] + [(i + 1, i) for i in range(0, size, 2)]
+    far = lax.ppermute(jnp.where(even, lower, upper), "slab", across)
+    near = lax.ppermute(jnp.where(even, upper, lower), "slab", within)
+    before = jnp.where(even, far, near)
+    after = jnp.where(even, near, far)
     fields = jnp.concatenate([before[:-1], body, after[:-1]], axis=1)
     rate_ext = jnp.concatenate([before[-1, 1:], rate_field, after[-1, :1]], axis=0)
     fields = update(fields, rate_ext)

time: 73.3 us -> 71.2 us (0.971)
  waiting for transfers between devices: 21.3 us -> 18.3 us
  starting transfers between devices: 30.4 us -> 31.3 us
    ppermute x2, waiting for transfers between devices: 7.75 us -> 4.73 us  [the longest x1 4.73 us: per_device(): far = lax.ppermute(jnp.where(even, lower, upper), 'slab', across)]
    all_to_all x1, starting transfers between devices: 7.43 us -> 8.88 us  [exchange_sum(): received = lax.all_to_all(copies, axis, 0, 0, tiled=False)]
  transfers between devices with their start and end apart: 4 -> 4, of which waited for: 4 -> 3; matrix products, arithmetic and copies ran while one was open for 4% -> 4% of each run, Pallas kernels for 0% -> 0%
where the time goes in v11:
time: 71.2 us; the launch traced here: 70.8 us
  starting transfers between devices  31.3 us (44%)
  waiting for transfers between devices  18.3 us (26%)
  other arithmetic  10.1 us (14%)
  local copies, waits for them, and re-layouts  7.47 us (10%)
  matrix products  2.81 us (4%)
  between operations  0.88 us (1%)
    all_to_all x1, starting transfers between devices, exchange_scatter(): received = jnp.sum(lax.all_to_all(message, axis, 0, 0, tiled=True), axis=0)  12.9 us
    all_to_all x1, starting transfers between devices, exchange_sum(): received = lax.all_to_all(copies, axis, 0, 0, tiled=False)  8.88 us
    all_to_all x1, waiting for transfers between devices, exchange_scatter(): received = jnp.sum(lax.all_to_all(message, axis, 0, 0, tiled=True), axis=0)  7.85 us
    all_to_all x1, waiting for transfers between devices, exchange_sum(): received = lax.all_to_all(copies, axis, 0, 0, tiled=False)  5.72 us
    ppermute x1, starting transfers between devices, per_device(): near = lax.ppermute(jnp.where(even, upper, lower), 'slab', within)  4.9 us
    ppermute x1, waiting for transfers between devices, per_device(): far = lax.ppermute(jnp.where(even, lower, upper), 'slab', across)  4.73 us
    ppermute x1, starting transfers between devices, per_device(): far = lax.ppermute(jnp.where(even, lower, upper), 'slab', across)  4.59 us
    add x2, other arithmetic, update(): return middle + rate_field * (zsum + lateral(middle) - 6.0 * middle)  4.48 us
  transfers between devices with their start and end apart: 4, of which 3 were waited for; matrix products, arithmetic and copies ran while one was open for 4% of the time, Pallas kernels for 0%

profile of v11, /device:TPU:1, one launch (start us, length us, event | category | flops | bytes accessed | tf_op | source)
XLA Modules:
  0.0 70.8 jit_solution(11227070321352050173)
XLA Ops:
  0.6 0.0 copy-start
  0.7 2.0 %copy.31 = f32[16,4,4096]{2,0,1:T(8,128)S(1)} copy(f32[16,4,4096]{2,1,0:T(4,128)} %param.7) | data formatting | bytes 2097152 | tf_op args[1]
  2.6 0.9 %copy.30 = f32[1,4,4096]{2,0,1:T(1,128)S(1)} copy(f32[1,4,4096]{2,1,0:T(4,128)} %bitcast.43) | data formatting | bytes 131072 | tf_op jit(solution)/shard_map/broadcast_in_dim | solution.py:78
  3.6 1.1 %select_reduce_fusion = f32[4,4096]{1,0:T(4,128)S(1)} fusion(f32[8]{0:T(128)} %param.9, s32[4,4096]{1,0:T(4,128)} %param.8), kind=kLoop, calls=%fused_computation.32 | loop fusion | flops 376832 | bytes 131104 | tf_op jit(solution)/shard_map/reduce_sum | solution.py:31
  4.8 0.1 fusion.16
  4.9 0.2 fusion.19
  5.1 4.6 %collective-permute-start = (f32[18,2,4096]{2,0,1:T(8,128)S(1)}, f32[18,2,4096]{2,0,1:T(8,128)S(1)}, u32[]{:S(2)}, u32[]{:S(2)}) collective-permute-start(f32[18,2,4096]{2,0,1:T(8,128)S(1)} %get-tuple-element.3), channel_id=1, source_target_pairs={{32,64},{96,128},{160,192},{224,256},{288,320},{352,384},{416,448}... | collective-permute-start | bytes 1769480 | tf_op jit(solution)/shard_map/ppermute | solution.py:88
  9.7 4.9 %collective-permute-start.1 = (f32[18,2,4096]{2,0,1:T(8,128)S(1)}, f32[18,2,4096]{2,0,1:T(8,128)S(1)}, u32[]{:S(2)}, u32[]{:S(2)}) collective-permute-start(f32[18,2,4096]{2,0,1:T(8,128)S(1)} %get-tuple-element.4), channel_id=1, source_target_pairs={{0,32},{64,96},{128,160},{192,224},{256,288},{320,352},{384,416},{... | collective-permute-start | bytes 1769480 | tf_op jit(solution)/shard_map/ppermute | solution.py:89
  14.7 4.7 %collective-permute-done = f32[18,2,4096]{2,0,1:T(8,128)S(1)} collective-permute-done((f32[18,2,4096]{2,0,1:T(8,128)S(1)}, f32[18,2,4096]{2,0,1:T(8,128)S(1)}, u32[]{:S(2)}, u32[]{:S(2)}) %collective-permute-start) | collective-permute-done | bytes 589856 | tf_op jit(solution)/shard_map/ppermute | solution.py:88
  19.4 0.0 collective-permute-done.1
  19.4 0.1 broadcast_select_fusion.1
  19.6 0.3 pad_maximum_fusion
  19.9 2.8 %fusion.3 = f32[17,6,4096]{2,0,1:T(8,128)S(1)} fusion(f32[17,6,4096]{2,0,1:T(8,128)S(1)} %pad_maximum_fusion, f32[17,2,4096]{2,0,1:T(8,128)S(1)} %bitcast.40, f32[16,4,4096]{2,0,1:T(8,128)S(1)} %copy.31, f32[1,4,4096]{2,0,1:T(1,128)S(1)} %copy.30, f32[17,2,4096]{2,0,1:T(8,128)S(1)} %bitcast.38, f32[6,4096]{1,0:T(8,128)S(1)} %pad_maximum_fusion.5, ...), kind=kLoop, calls=%fused_computation.7 | loop fusion | flops 6266880 | bytes 5677056 | tf_op jit(solution)/shard_map/add | solution.py:48
  22.7 0.1 slice.116
  22.8 1.7 %fusion.10 = f32[17,4,4096]{2,0,1:T(8,128)S(1)} fusion(f32[17,4,4096]{2,0,1:T(8,128)S(1)} %slice.116, f32[17,6,4096]{2,0,1:T(8,128)S(1)} %fusion.3, f32[4,4096]{1,0:T(4,128)S(1)} %broadcast_multiply_fusion, pred[4096]{0:T(1024)(128)(4,1)S(1)} %get-tuple-element.13, pred[4096]{0:T(1024)(128)(4,1)S(1)} %get-tuple-element.14), kind=kLoop, calls=%fused_computation.17 | loop fusion | flops 3063808 | bytes 4530176 | tf_op jit(solution)/shard_map/add | solution.py:48
  24.5 1.1 %copy-done.1 = f32[17,4,4096]{2,0,1:T(8,128)} copy-done((f32[17,4,4096]{2,0,1:T(8,128)}, f32[17,4,4096]{2,0,1:T(8,128)S(1)}, u32[]{:S(2)}) %copy-start.1) | copy-done | bytes 1114136
  25.7 2.8 %fusion.12 = f32[32,17]{0,1:T(8,128)S(1)} fusion(f32[17,4,4096]{2,0,1:T(8,128)S(1)} %fusion.10, f32[32,4,4096]{2,1,0:T(4,128)S(1)} %copy-done), kind=kOutput, calls=%fused_computation.23 | convolution fusion | flops 106954752 | bytes 3213440 | tf_op jit(solution)/shard_map/bzc,gzc->bg/dot_general | solution.py:99
  28.5 0.0 copy-start.2
  28.5 0.7 %reshape.33 = f32[16,1,544]{2,1,0:T(1,128)} reshape(f32[16,17,32]{2,1,0:T(8,128)S(1)} %broadcast_bitcast_fusion) | data formatting | bytes 69632
  29.3 8.9 %all-to-all-start = ((f32[16,1,544]{2,1,0:T(1,128)}), f32[16,1,544]{2,1,0:T(1,128)S(1)}, u32[]{:S(2)}, u32[]{:S(2)}) async-start(f32[16,1,544]{2,1,0:T(1,128)} %reshape.33), calls=%async_computation | async-start | bytes 81920 | tf_op jit(solution)/shard_map/all_to_all | solution.py:61
  38.1 1.7 %fusion.15 = f32[4,4096]{1,0:T(4,128)S(1)} fusion(f32[17,4,4096]{2,0,1:T(8,128)} %copy-done.1), kind=kLoop, calls=%fused_computation.25 | loop fusion | flops 507904 | bytes 1114112 | tf_op jit(solution)/shard_map/reduce_sum | solution.py:98
  39.8 5.7 %all-to-all-done = f32[16,1,544]{2,1,0:T(1,128)S(1)} async-done(((f32[16,1,544]{2,1,0:T(1,128)}), f32[16,1,544]{2,1,0:T(1,128)S(1)}, u32[]{:S(2)}, u32[]{:S(2)}) %all-to-all-start) | async-done | bytes 34848 | tf_op jit(solution)/shard_map/all_to_all | solution.py:61
  45.6 0.5 broadcast.26
  46.1 0.7 %reduce.1 = f32[16,544]{1,0:T(8,128)S(1)} reduce(f32[16,1,544]{2,1,0:T(1,128)S(1)} %all-to-all-done, f32[]{:T(128)} %broadcast.26), dimensions={1}, to_apply=%all_to_all.9.reduce_sub_computation | reduce | bytes 69636 | tf_op jit(solution)/shard_map/all_to_all | solution.py:61
  46.8 0.1 reshape.34
  47.0 0.7 %copy.35 = f32[32,1,544]{2,1,0:T(1,128)} copy(f32[32,1,544]{2,0,1:T(8,128)S(1)} %maximum_bitcast_fusion) | data formatting | bytes 139264 | tf_op jit(solution)/shard_map/all_to_all | solution.py:72
  47.7 12.9 %all-to-all-start.1 = ((f32[32,1,544]{2,1,0:T(1,128)}), f32[32,1,544]{2,1,0:T(1,128)S(1)}, u32[]{:S(2)}, u32[]{:S(2)}) async-start(f32[32,1,544]{2,1,0:T(1,128)} %copy.35), calls=%async_computation.1 | async-start | bytes 163840 | tf_op jit(solution)/shard_map/all_to_all | solution.py:72
  60.6 1.1 %slice.119 = f32[1,4,4096]{2,0,1:T(1,128)S(1)} slice(f32[17,4,4096]{2,0,1:T(8,128)} %copy-done.1), slice={[0:1], [0:4], [0:4096]} | slice | bytes 131072 | tf_op jit(solution)/shard_map/slice | solution.py:96
  61.7 7.8 %all-to-all-done.1 = f32[32,1,544]{2,1,0:T(1,128)S(1)} async-done(((f32[32,1,544]{2,1,0:T(1,128)}), f32[32,1,544]{2,1,0:T(1,128)S(1)}, u32[]{:S(2)}, u32[]{:S(2)}) %all-to-all-start.1) | async-done | bytes 69664 | tf_op jit(solution)/shard_map/all_to_all | solution.py:72
  69.5 0.1 reduce_sum.58
  69.6 0.6 bitcast_add_fusion
  70.2 0.6 select_reduce_fusion.1
  (18 shorter events, 0.3 us)
Async XLA Ops:
  0.6 25.0 %copy-start = (f32[32,4,4096]{2,1,0:T(4,128)S(1)}, f32[32,4,4096]{2,1,0:T(4,128)}, u32[]{:S(2)}) copy-start(f32[32,4,4096]{2,1,0:T(4,128)} %param.10) | copy-start | bytes 6291460
  5.1 14.3 %collective-permute-start = (f32[18,2,4096]{2,0,1:T(8,128)S(1)}, f32[18,2,4096]{2,0,1:T(8,128)S(1)}, u32[]{:S(2)}, u32[]{:S(2)}) collective-permute-start(f32[18,2,4096]{2,0,1:T(8,128)S(1)} %get-tuple-element.3), channel_id=1, source_target_pairs={{32,64},{96,128},{160,192},{224,256},{288,320},{352,384},{416,448}... | collective-permute-start | bytes 1769480 | tf_op jit(solution)/shard_map/ppermute | solution.py:88
  9.7 9.7 %collective-permute-start.1 = (f32[18,2,4096]{2,0,1:T(8,128)S(1)}, f32[18,2,4096]{2,0,1:T(8,128)S(1)}, u32[]{:S(2)}, u32[]{:S(2)}) collective-permute-start(f32[18,2,4096]{2,0,1:T(8,128)S(1)} %get-tuple-element.4), channel_id=1, source_target_pairs={{0,32},{64,96},{128,160},{192,224},{256,288},{320,352},{384,416},{... | collective-permute-start | bytes 1769480 | tf_op jit(solution)/shard_map/ppermute | solution.py:89
  24.5 1.2 %copy-start.1 = (f32[17,4,4096]{2,0,1:T(8,128)}, f32[17,4,4096]{2,0,1:T(8,128)S(1)}, u32[]{:S(2)}) copy-start(f32[17,4,4096]{2,0,1:T(8,128)S(1)} %fusion.10) | copy-start | bytes 3342340
  28.5 41.7 %copy-start.2 = (s32[128]{0:T(128)S(1)}, s32[128]{0:T(128)}, u32[]{:S(2)}) copy-start(s32[128]{0:T(128)} %param.11) | copy-start | bytes 1540
  29.3 16.3 %all-to-all-start = ((f32[16,1,544]{2,1,0:T(1,128)}), f32[16,1,544]{2,1,0:T(1,128)S(1)}, u32[]{:S(2)}, u32[]{:S(2)}) async-start(f32[16,1,544]{2,1,0:T(1,128)} %reshape.33), calls=%async_computation | async-start | bytes 81920 | tf_op jit(solution)/shard_map/all_to_all | solution.py:61
  47.7 21.8 %all-to-all-start.1 = ((f32[32,1,544]{2,1,0:T(1,128)}), f32[32,1,544]{2,1,0:T(1,128)S(1)}, u32[]{:S(2)}, u32[]{:S(2)}) async-start(f32[32,1,544]{2,1,0:T(1,128)} %copy.35), calls=%async_computation.1 | async-start | bytes 163840 | tf_op jit(solution)/shard_map/all_to_all | solution.py:72

commit v12 on v11

--- a/solution.py
+++ b/solution.py
@@ -85,20 +85,40 @@
     even = lax.axis_index("slab") % 2 == 0
     across = [(i, i + 1) for i in range(1, size - 1, 2)] + [(i, i - 1) for i in range(2, size, 2)]
     within = [(i, i + 1) for i in range(0, size, 2)] + [(i + 1, i) for i in range(0, size, 2)]
-    far = lax.ppermute(jnp.where(even, lower, upper), "slab", across)
+    outgoing = jnp.where(even, lower, upper)
+    split = (body.shape[0] + 1) // 2
+    first = jnp.concatenate([outgoing[:split], outgoing[-1:]], axis=0)
+    far_first = lax.ppermute(first, "slab", across)
     near = lax.ppermute(jnp.where(even, upper, lower), "slab", within)
-    before = jnp.where(even, far, near)
-    after = jnp.where(even, near, far)
-    fields = jnp.concatenate([before[:-1], body, after[:-1]], axis=1)
-    rate_ext = jnp.concatenate([before[-1, 1:], rate_field, after[-1, :1]], axis=0)
-    fields = update(fields, rate_ext)
-    fields = update(fields, rate_field)
-    centre_moved = fields[0]
-    gens_moved = fields[1:]
-    radius_local = jnp.sum(jnp.abs(gens_moved), axis=0)
-    all_proj = jnp.einsum(
-        "bzc,gzc->bg", direction_bank, fields, precision=lax.Precision.HIGHEST
+    second, near = lax.optimization_barrier((outgoing[split:-1], near))
+    far_second = lax.ppermute(second, "slab", across)
+    near_first = jnp.concatenate([near[:split], near[-1:]], axis=0)
+    rate_far = far_first[-1]
+    rate_before = jnp.where(even, rate_far, near[-1])
+    rate_after = jnp.where(even, near[-1], rate_far)
+    rate_ext = jnp.concatenate([rate_before[1:], rate_field, rate_after[:1]], axis=0)
+
+    def advance_part(part, far):
+        before = jnp.where(even, far, near[part])
+        after = jnp.where(even, near[part], far)
+        fields = jnp.concatenate([before, body[part], after], axis=1)
+        fields = update(fields, rate_ext)
+        fields = update(fields, rate_field)
+        proj = jnp.einsum(
+            "bzc,gzc->bg", direction_bank, fields, precision=lax.Precision.HIGHEST
+        )
+        return fields, proj
+
+    moved_first, proj_first = advance_part(slice(0, split), far_first[:-1])
+    far_second, proj_first, moved_first = lax.optimization_barrier(
+        (far_second, proj_first, moved_first)
     )
+    moved_second, proj_second = advance_part(slice(split, body.shape[0]), far_second)
+    centre_moved = moved_first[0]
+    radius_local = jnp.sum(jnp.abs(moved_first[1:]), axis=0) + jnp.sum(
+        jnp.abs(moved_second), axis=0
+    )
+    all_proj = jnp.concatenate([proj_first, proj_second], axis=1)
     summed = exchange_sum(all_proj, "slab")
     summed_centre, summed_proj = summed[:, 0], summed[:, 1:]
     partial_value = jnp.sum(jnp.abs(summed_proj), axis=1)

time: 71.2 us -> 76 us (1.067)
  waiting for transfers between devices: 18.3 us -> 24.4 us
  matrix products: 2.81 us -> 5.56 us
  local copies, waits for them, and re-layouts: 7.47 us -> 4.96 us
  starting transfers between devices: 31.3 us -> 29.6 us
    all_to_all x1, starting transfers between devices: 8.88 us -> 4 us  [exchange_sum(): received = lax.all_to_all(copies, axis, 0, 0, tiled=False)]
    ppermute x1, starting transfers between devices: 4.9 us -> 8.92 us  [per_device(): near = lax.ppermute(jnp.where(even, upper, lower), 'slab', within)]
    ppermute x1 -> x2, waiting for transfers between devices: 4.73 us -> 8.34 us  [the longest x1 8.33 us: per_device(): far_first = lax.ppermute(first, 'slab', across)]
    dot_general x1 -> x2, matrix products: 2.81 us -> 5.56 us  [advance_part(): jnp.einsum('bzc,gzc->bg', direction_bank, fields, precision=lax.Precision...]
    all_to_all x1, waiting for transfers between devices: 5.72 us -> 7.16 us  [exchange_sum(): received = lax.all_to_all(copies, axis, 0, 0, tiled=False)]
    unnamed x11 -> x13, local copies, waits for them, and re-layouts: 4 us -> 2.71 us
    all_to_all x1, waiting for transfers between devices: 7.85 us -> 8.89 us  [exchange_scatter(): received = jnp.sum(lax.all_to_all(message, axis, 0, 0, tiled=True), axis=0)]
    slice x1 -> x7, local copies, waits for them, and re-layouts: 1.08 us -> 0.23 us  [the longest x2 0.07 us: per_device(): first = jnp.concatenate([outgoing[:split], outgoing[-1:]], axis=0)]
  transfers between devices with their start and end apart: 4 -> 5, of which waited for: 3 -> 3; matrix products, arithmetic and copies ran while one was open for 4% -> 9% of each run, Pallas kernels for 0% -> 0%
where the time goes in v12:
time: 76 us; the launch traced here: 75.6 us
  starting transfers between devices  29.6 us (39%)
  waiting for transfers between devices  24.4 us (32%)
  other arithmetic  10 us (13%)
  matrix products  5.56 us (7%)
  local copies, waits for them, and re-layouts  4.96 us (7%)
  between operations  1.06 us (1%)
    all_to_all x1, starting transfers between devices, exchange_scatter(): received = jnp.sum(lax.all_to_all(message, axis, 0, 0, tiled=True), axis=0)  12.9 us
    ppermute x1, starting transfers between devices, per_device(): near = lax.ppermute(jnp.where(even, upper, lower), 'slab', within)  8.92 us
    all_to_all x1, waiting for transfers between devices, exchange_scatter(): received = jnp.sum(lax.all_to_all(message, axis, 0, 0, tiled=True), axis=0)  8.89 us
    ppermute x1, waiting for transfers between devices, per_device(): far_first = lax.ppermute(first, 'slab', across)  8.33 us
    all_to_all x1, waiting for transfers between devices, exchange_sum(): received = lax.all_to_all(copies, axis, 0, 0, tiled=False)  7.16 us
    dot_general x2, matrix products, advance_part(): jnp.einsum('bzc,gzc->bg', direction_bank, fields, precision=lax.Precision...  5.56 us
    all_to_all x1, starting transfers between devices, exchange_sum(): received = lax.all_to_all(copies, axis, 0, 0, tiled=False)  4 us
    add x3, other arithmetic, update(): return middle + rate_field * (zsum + lateral(middle) - 6.0 * middle)  3.99 us
  transfers between devices with their start and end apart: 5, of which 3 were waited for; matrix products, arithmetic and copies ran while one was open for 9% of the time, Pallas kernels for 0%

profile of v12, /device:TPU:1, one launch (start us, length us, event | category | flops | bytes accessed | tf_op | source)
XLA Modules:
  0.0 75.6 jit_solution(1397285222655967823)
XLA Ops:
  0.7 1.2 %select_reduce_fusion = f32[4,4096]{1,0:T(4,128)S(1)} fusion(f32[8]{0:T(128)} %param.9, s32[4,4096]{1,0:T(4,128)} %param.8), kind=kLoop, calls=%fused_computation.57 | loop fusion | flops 376832 | bytes 131104 | tf_op jit(solution)/shard_map/reduce_sum | solution.py:31
  2.0 1.8 %copy.53 = f32[16,4,4096]{2,0,1:T(8,128)S(1)} copy(f32[16,4,4096]{2,1,0:T(4,128)} %param.7) | data formatting | bytes 2097152 | tf_op args[1]
  4.0 0.2 fusion.26
  4.2 0.2 fusion.27
  4.4 8.9 %collective-permute-start = (f32[18,2,4096]{2,0,1:T(8,128)S(1)}, f32[18,2,4096]{2,0,1:T(8,128)S(1)}, u32[]{:S(2)}, u32[]{:S(2)}) collective-permute-start(f32[18,2,4096]{2,0,1:T(8,128)S(1)} %get-tuple-element.15), channel_id=1, source_target_pairs={{0,32},{64,96},{128,160},{192,224},{256,288},{320,352},{384,416},{... | collective-permute-start | bytes 1769480 | tf_op jit(solution)/shard_map/ppermute | solution.py:92
  13.5 1.9 %collective-permute-start.2 = (f32[10,2,4096]{2,0,1:T(8,128)S(1)}, f32[10,2,4096]{2,0,1:T(8,128)S(1)}, u32[]{:S(2)}, u32[]{:S(2)}) collective-permute-start(f32[10,2,4096]{2,0,1:T(8,128)S(1)} %pad_maximum_fusion.7), channel_id=1, source_target_pairs={{32,64},{96,128},{160,192},{224,256},{288,320},{352,384},{416,448}... | collective-permute-start | bytes 983048 | tf_op jit(solution)/shard_map/ppermute | solution.py:91
  15.5 0.1 pad_maximum_fusion.4
  15.6 8.3 %collective-permute-done.2 = f32[10,2,4096]{2,0,1:T(8,128)S(1)} collective-permute-done((f32[10,2,4096]{2,0,1:T(8,128)S(1)}, f32[10,2,4096]{2,0,1:T(8,128)S(1)}, u32[]{:S(2)}, u32[]{:S(2)}) %collective-permute-start.2) | collective-permute-done | bytes 327712 | tf_op jit(solution)/shard_map/ppermute | solution.py:91
  24.0 1.9 %collective-permute-start.1 = (f32[8,2,4096]{2,0,1:T(8,128)S(1)}, f32[8,2,4096]{2,0,1:T(8,128)S(1)}, u32[]{:S(2)}, u32[]{:S(2)}) collective-permute-start(f32[8,2,4096]{2,0,1:T(8,128)S(1)} %slice.209), channel_id=1, source_target_pairs={{32,64},{96,128},{160,192},{224,256},{288,320},{352,384},{416,448}... | collective-permute-start | bytes 786440 | tf_op jit(solution)/shard_map/ppermute | solution.py:94
  26.2 0.1 pad_maximum_fusion
  26.3 1.7 %fusion.7 = f32[9,6,4096]{2,0,1:T(8,128)S(1)} fusion(f32[9,6,4096]{2,0,1:T(8,128)S(1)} %pad_maximum_fusion, f32[9,2,4096]{2,0,1:T(8,128)S(1)} %get-tuple-element.18, f32[9,4,4096]{2,0,1:T(8,128)S(1)} %pad_maximum_fusion.4, f32[9,2,4096]{2,0,1:T(8,128)S(1)} %get-tuple-element.17, f32[6,4096]{1,0:T(8,128)S(1)} %pad_maximum_fusion.8, ...), kind=kLoop, calls=%fused_computation.14 | loop fusion | flops 2875392 | bytes 3055616 | tf_op jit(solution)/shard_map/add | solution.py:48
  28.0 1.2 %fusion.18 = f32[9,4,4096]{2,0,1:T(8,128)S(1)} fusion(f32[9,4,4096]{2,0,1:T(8,128)S(1)} %slice.218, f32[9,6,4096]{2,0,1:T(8,128)S(1)} %fusion.7, f32[4,4096]{1,0:T(4,128)S(1)} %broadcast_multiply_fusion, pred[4096]{0:T(1024)(128)(4,1)S(1)} %get-tuple-element.29, pred[4096]{0:T(1024)(128)(4,1)S(1)} %get-tuple-element.30), kind=kLoop, calls=%fused_computation.26 | loop fusion | flops 1622016 | bytes 2433024 | tf_op jit(solution)/shard_map/add | solution.py:48
  29.2 2.6 %fusion.9 = f32[32,9]{0,1:T(8,128)S(1)} fusion(f32[9,4,4096]{2,0,1:T(8,128)S(1)} %fusion.18, f32[32,4,4096]{2,1,0:T(4,128)S(1)} %copy-done), kind=kOutput, calls=%fused_computation.18 | convolution fusion | flops 56623104 | bytes 2688128 | tf_op jit(solution)/shard_map/bzc,gzc->bg/dot_general | solution.py:107
  31.9 0.2 copy.58
  32.1 0.2 copy.57
  32.3 0.4 pad_maximum_fusion.2
  32.7 1.2 %fusion.22 = f32[8,6,4096]{2,1,0:T(8,128)S(1)} fusion(f32[8,6,4096]{2,1,0:T(8,128)S(1)} %pad_maximum_fusion.2, f32[8,2,4096]{2,1,0:T(2,128)S(1)} %copy.58, f32[8,4,4096]{2,1,0:T(4,128)S(1)} %slice.186, f32[8,2,4096]{2,1,0:T(2,128)S(1)} %copy.57, f32[6,4096]{1,0:T(8,128)S(1)} %pad_maximum_fusion.8, pred[4096]{0:T(1024)(128)(4,1)S(1)} %get-tuple-element.29, ...), kind=kLoop, calls=%fused_computation.32 | loop fusion | flops 2555904 | bytes 2727936 | tf_op jit(solution)/shard_map/add | solution.py:48
  33.9 0.1 slice.221
  34.0 1.2 %abs_reduce_fusion = (f32[4,4096]{1,0:T(4,128)S(1)}, f32[8,4,4096]{2,1,0:T(4,128)S(1)}) fusion(f32[8,4,4096]{2,1,0:T(4,128)S(1)} %slice.221, pred[4096]{0:T(1024)(128)(4,1)S(1)} %get-tuple-element.29, pred[4096]{0:T(1024)(128)(4,1)S(1)} %get-tuple-element.30, f32[8,6,4096]{2,1,0:T(8,128)S(1)} %fusion.22, f32[4,4096]{1,0:T(4,128)S(1)} %broadcast_multiply_fusion), kind=kLoop, calls=%fused_computation.52 | loop fusion | flops 1687552 | bytes 2236416 | tf_op jit(solution)/shard_map/reduce_sum | solution.py:118
  35.3 2.9 %fusion.12 = f32[32,8]{0,1:T(8,128)S(1)} fusion(f32[32,4,4096]{2,1,0:T(4,128)S(1)} %copy-done, f32[8,4,4096]{2,1,0:T(4,128)S(1)} %get-tuple-element.14), kind=kOutput, calls=%fused_computation.19 | convolution fusion | flops 50331648 | bytes 2622464 | tf_op jit(solution)/shard_map/bzc,gzc->bg/dot_general | solution.py:107
  38.2 0.7 reshape.40
  39.0 4.0 %all-to-all-start = ((f32[16,1,544]{2,1,0:T(1,128)}), f32[16,1,544]{2,1,0:T(1,128)S(1)}, u32[]{:S(2)}, u32[]{:S(2)}) async-start(f32[16,1,544]{2,1,0:T(1,128)} %reshape.40), calls=%async_computation | async-start | bytes 81920 | tf_op jit(solution)/shard_map/all_to_all | solution.py:61
  43.0 0.2 abs_reduce_fusion.1
  43.2 7.2 %all-to-all-done = f32[16,1,544]{2,1,0:T(1,128)S(1)} async-done(((f32[16,1,544]{2,1,0:T(1,128)}), f32[16,1,544]{2,1,0:T(1,128)S(1)}, u32[]{:S(2)}, u32[]{:S(2)}) %all-to-all-start) | async-done | bytes 34848 | tf_op jit(solution)/shard_map/all_to_all | solution.py:61
  50.4 0.5 broadcast.35
  50.9 0.7 reduce.1
  51.6 0.1 reshape.41
  51.8 0.7 copy.63
  52.5 12.9 %all-to-all-start.1 = ((f32[32,1,544]{2,1,0:T(1,128)}), f32[32,1,544]{2,1,0:T(1,128)S(1)}, u32[]{:S(2)}, u32[]{:S(2)}) async-start(f32[32,1,544]{2,1,0:T(1,128)} %copy.63), calls=%async_computation.1 | async-start | bytes 163840 | tf_op jit(solution)/shard_map/all_to_all | solution.py:72
  65.5 8.9 %all-to-all-done.1 = f32[32,1,544]{2,1,0:T(1,128)S(1)} async-done(((f32[32,1,544]{2,1,0:T(1,128)}), f32[32,1,544]{2,1,0:T(1,128)S(1)}, u32[]{:S(2)}, u32[]{:S(2)}) %all-to-all-start.1) | async-done | bytes 69664 | tf_op jit(solution)/shard_map/all_to_all | solution.py:72
  74.5 0.6 bitcast_add_fusion
  75.0 0.6 select_reduce_fusion.1
  (40 shorter events, 1.0 us)
Async XLA Ops:
  0.6 28.6 %copy-start = (f32[32,4,4096]{2,1,0:T(4,128)S(1)}, f32[32,4,4096]{2,1,0:T(4,128)}, u32[]{:S(2)}) copy-start(f32[32,4,4096]{2,1,0:T(4,128)} %param.10) | copy-start | bytes 6291460
  0.6 3.2 %copy-start.2 = (f32[4,4096]{1,0:T(4,128)S(1)}, f32[4,4096]{1,0:T(4,128)}, u32[]{:S(2)}) copy-start(f32[4,4096]{1,0:T(4,128)} %param.6) | copy-start | bytes 196612
  4.4 11.1 %copy-start.1 = (f32[16,4,4096]{2,1,0:T(4,128)S(1)}, f32[16,4,4096]{2,1,0:T(4,128)}, u32[]{:S(2)}) copy-start(f32[16,4,4096]{2,1,0:T(4,128)} %param.7) | copy-start | bytes 3145732
  4.4 19.6 %collective-permute-start = (f32[18,2,4096]{2,0,1:T(8,128)S(1)}, f32[18,2,4096]{2,0,1:T(8,128)S(1)}, u32[]{:S(2)}, u32[]{:S(2)}) collective-permute-start(f32[18,2,4096]{2,0,1:T(8,128)S(1)} %get-tuple-element.15), channel_id=1, source_target_pairs={{0,32},{64,96},{128,160},{192,224},{256,288},{320,352},{384,416},{... | collective-permute-start | bytes 1769480 | tf_op jit(solution)/shard_map/ppermute | solution.py:92
  13.5 10.5 %collective-permute-start.2 = (f32[10,2,4096]{2,0,1:T(8,128)S(1)}, f32[10,2,4096]{2,0,1:T(8,128)S(1)}, u32[]{:S(2)}, u32[]{:S(2)}) collective-permute-start(f32[10,2,4096]{2,0,1:T(8,128)S(1)} %pad_maximum_fusion.7), channel_id=1, source_target_pairs={{32,64},{96,128},{160,192},{224,256},{288,320},{352,384},{416,448}... | collective-permute-start | bytes 983048 | tf_op jit(solution)/shard_map/ppermute | solution.py:91
  24.0 7.8 %collective-permute-start.1 = (f32[8,2,4096]{2,0,1:T(8,128)S(1)}, f32[8,2,4096]{2,0,1:T(8,128)S(1)}, u32[]{:S(2)}, u32[]{:S(2)}) collective-permute-start(f32[8,2,4096]{2,0,1:T(8,128)S(1)} %slice.209), channel_id=1, source_target_pairs={{32,64},{96,128},{160,192},{224,256},{288,320},{352,384},{416,448}... | collective-permute-start | bytes 786440 | tf_op jit(solution)/shard_map/ppermute | solution.py:94
  38.2 36.9 %copy-start.3 = (s32[128]{0:T(128)S(1)}, s32[128]{0:T(128)}, u32[]{:S(2)}) copy-start(s32[128]{0:T(128)} %param.11) | copy-start | bytes 1540
  39.0 11.4 %all-to-all-start = ((f32[16,1,544]{2,1,0:T(1,128)}), f32[16,1,544]{2,1,0:T(1,128)S(1)}, u32[]{:S(2)}, u32[]{:S(2)}) async-start(f32[16,1,544]{2,1,0:T(1,128)} %reshape.40), calls=%async_computation | async-start | bytes 81920 | tf_op jit(solution)/shard_map/all_to_all | solution.py:61
  52.5 21.9 %all-to-all-start.1 = ((f32[32,1,544]{2,1,0:T(1,128)}), f32[32,1,544]{2,1,0:T(1,128)S(1)}, u32[]{:S(2)}, u32[]{:S(2)}) async-start(f32[32,1,544]{2,1,0:T(1,128)} %copy.63), calls=%async_computation.1 | async-start | bytes 163840 | tf_op jit(solution)/shard_map/all_to_all | solution.py:72

commit v13 on v12

--- a/solution.py
+++ b/solution.py
@@ -89,9 +89,11 @@
     split = (body.shape[0] + 1) // 2
     first = jnp.concatenate([outgoing[:split], outgoing[-1:]], axis=0)
     far_first = lax.ppermute(first, "slab", across)
-    near = lax.ppermute(jnp.where(even, upper, lower), "slab", within)
-    second, near = lax.optimization_barrier((outgoing[split:-1], near))
+    second, inner, far_first = lax.optimization_barrier(
+        (outgoing[split:-1], jnp.where(even, upper, lower), far_first)
+    )
     far_second = lax.ppermute(second, "slab", across)
+    near = lax.ppermute(inner, "slab", within)
     near_first = jnp.concatenate([near[:split], near[-1:]], axis=0)
     rate_far = far_first[-1]
     rate_before = jnp.where(even, rate_far, near[-1])

time: 76 us -> 76.1 us (level)
  starting transfers between devices: 29.6 us -> 31.3 us
  waiting for transfers between devices: 24.4 us -> 22.9 us
    ppermute x1, starting transfers between devices: 8.92 us -> 1.91 us  [per_device(): near = lax.ppermute(inner, 'slab', within)]
    all_to_all x1, starting transfers between devices: 4 us -> 8.04 us  [exchange_sum(): received = lax.all_to_all(copies, axis, 0, 0, tiled=False)]
    ppermute x1, starting transfers between devices: 1.92 us -> 4.73 us  [per_device(): far_first = lax.ppermute(first, 'slab', across)]
    ppermute x1, starting transfers between devices: 1.92 us -> 3.75 us  [per_device(): far_second = lax.ppermute(second, 'slab', across)]
    ppermute x1, waiting for transfers between devices: 8.33 us -> 6.81 us  [per_device(): far_first = lax.ppermute(first, 'slab', across)]
  transfers between devices with their start and end apart: 5 -> 5, of which waited for: 3 -> 3; matrix products, arithmetic and copies ran while one was open for 9% -> 8% of each run, Pallas kernels for 0% -> 0%
where the time goes in v13:
time: 76.1 us; the launch traced here: 75.8 us
  starting transfers between devices  31.3 us (41%)
  waiting for transfers between devices  22.9 us (30%)
  other arithmetic  10 us (13%)
  matrix products  5.56 us (7%)
  local copies, waits for them, and re-layouts  4.96 us (7%)
  between operations  1.07 us (1%)
    all_to_all x1, starting transfers between devices, exchange_scatter(): received = jnp.sum(lax.all_to_all(message, axis, 0, 0, tiled=True), axis=0)  12.9 us
    all_to_all x1, waiting for transfers between devices, exchange_scatter(): received = jnp.sum(lax.all_to_all(message, axis, 0, 0, tiled=True), axis=0)  8.89 us
    all_to_all x1, starting transfers between devices, exchange_sum(): received = lax.all_to_all(copies, axis, 0, 0, tiled=False)  8.04 us
    all_to_all x1, waiting for transfers between devices, exchange_sum(): received = lax.all_to_all(copies, axis, 0, 0, tiled=False)  7.16 us
    ppermute x1, waiting for transfers between devices, per_device(): far_first = lax.ppermute(first, 'slab', across)  6.81 us
    dot_general x2, matrix products, advance_part(): jnp.einsum('bzc,gzc->bg', direction_bank, fields, precision=lax.Precision...  5.56 us
    ppermute x1, starting transfers between devices, per_device(): far_first = lax.ppermute(first, 'slab', across)  4.73 us
    add x3, other arithmetic, update(): return middle + rate_field * (zsum + lateral(middle) - 6.0 * middle)  3.99 us
  transfers between devices with their start and end apart: 5, of which 3 were waited for; matrix products, arithmetic and copies ran while one was open for 8% of the time, Pallas kernels for 0%

profile of v13, /device:TPU:1, one launch (start us, length us, event | category | flops | bytes accessed | tf_op | source)
XLA Modules:
  0.0 75.8 jit_solution(10406065438399870525)
XLA Ops:
  0.7 1.2 %select_reduce_fusion = f32[4,4096]{1,0:T(4,128)S(1)} fusion(f32[8]{0:T(128)} %param.9, s32[4,4096]{1,0:T(4,128)} %param.8), kind=kLoop, calls=%fused_computation.57 | loop fusion | flops 376832 | bytes 131104 | tf_op jit(solution)/shard_map/reduce_sum | solution.py:31
  2.0 1.8 %copy.53 = f32[16,4,4096]{2,0,1:T(8,128)S(1)} copy(f32[16,4,4096]{2,1,0:T(4,128)} %param.7) | data formatting | bytes 2097152 | tf_op args[1]
  4.0 0.2 fusion.26
  4.2 0.2 fusion.27
  4.5 4.7 %collective-permute-start = (f32[10,2,4096]{2,0,1:T(8,128)S(1)}, f32[10,2,4096]{2,0,1:T(8,128)S(1)}, u32[]{:S(2)}, u32[]{:S(2)}) collective-permute-start(f32[10,2,4096]{2,0,1:T(8,128)S(1)} %pad_maximum_fusion.7), channel_id=1, source_target_pairs={{32,64},{96,128},{160,192},{224,256},{288,320},{352,384},{416,448}... | collective-permute-start | bytes 983048 | tf_op jit(solution)/shard_map/ppermute | solution.py:91
  9.3 6.8 %collective-permute-done = f32[10,2,4096]{2,0,1:T(8,128)S(1)} collective-permute-done((f32[10,2,4096]{2,0,1:T(8,128)S(1)}, f32[10,2,4096]{2,0,1:T(8,128)S(1)}, u32[]{:S(2)}, u32[]{:S(2)}) %collective-permute-start) | collective-permute-done | bytes 327712 | tf_op jit(solution)/shard_map/ppermute | solution.py:91
  16.1 1.9 %collective-permute-start.2 = (f32[18,2,4096]{2,0,1:T(8,128)S(1)}, f32[18,2,4096]{2,0,1:T(8,128)S(1)}, u32[]{:S(2)}, u32[]{:S(2)}) collective-permute-start(f32[18,2,4096]{2,0,1:T(8,128)S(1)} %get-tuple-element.11), channel_id=1, source_target_pairs={{0,32},{64,96},{128,160},{192,224},{256,288},{320,352},{384,416},{... | collective-permute-start | bytes 1769480 | tf_op jit(solution)/shard_map/ppermute | solution.py:96
  18.1 0.1 pad_maximum_fusion.4
  18.2 3.7 %collective-permute-start.1 = (f32[8,2,4096]{2,0,1:T(8,128)S(1)}, f32[8,2,4096]{2,0,1:T(8,128)S(1)}, u32[]{:S(2)}, u32[]{:S(2)}) collective-permute-start(f32[8,2,4096]{2,0,1:T(8,128)S(1)} %slice.209), channel_id=1, source_target_pairs={{32,64},{96,128},{160,192},{224,256},{288,320},{352,384},{416,448}... | collective-permute-start | bytes 786440 | tf_op jit(solution)/shard_map/ppermute | solution.py:95
  22.3 0.1 pad_maximum_fusion
  22.4 1.7 %fusion.7 = f32[9,6,4096]{2,0,1:T(8,128)S(1)} fusion(f32[9,6,4096]{2,0,1:T(8,128)S(1)} %pad_maximum_fusion, f32[9,2,4096]{2,0,1:T(8,128)S(1)} %get-tuple-element.20, f32[9,4,4096]{2,0,1:T(8,128)S(1)} %pad_maximum_fusion.4, f32[9,2,4096]{2,0,1:T(8,128)S(1)} %get-tuple-element.19, f32[6,4096]{1,0:T(8,128)S(1)} %pad_maximum_fusion.8, ...), kind=kLoop, calls=%fused_computation.14 | loop fusion | flops 2875392 | bytes 3055616 | tf_op jit(solution)/shard_map/add | solution.py:48
  24.1 1.2 %fusion.18 = f32[9,4,4096]{2,0,1:T(8,128)S(1)} fusion(f32[9,4,4096]{2,0,1:T(8,128)S(1)} %slice.218, f32[9,6,4096]{2,0,1:T(8,128)S(1)} %fusion.7, f32[4,4096]{1,0:T(4,128)S(1)} %broadcast_multiply_fusion, pred[4096]{0:T(1024)(128)(4,1)S(1)} %get-tuple-element.31, pred[4096]{0:T(1024)(128)(4,1)S(1)} %get-tuple-element.32), kind=kLoop, calls=%fused_computation.26 | loop fusion | flops 1622016 | bytes 2433024 | tf_op jit(solution)/shard_map/add | solution.py:48
  25.3 2.6 %fusion.9 = f32[32,9]{0,1:T(8,128)S(1)} fusion(f32[9,4,4096]{2,0,1:T(8,128)S(1)} %fusion.18, f32[32,4,4096]{2,1,0:T(4,128)S(1)} %copy-done), kind=kOutput, calls=%fused_computation.18 | convolution fusion | flops 56623104 | bytes 2688128 | tf_op jit(solution)/shard_map/bzc,gzc->bg/dot_general | solution.py:109
  28.0 0.2 copy.58
  28.2 0.2 copy.57
  28.4 0.4 pad_maximum_fusion.2
  28.8 1.2 %fusion.22 = f32[8,6,4096]{2,1,0:T(8,128)S(1)} fusion(f32[8,6,4096]{2,1,0:T(8,128)S(1)} %pad_maximum_fusion.2, f32[8,2,4096]{2,1,0:T(2,128)S(1)} %copy.58, f32[8,4,4096]{2,1,0:T(4,128)S(1)} %slice.186, f32[8,2,4096]{2,1,0:T(2,128)S(1)} %copy.57, f32[6,4096]{1,0:T(8,128)S(1)} %pad_maximum_fusion.8, pred[4096]{0:T(1024)(128)(4,1)S(1)} %get-tuple-element.31, ...), kind=kLoop, calls=%fused_computation.32 | loop fusion | flops 2555904 | bytes 2727936 | tf_op jit(solution)/shard_map/add | solution.py:48
  30.0 0.1 slice.222
  30.1 1.2 %abs_reduce_fusion = (f32[4,4096]{1,0:T(4,128)S(1)}, f32[8,4,4096]{2,1,0:T(4,128)S(1)}) fusion(f32[8,4,4096]{2,1,0:T(4,128)S(1)} %slice.222, pred[4096]{0:T(1024)(128)(4,1)S(1)} %get-tuple-element.31, pred[4096]{0:T(1024)(128)(4,1)S(1)} %get-tuple-element.32, f32[8,6,4096]{2,1,0:T(8,128)S(1)} %fusion.22, f32[4,4096]{1,0:T(4,128)S(1)} %broadcast_multiply_fusion), kind=kLoop, calls=%fused_computation.52 | loop fusion | flops 1687552 | bytes 2236416 | tf_op jit(solution)/shard_map/reduce_sum | solution.py:120
  31.4 2.9 %fusion.12 = f32[32,8]{0,1:T(8,128)S(1)} fusion(f32[32,4,4096]{2,1,0:T(4,128)S(1)} %copy-done, f32[8,4,4096]{2,1,0:T(4,128)S(1)} %get-tuple-element.16), kind=kOutput, calls=%fused_computation.19 | convolution fusion | flops 50331648 | bytes 2622464 | tf_op jit(solution)/shard_map/bzc,gzc->bg/dot_general | solution.py:109
  34.3 0.7 reshape.40
  35.1 8.0 %all-to-all-start = ((f32[16,1,544]{2,1,0:T(1,128)}), f32[16,1,544]{2,1,0:T(1,128)S(1)}, u32[]{:S(2)}, u32[]{:S(2)}) async-start(f32[16,1,544]{2,1,0:T(1,128)} %reshape.40), calls=%async_computation | async-start | bytes 81920 | tf_op jit(solution)/shard_map/all_to_all | solution.py:61
  43.1 0.2 abs_reduce_fusion.1
  43.4 7.2 %all-to-all-done = f32[16,1,544]{2,1,0:T(1,128)S(1)} async-done(((f32[16,1,544]{2,1,0:T(1,128)}), f32[16,1,544]{2,1,0:T(1,128)S(1)}, u32[]{:S(2)}, u32[]{:S(2)}) %all-to-all-start) | async-done | bytes 34848 | tf_op jit(solution)/shard_map/all_to_all | solution.py:61
  50.5 0.5 broadcast.35
  51.0 0.7 reduce.1
  51.8 0.1 reshape.41
  52.0 0.7 copy.63
  52.7 12.9 %all-to-all-start.1 = ((f32[32,1,544]{2,1,0:T(1,128)}), f32[32,1,544]{2,1,0:T(1,128)S(1)}, u32[]{:S(2)}, u32[]{:S(2)}) async-start(f32[32,1,544]{2,1,0:T(1,128)} %copy.63), calls=%async_computation.1 | async-start | bytes 163840 | tf_op jit(solution)/shard_map/all_to_all | solution.py:72
  65.6 8.9 %all-to-all-done.1 = f32[32,1,544]{2,1,0:T(1,128)S(1)} async-done(((f32[32,1,544]{2,1,0:T(1,128)}), f32[32,1,544]{2,1,0:T(1,128)S(1)}, u32[]{:S(2)}, u32[]{:S(2)}) %all-to-all-start.1) | async-done | bytes 69664 | tf_op jit(solution)/shard_map/all_to_all | solution.py:72
  74.6 0.6 bitcast_add_fusion
  75.2 0.6 select_reduce_fusion.1
  (40 shorter events, 1.0 us)
Async XLA Ops:
  0.6 24.7 %copy-start = (f32[32,4,4096]{2,1,0:T(4,128)S(1)}, f32[32,4,4096]{2,1,0:T(4,128)}, u32[]{:S(2)}) copy-start(f32[32,4,4096]{2,1,0:T(4,128)} %param.10) | copy-start | bytes 6291460
  0.6 3.2 %copy-start.2 = (f32[4,4096]{1,0:T(4,128)S(1)}, f32[4,4096]{1,0:T(4,128)}, u32[]{:S(2)}) copy-start(f32[4,4096]{1,0:T(4,128)} %param.6) | copy-start | bytes 196612
  4.4 13.7 %copy-start.1 = (f32[16,4,4096]{2,1,0:T(4,128)S(1)}, f32[16,4,4096]{2,1,0:T(4,128)}, u32[]{:S(2)}) copy-start(f32[16,4,4096]{2,1,0:T(4,128)} %param.7) | copy-start | bytes 3145732
  4.5 11.6 %collective-permute-start = (f32[10,2,4096]{2,0,1:T(8,128)S(1)}, f32[10,2,4096]{2,0,1:T(8,128)S(1)}, u32[]{:S(2)}, u32[]{:S(2)}) collective-permute-start(f32[10,2,4096]{2,0,1:T(8,128)S(1)} %pad_maximum_fusion.7), channel_id=1, source_target_pairs={{32,64},{96,128},{160,192},{224,256},{288,320},{352,384},{416,448}... | collective-permute-start | bytes 983048 | tf_op jit(solution)/shard_map/ppermute | solution.py:91
  16.1 5.9 %collective-permute-start.2 = (f32[18,2,4096]{2,0,1:T(8,128)S(1)}, f32[18,2,4096]{2,0,1:T(8,128)S(1)}, u32[]{:S(2)}, u32[]{:S(2)}) collective-permute-start(f32[18,2,4096]{2,0,1:T(8,128)S(1)} %get-tuple-element.11), channel_id=1, source_target_pairs={{0,32},{64,96},{128,160},{192,224},{256,288},{320,352},{384,416},{... | collective-permute-start | bytes 1769480 | tf_op jit(solution)/shard_map/ppermute | solution.py:96
  18.2 9.7 %collective-permute-start.1 = (f32[8,2,4096]{2,0,1:T(8,128)S(1)}, f32[8,2,4096]{2,0,1:T(8,128)S(1)}, u32[]{:S(2)}, u32[]{:S(2)}) collective-permute-start(f32[8,2,4096]{2,0,1:T(8,128)S(1)} %slice.209), channel_id=1, source_target_pairs={{32,64},{96,128},{160,192},{224,256},{288,320},{352,384},{416,448}... | collective-permute-start | bytes 786440 | tf_op jit(solution)/shard_map/ppermute | solution.py:95
  34.3 40.9 %copy-start.3 = (s32[128]{0:T(128)S(1)}, s32[128]{0:T(128)}, u32[]{:S(2)}) copy-start(s32[128]{0:T(128)} %param.11) | copy-start | bytes 1540
  35.1 15.5 %all-to-all-start = ((f32[16,1,544]{2,1,0:T(1,128)}), f32[16,1,544]{2,1,0:T(1,128)S(1)}, u32[]{:S(2)}, u32[]{:S(2)}) async-start(f32[16,1,544]{2,1,0:T(1,128)} %reshape.40), calls=%async_computation | async-start | bytes 81920 | tf_op jit(solution)/shard_map/all_to_all | solution.py:61
  52.7 21.8 %all-to-all-start.1 = ((f32[32,1,544]{2,1,0:T(1,128)}), f32[32,1,544]{2,1,0:T(1,128)S(1)}, u32[]{:S(2)}, u32[]{:S(2)}) async-start(f32[32,1,544]{2,1,0:T(1,128)} %copy.63), calls=%async_computation.1 | async-start | bytes 163840 | tf_op jit(solution)/shard_map/all_to_all | solution.py:72

commit v14 on v11

--- a/solution.py
+++ b/solution.py
@@ -24,11 +24,10 @@
 
 
 def lookup_rate(conductivity, cond_table):
-    classes = jnp.arange(cond_table.shape[0], dtype=jnp.int32)
-    picked = jnp.where(
-        conductivity[None] == classes[:, None, None], cond_table[:, None, None], jnp.float32(0.0)
-    )
-    return TIME_STEP * jnp.sum(picked, axis=0)
+    picked = jnp.full(conductivity.shape, cond_table[0], jnp.float32)
+    for k in range(1, cond_table.shape[0]):
+        picked = jnp.where(conductivity == k, cond_table[k], picked)
+    return TIME_STEP * picked
 
 
 def lateral(middle):

time: 71.2 us -> 76.8 us (1.079)
  other arithmetic: 10.1 us -> 14.9 us
    mul x1, other arithmetic: 0.02 us -> 5.97 us  [lookup_rate(): return TIME_STEP * picked]
    slice x0 -> x1, local copies, waits for them, and re-layouts: none -> 1.63 us  [lookup_rate(): picked = jnp.where(conductivity == k, cond_table[k], picked)]
    reduce_sum x1 -> x0, other arithmetic: 1.11 us -> none  [lookup_rate(): return TIME_STEP * jnp.sum(picked, axis=0)]
    broadcast_in_dim x1, local copies, waits for them, and re-layouts: 0.91 us -> 0.07 us  [per_device(): body = jnp.concatenate([center[None], generators], axis=0)]
    unnamed x11 -> x13, local copies, waits for them, and re-layouts: 4 us -> 3.86 us
where the time goes in v14:
time: 76.8 us; the launch traced here: 76.3 us
  starting transfers between devices  31.3 us (41%)
  waiting for transfers between devices  18.3 us (24%)
  other arithmetic  14.9 us (19%)
  local copies, waits for them, and re-layouts  8.11 us (11%)
  matrix products  2.81 us (4%)
  between operations  0.89 us (1%)
    all_to_all x1, starting transfers between devices, exchange_scatter(): received = jnp.sum(lax.all_to_all(message, axis, 0, 0, tiled=True), axis=0)  12.9 us
    all_to_all x1, starting transfers between devices, exchange_sum(): received = lax.all_to_all(copies, axis, 0, 0, tiled=False)  8.88 us
    all_to_all x1, waiting for transfers between devices, exchange_scatter(): received = jnp.sum(lax.all_to_all(message, axis, 0, 0, tiled=True), axis=0)  7.85 us
    mul x1, other arithmetic, lookup_rate(): return TIME_STEP * picked  5.97 us
    all_to_all x1, waiting for transfers between devices, exchange_sum(): received = lax.all_to_all(copies, axis, 0, 0, tiled=False)  5.72 us
    ppermute x1, starting transfers between devices, per_device(): near = lax.ppermute(jnp.where(even, upper, lower), 'slab', within)  4.9 us
    ppermute x1, waiting for transfers between devices, per_device(): far = lax.ppermute(jnp.where(even, lower, upper), 'slab', across)  4.73 us
    ppermute x1, starting transfers between devices, per_device(): far = lax.ppermute(jnp.where(even, lower, upper), 'slab', across)  4.59 us
  transfers between devices with their start and end apart: 4, of which 3 were waited for; matrix products, arithmetic and copies ran while one was open for 4% of the time, Pallas kernels for 0%

profile of v14, /device:TPU:1, one launch (start us, length us, event | category | flops | bytes accessed | tf_op | source)
XLA Modules:
  0.0 76.3 jit_solution(5619199998254166310)
XLA Ops:
  0.6 0.0 copy-start
  0.7 1.6 %fusion.27 = (f32[1]{0:T(128)}, f32[1]{0:T(128)}, f32[1]{0:T(128)}, f32[1]{0:T(128)}, f32[1]{0:T(128)}, /*index=5*/f32[1]{0:T(128)}, f32[1]{0:T(128)}, f32[1]{0:T(128)}) fusion(f32[8]{0:T(128)} %param.9), kind=kLoop, calls=%fused_computation.58 | loop fusion | bytes 64 | tf_op jit(solution)/shard_map/slice | solution.py:29
  2.3 6.0 %select_multiply_fusion = f32[4,4096]{1,0:T(4,128)S(1)} fusion(s32[4,4096]{1,0:T(4,128)} %param.8, f32[]{:T(128)} %bitcast.8, f32[]{:T(128)} %bitcast.7, f32[]{:T(128)} %bitcast.6, f32[]{:T(128)} %bitcast.5, f32[]{:T(128)} %bitcast.4, f32[]{:T(128)} %bitcast.3, f32[]{:T(128)} %bitcast.2, f32[]{:T(128)} %bitcast.1), kind=kLoop, calls=%fused_computation.37 | loop fusion | flops 245760 | bytes 131104 | tf_op jit(solution)/shard_map/mul | solution.py:30
  8.4 1.8 %copy.31 = f32[16,4,4096]{2,0,1:T(8,128)S(1)} copy(f32[16,4,4096]{2,1,0:T(4,128)} %param.7) | data formatting | bytes 2097152 | tf_op args[1]
  10.2 0.1 copy.30
  10.3 0.1 fusion.16
  10.4 0.2 fusion.19
  10.6 4.6 %collective-permute-start = (f32[18,2,4096]{2,0,1:T(8,128)S(1)}, f32[18,2,4096]{2,0,1:T(8,128)S(1)}, u32[]{:S(2)}, u32[]{:S(2)}) collective-permute-start(f32[18,2,4096]{2,0,1:T(8,128)S(1)} %get-tuple-element.3), channel_id=1, source_target_pairs={{32,64},{96,128},{160,192},{224,256},{288,320},{352,384},{416,448}... | collective-permute-start | bytes 1769480 | tf_op jit(solution)/shard_map/ppermute | solution.py:87
  15.2 4.9 %collective-permute-start.1 = (f32[18,2,4096]{2,0,1:T(8,128)S(1)}, f32[18,2,4096]{2,0,1:T(8,128)S(1)}, u32[]{:S(2)}, u32[]{:S(2)}) collective-permute-start(f32[18,2,4096]{2,0,1:T(8,128)S(1)} %get-tuple-element.4), channel_id=1, source_target_pairs={{0,32},{64,96},{128,160},{192,224},{256,288},{320,352},{384,416},{... | collective-permute-start | bytes 1769480 | tf_op jit(solution)/shard_map/ppermute | solution.py:88
  20.2 4.7 %collective-permute-done = f32[18,2,4096]{2,0,1:T(8,128)S(1)} collective-permute-done((f32[18,2,4096]{2,0,1:T(8,128)S(1)}, f32[18,2,4096]{2,0,1:T(8,128)S(1)}, u32[]{:S(2)}, u32[]{:S(2)}) %collective-permute-start) | collective-permute-done | bytes 589856 | tf_op jit(solution)/shard_map/ppermute | solution.py:87
  24.9 0.1 broadcast_select_fusion.1
  25.1 0.3 pad_maximum_fusion
  25.4 2.8 %fusion.3 = f32[17,6,4096]{2,0,1:T(8,128)S(1)} fusion(f32[17,6,4096]{2,0,1:T(8,128)S(1)} %pad_maximum_fusion, f32[17,2,4096]{2,0,1:T(8,128)S(1)} %bitcast.48, f32[16,4,4096]{2,0,1:T(8,128)S(1)} %copy.31, f32[1,4,4096]{2,0,1:T(1,128)S(1)} %copy.30, f32[17,2,4096]{2,0,1:T(8,128)S(1)} %bitcast.46, f32[6,4096]{1,0:T(8,128)S(1)} %pad_maximum_fusion.5, ...), kind=kLoop, calls=%fused_computation.7 | loop fusion | flops 6266880 | bytes 5677056 | tf_op jit(solution)/shard_map/add | solution.py:47
  28.2 0.1 slice.148
  28.3 1.7 %fusion.10 = f32[17,4,4096]{2,0,1:T(8,128)S(1)} fusion(f32[17,4,4096]{2,0,1:T(8,128)S(1)} %slice.148, f32[17,6,4096]{2,0,1:T(8,128)S(1)} %fusion.3, f32[4,4096]{1,0:T(4,128)S(1)} %select_multiply_fusion, pred[4096]{0:T(1024)(128)(4,1)S(1)} %get-tuple-element.21, pred[4096]{0:T(1024)(128)(4,1)S(1)} %get-tuple-element.22), kind=kLoop, calls=%fused_computation.17 | loop fusion | flops 3063808 | bytes 4530176 | tf_op jit(solution)/shard_map/add | solution.py:47
  30.0 1.1 %copy-done.1 = f32[17,4,4096]{2,0,1:T(8,128)} copy-done((f32[17,4,4096]{2,0,1:T(8,128)}, f32[17,4,4096]{2,0,1:T(8,128)S(1)}, u32[]{:S(2)}) %copy-start.1) | copy-done | bytes 1114136
  31.2 2.8 %fusion.12 = f32[32,17]{0,1:T(8,128)S(1)} fusion(f32[17,4,4096]{2,0,1:T(8,128)S(1)} %fusion.10, f32[32,4,4096]{2,1,0:T(4,128)S(1)} %copy-done), kind=kOutput, calls=%fused_computation.23 | convolution fusion | flops 106954752 | bytes 3213440 | tf_op jit(solution)/shard_map/bzc,gzc->bg/dot_general | solution.py:98
  34.0 0.0 copy-start.3
  34.0 0.7 reshape.29
  34.8 8.9 %all-to-all-start = ((f32[16,1,544]{2,1,0:T(1,128)}), f32[16,1,544]{2,1,0:T(1,128)S(1)}, u32[]{:S(2)}, u32[]{:S(2)}) async-start(f32[16,1,544]{2,1,0:T(1,128)} %reshape.29), calls=%async_computation | async-start | bytes 81920 | tf_op jit(solution)/shard_map/all_to_all | solution.py:60
  43.6 1.7 %fusion.15 = f32[4,4096]{1,0:T(4,128)S(1)} fusion(f32[17,4,4096]{2,0,1:T(8,128)} %copy-done.1), kind=kLoop, calls=%fused_computation.25 | loop fusion | flops 507904 | bytes 1114112 | tf_op jit(solution)/shard_map/reduce_sum | solution.py:97
  45.3 5.7 %all-to-all-done = f32[16,1,544]{2,1,0:T(1,128)S(1)} async-done(((f32[16,1,544]{2,1,0:T(1,128)}), f32[16,1,544]{2,1,0:T(1,128)S(1)}, u32[]{:S(2)}, u32[]{:S(2)}) %all-to-all-start) | async-done | bytes 34848 | tf_op jit(solution)/shard_map/all_to_all | solution.py:60
  51.1 0.5 broadcast.21
  51.6 0.7 reduce.1
  52.3 0.1 reshape.30
  52.5 0.7 copy.35
  53.2 12.9 %all-to-all-start.1 = ((f32[32,1,544]{2,1,0:T(1,128)}), f32[32,1,544]{2,1,0:T(1,128)S(1)}, u32[]{:S(2)}, u32[]{:S(2)}) async-start(f32[32,1,544]{2,1,0:T(1,128)} %copy.35), calls=%async_computation.1 | async-start | bytes 163840 | tf_op jit(solution)/shard_map/all_to_all | solution.py:71
  66.1 1.1 %slice.151 = f32[1,4,4096]{2,0,1:T(1,128)S(1)} slice(f32[17,4,4096]{2,0,1:T(8,128)} %copy-done.1), slice={[0:1], [0:4], [0:4096]} | slice | bytes 131072 | tf_op jit(solution)/shard_map/slice | solution.py:95
  67.2 7.8 %all-to-all-done.1 = f32[32,1,544]{2,1,0:T(1,128)S(1)} async-done(((f32[32,1,544]{2,1,0:T(1,128)}), f32[32,1,544]{2,1,0:T(1,128)S(1)}, u32[]{:S(2)}, u32[]{:S(2)}) %all-to-all-start.1) | async-done | bytes 69664 | tf_op jit(solution)/shard_map/all_to_all | solution.py:71
  75.0 0.1 reduce_sum.48
  75.1 0.6 bitcast_add_fusion
  75.7 0.6 select_reduce_fusion
  (20 shorter events, 0.3 us)
Async XLA Ops:
  0.6 30.5 %copy-start = (f32[32,4,4096]{2,1,0:T(4,128)S(1)}, f32[32,4,4096]{2,1,0:T(4,128)}, u32[]{:S(2)}) copy-start(f32[32,4,4096]{2,1,0:T(4,128)} %param.10) | copy-start | bytes 6291460
  0.6 9.6 %copy-start.2 = (f32[4,4096]{1,0:T(4,128)S(1)}, f32[4,4096]{1,0:T(4,128)}, u32[]{:S(2)}) copy-start(f32[4,4096]{1,0:T(4,128)} %param.6) | copy-start | bytes 196612
  10.6 14.3 %collective-permute-start = (f32[18,2,4096]{2,0,1:T(8,128)S(1)}, f32[18,2,4096]{2,0,1:T(8,128)S(1)}, u32[]{:S(2)}, u32[]{:S(2)}) collective-permute-start(f32[18,2,4096]{2,0,1:T(8,128)S(1)} %get-tuple-element.3), channel_id=1, source_target_pairs={{32,64},{96,128},{160,192},{224,256},{288,320},{352,384},{416,448}... | collective-permute-start | bytes 1769480 | tf_op jit(solution)/shard_map/ppermute | solution.py:87
  15.2 9.7 %collective-permute-start.1 = (f32[18,2,4096]{2,0,1:T(8,128)S(1)}, f32[18,2,4096]{2,0,1:T(8,128)S(1)}, u32[]{:S(2)}, u32[]{:S(2)}) collective-permute-start(f32[18,2,4096]{2,0,1:T(8,128)S(1)} %get-tuple-element.4), channel_id=1, source_target_pairs={{0,32},{64,96},{128,160},{192,224},{256,288},{320,352},{384,416},{... | collective-permute-start | bytes 1769480 | tf_op jit(solution)/shard_map/ppermute | solution.py:88
  30.0 1.2 %copy-start.1 = (f32[17,4,4096]{2,0,1:T(8,128)}, f32[17,4,4096]{2,0,1:T(8,128)S(1)}, u32[]{:S(2)}) copy-start(f32[17,4,4096]{2,0,1:T(8,128)S(1)} %fusion.10) | copy-start | bytes 3342340
  34.0 41.7 %copy-start.3 = (s32[128]{0:T(128)S(1)}, s32[128]{0:T(128)}, u32[]{:S(2)}) copy-start(s32[128]{0:T(128)} %param.11) | copy-start | bytes 1540
  34.8 16.3 %all-to-all-start = ((f32[16,1,544]{2,1,0:T(1,128)}), f32[16,1,544]{2,1,0:T(1,128)S(1)}, u32[]{:S(2)}, u32[]{:S(2)}) async-start(f32[16,1,544]{2,1,0:T(1,128)} %reshape.29), calls=%async_computation | async-start | bytes 81920 | tf_op jit(solution)/shard_map/all_to_all | solution.py:60
  53.2 21.8 %all-to-all-start.1 = ((f32[32,1,544]{2,1,0:T(1,128)}), f32[32,1,544]{2,1,0:T(1,128)S(1)}, u32[]{:S(2)}, u32[]{:S(2)}) async-start(f32[32,1,544]{2,1,0:T(1,128)} %copy.35), calls=%async_computation.1 | async-start | bytes 163840 | tf_op jit(solution)/shard_map/all_to_all | solution.py:71

commit v15 on v11

--- a/solution.py
+++ b/solution.py
@@ -91,10 +91,9 @@
     after = jnp.where(even, near, far)
     fields = jnp.concatenate([before[:-1], body, after[:-1]], axis=1)
     rate_ext = jnp.concatenate([before[-1, 1:], rate_field, after[-1, :1]], axis=0)
-    fields = update(fields, rate_ext)
-    fields = update(fields, rate_field)
-    centre_moved = fields[0]
-    gens_moved = fields[1:]
+    centre_moved = update(update(fields[:1], rate_ext), rate_field)[0]
+    gens_moved = update(update(fields[1:], rate_ext), rate_field)
+    fields = jnp.concatenate([centre_moved[None], gens_moved], axis=0)
     radius_local = jnp.sum(jnp.abs(gens_moved), axis=0)
     all_proj = jnp.einsum(
         "bzc,gzc->bg", direction_bank, fields, precision=lax.Precision.HIGHEST

time: 71.2 us -> 71.4 us (level)
  waiting for transfers between devices: 18.3 us -> 25.1 us
  starting transfers between devices: 31.3 us -> 27 us
  local copies, waits for them, and re-layouts: 7.47 us -> 5.95 us
  other arithmetic: 10.1 us -> 9.24 us
    all_to_all x1, starting transfers between devices: 8.88 us -> 3.39 us  [exchange_sum(): received = lax.all_to_all(copies, axis, 0, 0, tiled=False)]
    ppermute x1, waiting for transfers between devices: 4.73 us -> 9.25 us  [per_device(): far = lax.ppermute(jnp.where(even, lower, upper), 'slab', across)]
    ppermute x1, starting transfers between devices: 4.9 us -> 8.79 us  [per_device(): near = lax.ppermute(jnp.where(even, upper, lower), 'slab', within)]
    ppermute x1, starting transfers between devices: 4.59 us -> 1.92 us  [per_device(): far = lax.ppermute(jnp.where(even, lower, upper), 'slab', across)]
    unnamed x11 -> x9, local copies, waits for them, and re-layouts: 4 us -> 2.71 us
    all_to_all x1, waiting for transfers between devices: 5.72 us -> 6.97 us  [exchange_sum(): received = lax.all_to_all(copies, axis, 0, 0, tiled=False)]
    add x2 -> x3, other arithmetic: 4.48 us -> 3.35 us  [update(): return middle + rate_field * (zsum + lateral(middle) - 6.0 * middle)]
    all_to_all x1, waiting for transfers between devices: 7.85 us -> 8.93 us  [exchange_scatter(): received = jnp.sum(lax.all_to_all(message, axis, 0, 0, tiled=True), axis=0)]
  transfers between devices with their start and end apart: 4 -> 4, of which waited for: 3 -> 3; matrix products, arithmetic and copies ran while one was open for 4% -> 1% of each run, Pallas kernels for 0% -> 0%
where the time goes in v15:
time: 71.4 us; the launch traced here: 71.1 us
  starting transfers between devices  27 us (38%)
  waiting for transfers between devices  25.1 us (35%)
  other arithmetic  9.24 us (13%)
  local copies, waits for them, and re-layouts  5.95 us (8%)
  matrix products  2.84 us (4%)
  between operations  0.92 us (1%)
    all_to_all x1, starting transfers between devices, exchange_scatter(): received = jnp.sum(lax.all_to_all(message, axis, 0, 0, tiled=True), axis=0)  12.9 us
    ppermute x1, waiting for transfers between devices, per_device(): far = lax.ppermute(jnp.where(even, lower, upper), 'slab', across)  9.25 us
    all_to_all x1, waiting for transfers between devices, exchange_scatter(): received = jnp.sum(lax.all_to_all(message, axis, 0, 0, tiled=True), axis=0)  8.93 us
    ppermute x1, starting transfers between devices, per_device(): near = lax.ppermute(jnp.where(even, upper, lower), 'slab', within)  8.79 us
    all_to_all x1, waiting for transfers between devices, exchange_sum(): received = lax.all_to_all(copies, axis, 0, 0, tiled=False)  6.97 us
    all_to_all x1, starting transfers between devices, exchange_sum(): received = lax.all_to_all(copies, axis, 0, 0, tiled=False)  3.39 us
    add x3, other arithmetic, update(): return middle + rate_field * (zsum + lateral(middle) - 6.0 * middle)  3.35 us
    dot_general x1, matrix products, per_device(): jnp.einsum('bzc,gzc->bg', direction_bank, fields, precision=lax.Precision...  2.84 us
  transfers between devices with their start and end apart: 4, of which 3 were waited for; matrix products, arithmetic and copies ran while one was open for 1% of the time, Pallas kernels for 0%

profile of v15, /device:TPU:1, one launch (start us, length us, event | category | flops | bytes accessed | tf_op | source)
XLA Modules:
  0.0 71.1 jit_solution(9187501940404247329)
XLA Ops:
  0.7 1.2 %select_reduce_fusion = f32[4,4096]{1,0:T(4,128)S(1)} fusion(f32[8]{0:T(128)} %param.9, s32[4,4096]{1,0:T(4,128)} %param.8), kind=kLoop, calls=%fused_computation.40 | loop fusion | flops 376832 | bytes 131104 | tf_op jit(solution)/shard_map/reduce_sum | solution.py:31
  2.0 0.9 %broadcast_in_dim.105 = f32[1,4,4096]{2,0,1:T(1,128)S(1)} reshape(f32[4,4096]{1,0:T(4,128)} %param.6) | data formatting | bytes 131072 | tf_op jit(solution)/shard_map/broadcast_in_dim | solution.py:78
  2.9 1.8 %copy.33 = f32[16,4,4096]{2,0,1:T(8,128)S(1)} copy(f32[16,4,4096]{2,1,0:T(4,128)} %param.7) | data formatting | bytes 2097152 | tf_op args[1]
  4.8 0.1 fusion.21
  4.9 0.2 fusion.24
  5.1 0.5 copy.37
  5.6 8.8 %collective-permute-start.1 = (f32[18,2,4096]{2,1,0:T(2,128)S(1)}, f32[18,2,4096]{2,1,0:T(2,128)S(1)}, u32[]{:S(2)}, u32[]{:S(2)}) collective-permute-start(f32[18,2,4096]{2,1,0:T(2,128)S(1)} %copy.37), channel_id=1, source_target_pairs={{0,32},{64,96},{128,160},{192,224},{256,288},{320,352},{384,416},{... | collective-permute-start | bytes 1769480 | tf_op jit(solution)/shard_map/ppermute | solution.py:89
  14.4 0.5 copy.36
  14.8 1.9 %collective-permute-start = (f32[18,2,4096]{2,1,0:T(2,128)S(1)}, f32[18,2,4096]{2,1,0:T(2,128)S(1)}, u32[]{:S(2)}, u32[]{:S(2)}) collective-permute-start(f32[18,2,4096]{2,1,0:T(2,128)S(1)} %copy.36), channel_id=1, source_target_pairs={{32,64},{96,128},{160,192},{224,256},{288,320},{352,384},{416,448}... | collective-permute-start | bytes 1769480 | tf_op jit(solution)/shard_map/ppermute | solution.py:88
  16.8 9.2 %collective-permute-done = f32[18,2,4096]{2,1,0:T(2,128)S(1)} collective-permute-done((f32[18,2,4096]{2,1,0:T(2,128)S(1)}, f32[18,2,4096]{2,1,0:T(2,128)S(1)}, u32[]{:S(2)}, u32[]{:S(2)}) %collective-permute-start) | collective-permute-done | bytes 589856 | tf_op jit(solution)/shard_map/ppermute | solution.py:88
  26.0 0.7 copy_select_fusion.1
  26.7 0.1 pad_maximum_fusion.10
  26.8 0.2 pad_maximum_fusion.4
  27.1 0.1 pad_maximum_fusion.9
  27.1 0.9 %fusion.28 = f32[1,6,4096]{2,0,1:T(1,128)S(1)} fusion(f32[1,6,4096]{2,0,1:T(1,128)S(1)} %pad_maximum_fusion.10, f32[1,6,4096]{2,1,0:T(8,128)S(1)} %get-tuple-element.10, pred[4096]{0:T(1024)(128)(4,1)S(1)} %get-tuple-element.17, pred[4096]{0:T(1024)(128)(4,1)S(1)} %get-tuple-element.18, f32[16,4,4096]{2,0,1:T(8,128)S(1)} %copy.33, ...), kind=kLoop, calls=%fused_computation.53 | loop fusion | flops 368640 | bytes 2531328 | tf_op jit(solution)/shard_map/add | solution.py:48
  28.0 0.6 multiply_add_fusion
  28.6 1.9 %fusion.6 = f32[16,6,4096]{2,0,1:T(8,128)S(1)} fusion(f32[16,6,4096]{2,0,1:T(8,128)S(1)} %pad_maximum_fusion.4, f32[17,2,4096]{2,0,1:T(8,128)S(1)} %bitcast.40, f32[16,4,4096]{2,0,1:T(8,128)S(1)} %copy.33, f32[1,4,4096]{2,0,1:T(1,128)S(1)} %broadcast_in_dim.105, f32[17,2,4096]{2,0,1:T(8,128)S(1)} %bitcast.44, f32[6,4096]{1,0:T(8,128)S(1)} %get-tuple-element.9, ...), kind=kLoop, calls=%fused_computation.7 | loop fusion | flops 5898240 | bytes 5480448 | tf_op jit(solution)/shard_map/add | solution.py:48
  30.5 0.1 slice.183
  30.6 1.2 %abs_reduce_fusion = (f32[4,4096]{1,0:T(4,128)S(1)}, f32[16,4,4096]{2,0,1:T(8,128)S(1)}) fusion(f32[16,4,4096]{2,0,1:T(8,128)S(1)} %slice.183, pred[4096]{0:T(1024)(128)(4,1)S(1)} %get-tuple-element.17, pred[4096]{0:T(1024)(128)(4,1)S(1)} %get-tuple-element.18, f32[16,6,4096]{2,0,1:T(8,128)S(1)} %fusion.6, f32[4,4096]{1,0:T(4,128)S(1)} %broadcast_multiply_fusion), kind=kLoop, calls=%fused_computation.28 | loop fusion | flops 3391488 | bytes 4333568 | tf_op jit(solution)/shard_map/reduce_sum | solution.py:97
  31.8 2.8 %fusion.11 = f32[32,17]{0,1:T(8,128)S(1)} fusion(f32[32,4,4096]{2,1,0:T(4,128)S(1)} %copy-done, f32[16,4,4096]{2,0,1:T(8,128)S(1)} %get-tuple-element.4, f32[1,4,4096]{2,0,1:T(1,128)S(1)} %multiply_add_fusion), kind=kOutput, calls=%fused_computation.22 | convolution fusion | flops 107233280 | bytes 3213440 | tf_op jit(solution)/shard_map/bzc,gzc->bg/dot_general | solution.py:98
  34.7 0.7 %reshape.39 = f32[16,1,544]{2,1,0:T(1,128)} reshape(f32[16,17,32]{2,1,0:T(8,128)S(1)} %broadcast_bitcast_fusion) | data formatting | bytes 69632
  35.4 3.4 %all-to-all-start = ((f32[16,1,544]{2,1,0:T(1,128)}), f32[16,1,544]{2,1,0:T(1,128)S(1)}, u32[]{:S(2)}, u32[]{:S(2)}) async-start(f32[16,1,544]{2,1,0:T(1,128)} %reshape.39), calls=%async_computation | async-start | bytes 81920 | tf_op jit(solution)/shard_map/all_to_all | solution.py:61
  38.9 7.0 %all-to-all-done = f32[16,1,544]{2,1,0:T(1,128)S(1)} async-done(((f32[16,1,544]{2,1,0:T(1,128)}), f32[16,1,544]{2,1,0:T(1,128)S(1)}, u32[]{:S(2)}, u32[]{:S(2)}) %all-to-all-start) | async-done | bytes 34848 | tf_op jit(solution)/shard_map/all_to_all | solution.py:61
  45.8 0.5 broadcast.38
  46.3 0.7 %reduce.1 = f32[16,544]{1,0:T(8,128)S(1)} reduce(f32[16,1,544]{2,1,0:T(1,128)S(1)} %all-to-all-done, f32[]{:T(128)} %broadcast.38), dimensions={1}, to_apply=%all_to_all.9.reduce_sub_computation | reduce | bytes 69636 | tf_op jit(solution)/shard_map/all_to_all | solution.py:61
  47.1 0.1 reshape.40
  47.3 0.7 copy.44
  48.0 12.9 %all-to-all-start.1 = ((f32[32,1,544]{2,1,0:T(1,128)}), f32[32,1,544]{2,1,0:T(1,128)S(1)}, u32[]{:S(2)}, u32[]{:S(2)}) async-start(f32[32,1,544]{2,1,0:T(1,128)} %copy.44), calls=%async_computation.1 | async-start | bytes 163840 | tf_op jit(solution)/shard_map/all_to_all | solution.py:72
  60.9 8.9 %all-to-all-done.1 = f32[32,1,544]{2,1,0:T(1,128)S(1)} async-done(((f32[32,1,544]{2,1,0:T(1,128)}), f32[32,1,544]{2,1,0:T(1,128)S(1)}, u32[]{:S(2)}, u32[]{:S(2)}) %all-to-all-start.1) | async-done | bytes 69664 | tf_op jit(solution)/shard_map/all_to_all | solution.py:72
  69.8 0.1 reduce_sum.58
  69.9 0.6 bitcast_add_fusion
  70.5 0.6 select_reduce_fusion.1
  (20 shorter events, 0.3 us)
Async XLA Ops:
  0.6 31.2 %copy-start = (f32[32,4,4096]{2,1,0:T(4,128)S(1)}, f32[32,4,4096]{2,1,0:T(4,128)}, u32[]{:S(2)}) copy-start(f32[32,4,4096]{2,1,0:T(4,128)} %param.10) | copy-start | bytes 6291460
  5.6 11.2 %collective-permute-start.1 = (f32[18,2,4096]{2,1,0:T(2,128)S(1)}, f32[18,2,4096]{2,1,0:T(2,128)S(1)}, u32[]{:S(2)}, u32[]{:S(2)}) collective-permute-start(f32[18,2,4096]{2,1,0:T(2,128)S(1)} %copy.37), channel_id=1, source_target_pairs={{0,32},{64,96},{128,160},{192,224},{256,288},{320,352},{384,416},{... | collective-permute-start | bytes 1769480 | tf_op jit(solution)/shard_map/ppermute | solution.py:89
  14.8 11.2 %collective-permute-start = (f32[18,2,4096]{2,1,0:T(2,128)S(1)}, f32[18,2,4096]{2,1,0:T(2,128)S(1)}, u32[]{:S(2)}, u32[]{:S(2)}) collective-permute-start(f32[18,2,4096]{2,1,0:T(2,128)S(1)} %copy.36), channel_id=1, source_target_pairs={{32,64},{96,128},{160,192},{224,256},{288,320},{352,384},{416,448}... | collective-permute-start | bytes 1769480 | tf_op jit(solution)/shard_map/ppermute | solution.py:88
  34.7 35.8 %copy-start.1 = (s32[128]{0:T(128)S(1)}, s32[128]{0:T(128)}, u32[]{:S(2)}) copy-start(s32[128]{0:T(128)} %param.11) | copy-start | bytes 1540
  35.4 10.4 %all-to-all-start = ((f32[16,1,544]{2,1,0:T(1,128)}), f32[16,1,544]{2,1,0:T(1,128)S(1)}, u32[]{:S(2)}, u32[]{:S(2)}) async-start(f32[16,1,544]{2,1,0:T(1,128)} %reshape.39), calls=%async_computation | async-start | bytes 81920 | tf_op jit(solution)/shard_map/all_to_all | solution.py:61
  48.0 21.8 %all-to-all-start.1 = ((f32[32,1,544]{2,1,0:T(1,128)}), f32[32,1,544]{2,1,0:T(1,128)S(1)}, u32[]{:S(2)}, u32[]{:S(2)}) async-start(f32[32,1,544]{2,1,0:T(1,128)} %copy.44), calls=%async_computation.1 | async-start | bytes 163840 | tf_op jit(solution)/shard_map/all_to_all | solution.py:72

commit v16 on v15

--- a/solution.py
+++ b/solution.py
@@ -57,9 +57,10 @@
 
 def exchange_sum(x, axis):
     size = lax.axis_size(axis)
-    copies = jnp.broadcast_to(x[None], (size,) + x.shape)
-    received = lax.all_to_all(copies, axis, 0, 0, tiled=False)
-    return jnp.sum(received, axis=0)
+    flat = x.reshape(-1)
+    copies = jnp.broadcast_to(flat[None], (size, flat.shape[0]))
+    received = lax.all_to_all(copies, axis, 0, 0, tiled=True)
+    return jnp.sum(received, axis=0).reshape(x.shape)
 
 
 def exchange_scatter(x, extra, axis):

time: 71.4 us -> 70.3 us (0.985)
  other arithmetic: 9.24 us -> 8.46 us
    unnamed x9 -> x6, local copies, waits for them, and re-layouts: 2.71 us -> 1.86 us
    broadcast_in_dim x0 -> x2, local copies, waits for them, and re-layouts: none -> 0.74 us  [exchange_sum(): copies = jnp.broadcast_to(flat[None], (size, flat.shape[0]))]
    all_to_all x1 -> x0, other arithmetic: 0.74 us -> none  [exchange_sum(): received = lax.all_to_all(copies, axis, 0, 0, tiled=False)]
where the time goes in v16:
time: 70.3 us; the launch traced here: 70 us
  starting transfers between devices  27 us (38%)
  waiting for transfers between devices  25 us (36%)
  other arithmetic  8.46 us (12%)
  local copies, waits for them, and re-layouts  5.77 us (8%)
  matrix products  2.84 us (4%)
  between operations  0.91 us (1%)
    all_to_all x1, starting transfers between devices, exchange_scatter(): received = jnp.sum(lax.all_to_all(message, axis, 0, 0, tiled=True), axis=0)  12.9 us
    ppermute x1, waiting for transfers between devices, per_device(): far = lax.ppermute(jnp.where(even, lower, upper), 'slab', across)  9.25 us
    all_to_all x1, waiting for transfers between devices, exchange_scatter(): received = jnp.sum(lax.all_to_all(message, axis, 0, 0, tiled=True), axis=0)  8.82 us
    ppermute x1, starting transfers between devices, per_device(): near = lax.ppermute(jnp.where(even, upper, lower), 'slab', within)  8.79 us
    all_to_all x1, waiting for transfers between devices, exchange_sum(): received = lax.all_to_all(copies, axis, 0, 0, tiled=True)  6.96 us
    all_to_all x1, starting transfers between devices, exchange_sum(): received = lax.all_to_all(copies, axis, 0, 0, tiled=True)  3.39 us
    add x3, other arithmetic, update(): return middle + rate_field * (zsum + lateral(middle) - 6.0 * middle)  3.33 us
    dot_general x1, matrix products, per_device(): jnp.einsum('bzc,gzc->bg', direction_bank, fields, precision=lax.Precision...  2.84 us
  transfers between devices with their start and end apart: 4, of which 3 were waited for; matrix products, arithmetic and copies ran while one was open for 1% of the time, Pallas kernels for 0%

profile of v16, /device:TPU:1, one launch (start us, length us, event | category | flops | bytes accessed | tf_op | source)
XLA Modules:
  0.0 70.0 jit_solution(12414065414766294554)
XLA Ops:
  0.7 1.0 %broadcast_in_dim.106 = f32[1,4,4096]{2,0,1:T(1,128)S(1)} reshape(f32[4,4096]{1,0:T(4,128)} %param.6) | data formatting | bytes 131072 | tf_op jit(solution)/shard_map/broadcast_in_dim | solution.py:79
  1.7 1.1 %select_reduce_fusion = f32[4,4096]{1,0:T(4,128)S(1)} fusion(f32[8]{0:T(128)} %param.9, s32[4,4096]{1,0:T(4,128)} %param.8), kind=kLoop, calls=%fused_computation.40 | loop fusion | flops 376832 | bytes 131104 | tf_op jit(solution)/shard_map/reduce_sum | solution.py:31
  3.0 1.8 %copy.52 = f32[16,4,4096]{2,0,1:T(8,128)S(1)} copy(f32[16,4,4096]{2,1,0:T(4,128)} %param.7) | data formatting | bytes 2097152 | tf_op args[1]
  4.8 0.1 fusion.21
  4.9 0.2 fusion.24
  5.1 0.5 copy.56
  5.6 8.8 %collective-permute-start.1 = (f32[18,2,4096]{2,1,0:T(2,128)S(1)}, f32[18,2,4096]{2,1,0:T(2,128)S(1)}, u32[]{:S(2)}, u32[]{:S(2)}) collective-permute-start(f32[18,2,4096]{2,1,0:T(2,128)S(1)} %copy.56), channel_id=1, source_target_pairs={{0,32},{64,96},{128,160},{192,224},{256,288},{320,352},{384,416},{... | collective-permute-start | bytes 1769480 | tf_op jit(solution)/shard_map/ppermute | solution.py:90
  14.4 0.5 copy.55
  14.8 1.9 %collective-permute-start = (f32[18,2,4096]{2,1,0:T(2,128)S(1)}, f32[18,2,4096]{2,1,0:T(2,128)S(1)}, u32[]{:S(2)}, u32[]{:S(2)}) collective-permute-start(f32[18,2,4096]{2,1,0:T(2,128)S(1)} %copy.55), channel_id=1, source_target_pairs={{32,64},{96,128},{160,192},{224,256},{288,320},{352,384},{416,448}... | collective-permute-start | bytes 1769480 | tf_op jit(solution)/shard_map/ppermute | solution.py:89
  16.8 9.2 %collective-permute-done = f32[18,2,4096]{2,1,0:T(2,128)S(1)} collective-permute-done((f32[18,2,4096]{2,1,0:T(2,128)S(1)}, f32[18,2,4096]{2,1,0:T(2,128)S(1)}, u32[]{:S(2)}, u32[]{:S(2)}) %collective-permute-start) | collective-permute-done | bytes 589856 | tf_op jit(solution)/shard_map/ppermute | solution.py:89
  26.0 0.7 copy_select_fusion.1
  26.7 0.1 pad_maximum_fusion.10
  26.8 0.2 pad_maximum_fusion.4
  27.1 0.9 %fusion.28 = f32[1,6,4096]{2,0,1:T(1,128)S(1)} fusion(f32[1,6,4096]{2,0,1:T(1,128)S(1)} %pad_maximum_fusion.10, f32[1,6,4096]{2,1,0:T(8,128)S(1)} %get-tuple-element.10, pred[4096]{0:T(1024)(128)(4,1)S(1)} %get-tuple-element.17, pred[4096]{0:T(1024)(128)(4,1)S(1)} %get-tuple-element.18, f32[16,4,4096]{2,0,1:T(8,128)S(1)} %copy.52, ...), kind=kLoop, calls=%fused_computation.53 | loop fusion | flops 368640 | bytes 2531328 | tf_op jit(solution)/shard_map/add | solution.py:48
  28.0 0.6 multiply_add_fusion
  28.6 1.8 %fusion.6 = f32[16,6,4096]{2,0,1:T(8,128)S(1)} fusion(f32[16,6,4096]{2,0,1:T(8,128)S(1)} %pad_maximum_fusion.4, f32[17,2,4096]{2,0,1:T(8,128)S(1)} %bitcast.32, f32[16,4,4096]{2,0,1:T(8,128)S(1)} %copy.52, f32[1,4,4096]{2,0,1:T(1,128)S(1)} %broadcast_in_dim.106, f32[17,2,4096]{2,0,1:T(8,128)S(1)} %bitcast.36, f32[6,4096]{1,0:T(8,128)S(1)} %get-tuple-element.9, ...), kind=kLoop, calls=%fused_computation.7 | loop fusion | flops 5898240 | bytes 5480448 | tf_op jit(solution)/shard_map/add | solution.py:48
  30.4 0.1 slice.183
  30.5 1.2 %abs_reduce_fusion = (f32[4,4096]{1,0:T(4,128)S(1)}, f32[16,4,4096]{2,0,1:T(8,128)S(1)}) fusion(f32[16,4,4096]{2,0,1:T(8,128)S(1)} %slice.183, pred[4096]{0:T(1024)(128)(4,1)S(1)} %get-tuple-element.17, pred[4096]{0:T(1024)(128)(4,1)S(1)} %get-tuple-element.18, f32[16,6,4096]{2,0,1:T(8,128)S(1)} %fusion.6, f32[4,4096]{1,0:T(4,128)S(1)} %broadcast_multiply_fusion), kind=kLoop, calls=%fused_computation.28 | loop fusion | flops 3391488 | bytes 4333568 | tf_op jit(solution)/shard_map/reduce_sum | solution.py:98
  31.8 2.8 %fusion.11 = f32[32,17]{0,1:T(8,128)S(1)} fusion(f32[32,4,4096]{2,1,0:T(4,128)S(1)} %copy-done, f32[16,4,4096]{2,0,1:T(8,128)S(1)} %get-tuple-element.4, f32[1,4,4096]{2,0,1:T(1,128)S(1)} %multiply_add_fusion), kind=kOutput, calls=%fused_computation.22 | convolution fusion | flops 107233280 | bytes 3213440 | tf_op jit(solution)/shard_map/bzc,gzc->bg/dot_general | solution.py:99
  34.6 0.1 copy.63
  34.7 0.1 broadcast_in_dim.124
  34.8 0.6 broadcast_in_dim.125
  35.4 3.4 %all-to-all-start = ((f32[16,1,544]{2,1,0:T(1,128)}), f32[16,1,544]{2,1,0:T(1,128)S(1)}, u32[]{:S(2)}, u32[]{:S(2)}) async-start(f32[16,1,544]{2,1,0:T(1,128)} %broadcast_in_dim.125), calls=%async_computation | async-start | bytes 81920 | tf_op jit(solution)/shard_map/all_to_all | solution.py:62
  38.9 7.0 %all-to-all-done = f32[16,1,544]{2,1,0:T(1,128)S(1)} async-done(((f32[16,1,544]{2,1,0:T(1,128)}), f32[16,1,544]{2,1,0:T(1,128)S(1)}, u32[]{:S(2)}, u32[]{:S(2)}) %all-to-all-start) | async-done | bytes 34848 | tf_op jit(solution)/shard_map/all_to_all | solution.py:62
  45.9 0.1 reshape.46
  46.0 0.2 fusion.32
  46.2 0.7 %copy.65 = f32[32,1,544]{2,1,0:T(1,128)} copy(f32[32,1,544]{2,0,1:T(8,128)S(1)} %maximum_bitcast_fusion) | data formatting | bytes 139264 | tf_op jit(solution)/shard_map/all_to_all | solution.py:73
  46.9 12.9 %all-to-all-start.1 = ((f32[32,1,544]{2,1,0:T(1,128)}), f32[32,1,544]{2,1,0:T(1,128)S(1)}, u32[]{:S(2)}, u32[]{:S(2)}) async-start(f32[32,1,544]{2,1,0:T(1,128)} %copy.65), calls=%async_computation.1 | async-start | bytes 163840 | tf_op jit(solution)/shard_map/all_to_all | solution.py:73
  59.8 0.1 slice_reduce_fusion
  59.9 8.8 %all-to-all-done.1 = f32[32,1,544]{2,1,0:T(1,128)S(1)} async-done(((f32[32,1,544]{2,1,0:T(1,128)}), f32[32,1,544]{2,1,0:T(1,128)S(1)}, u32[]{:S(2)}, u32[]{:S(2)}) %all-to-all-start.1) | async-done | bytes 69664 | tf_op jit(solution)/shard_map/all_to_all | solution.py:73
  68.8 0.6 bitcast_add_fusion
  69.4 0.6 select_reduce_fusion.1
  (20 shorter events, 0.4 us)
Async XLA Ops:
  0.6 31.1 %copy-start = (f32[32,4,4096]{2,1,0:T(4,128)S(1)}, f32[32,4,4096]{2,1,0:T(4,128)}, u32[]{:S(2)}) copy-start(f32[32,4,4096]{2,1,0:T(4,128)} %param.10) | copy-start | bytes 6291460
  5.6 11.2 %collective-permute-start.1 = (f32[18,2,4096]{2,1,0:T(2,128)S(1)}, f32[18,2,4096]{2,1,0:T(2,128)S(1)}, u32[]{:S(2)}, u32[]{:S(2)}) collective-permute-start(f32[18,2,4096]{2,1,0:T(2,128)S(1)} %copy.56), channel_id=1, source_target_pairs={{0,32},{64,96},{128,160},{192,224},{256,288},{320,352},{384,416},{... | collective-permute-start | bytes 1769480 | tf_op jit(solution)/shard_map/ppermute | solution.py:90
  14.8 11.2 %collective-permute-start = (f32[18,2,4096]{2,1,0:T(2,128)S(1)}, f32[18,2,4096]{2,1,0:T(2,128)S(1)}, u32[]{:S(2)}, u32[]{:S(2)}) collective-permute-start(f32[18,2,4096]{2,1,0:T(2,128)S(1)} %copy.55), channel_id=1, source_target_pairs={{32,64},{96,128},{160,192},{224,256},{288,320},{352,384},{416,448}... | collective-permute-start | bytes 1769480 | tf_op jit(solution)/shard_map/ppermute | solution.py:89
  31.8 37.6 %copy-start.1 = (s32[128]{0:T(128)S(1)}, s32[128]{0:T(128)}, u32[]{:S(2)}) copy-start(s32[128]{0:T(128)} %param.11) | copy-start | bytes 1540
  35.4 10.4 %all-to-all-start = ((f32[16,1,544]{2,1,0:T(1,128)}), f32[16,1,544]{2,1,0:T(1,128)S(1)}, u32[]{:S(2)}, u32[]{:S(2)}) async-start(f32[16,1,544]{2,1,0:T(1,128)} %broadcast_in_dim.125), calls=%async_computation | async-start | bytes 81920 | tf_op jit(solution)/shard_map/all_to_all | solution.py:62
  46.9 21.8 %all-to-all-start.1 = ((f32[32,1,544]{2,1,0:T(1,128)}), f32[32,1,544]{2,1,0:T(1,128)S(1)}, u32[]{:S(2)}, u32[]{:S(2)}) async-start(f32[32,1,544]{2,1,0:T(1,128)} %copy.65), calls=%async_computation.1 | async-start | bytes 163840 | tf_op jit(solution)/shard_map/all_to_all | solution.py:73

commit v17 on v16

--- a/solution.py
+++ b/solution.py
@@ -67,11 +67,12 @@
     size = lax.axis_size(axis)
     rows, cols = x.shape
     width = cols // size
-    blocks = x.reshape(rows, size, width).transpose(1, 0, 2).reshape(size, rows * width)
-    extras = jnp.broadcast_to(extra[None], (size, extra.shape[0]))
-    message = jnp.concatenate([blocks, extras], axis=1)
-    received = jnp.sum(lax.all_to_all(message, axis, 0, 0, tiled=True), axis=0)
-    return received[: rows * width].reshape(rows, width), received[rows * width :]
+    blocks = x.reshape(rows, size, width)
+    padded = jnp.pad(extra, (0, width - extra.shape[0]))
+    extras = jnp.broadcast_to(padded[None, None], (1, size, width))
+    message = jnp.concatenate([blocks, extras], axis=0)
+    received = jnp.sum(lax.all_to_all(message, axis, 1, 1, tiled=True), axis=1)
+    return received[:rows], received[rows, : extra.shape[0]]
 
 
 def per_device(center, generators, conductivity, cond_table, direction_bank, selection):

time: 70.3 us -> 70.7 us (level)
    all_to_all x1 -> x0, local copies, waits for them, and re-layouts: 0.71 us -> none  [exchange_scatter(): received = jnp.sum(lax.all_to_all(message, axis, 0, 0, tiled=True), axis=0)]
    unnamed x6 -> x5, local copies, waits for them, and re-layouts: 1.86 us -> 1.85 us
where the time goes in v17:
time: 70.7 us; the launch traced here: 70.3 us
  starting transfers between devices  27 us (38%)
  waiting for transfers between devices  25.4 us (36%)
  other arithmetic  9.09 us (13%)
  local copies, waits for them, and re-layouts  5.07 us (7%)
  matrix products  2.84 us (4%)
  between operations  0.91 us (1%)
    all_to_all x1, starting transfers between devices, exchange_scatter(): received = jnp.sum(lax.all_to_all(message, axis, 1, 1, tiled=True), axis=1)  12.9 us
    ppermute x1, waiting for transfers between devices, per_device(): far = lax.ppermute(jnp.where(even, lower, upper), 'slab', across)  9.25 us
    all_to_all x1, waiting for transfers between devices, exchange_scatter(): received = jnp.sum(lax.all_to_all(message, axis, 1, 1, tiled=True), axis=1)  9.22 us
    ppermute x1, starting transfers between devices, per_device(): near = lax.ppermute(jnp.where(even, upper, lower), 'slab', within)  8.79 us
    all_to_all x1, waiting for transfers between devices, exchange_sum(): received = lax.all_to_all(copies, axis, 0, 0, tiled=True)  6.97 us
    all_to_all x1, starting transfers between devices, exchange_sum(): received = lax.all_to_all(copies, axis, 0, 0, tiled=True)  3.39 us
    add x3, other arithmetic, update(): return middle + rate_field * (zsum + lateral(middle) - 6.0 * middle)  3.33 us
    dot_general x1, matrix products, per_device(): jnp.einsum('bzc,gzc->bg', direction_bank, fields, precision=lax.Precision...  2.84 us
  transfers between devices with their start and end apart: 4, of which 3 were waited for; matrix products, arithmetic and copies ran while one was open for 1% of the time, Pallas kernels for 0%

profile of v17, /device:TPU:1, one launch (start us, length us, event | category | flops | bytes accessed | tf_op | source)
XLA Modules:
  0.0 70.3 jit_solution(17208412739842029052)
XLA Ops:
  0.7 1.0 %broadcast_in_dim.108 = f32[1,4,4096]{2,0,1:T(1,128)S(1)} reshape(f32[4,4096]{1,0:T(4,128)} %param.6) | data formatting | bytes 131072 | tf_op jit(solution)/shard_map/broadcast_in_dim | solution.py:80
  1.7 1.1 %select_reduce_fusion = f32[4,4096]{1,0:T(4,128)S(1)} fusion(f32[8]{0:T(128)} %param.9, s32[4,4096]{1,0:T(4,128)} %param.8), kind=kLoop, calls=%fused_computation.40 | loop fusion | flops 376832 | bytes 131104 | tf_op jit(solution)/shard_map/reduce_sum | solution.py:31
  3.0 1.8 %copy.50 = f32[16,4,4096]{2,0,1:T(8,128)S(1)} copy(f32[16,4,4096]{2,1,0:T(4,128)} %param.7) | data formatting | bytes 2097152 | tf_op args[1]
  4.8 0.1 fusion.21
  4.9 0.2 fusion.24
  5.1 0.5 copy.54
  5.6 8.8 %collective-permute-start.1 = (f32[18,2,4096]{2,1,0:T(2,128)S(1)}, f32[18,2,4096]{2,1,0:T(2,128)S(1)}, u32[]{:S(2)}, u32[]{:S(2)}) collective-permute-start(f32[18,2,4096]{2,1,0:T(2,128)S(1)} %copy.54), channel_id=1, source_target_pairs={{0,32},{64,96},{128,160},{192,224},{256,288},{320,352},{384,416},{... | collective-permute-start | bytes 1769480 | tf_op jit(solution)/shard_map/ppermute | solution.py:91
  14.4 0.5 copy.53
  14.8 1.9 %collective-permute-start = (f32[18,2,4096]{2,1,0:T(2,128)S(1)}, f32[18,2,4096]{2,1,0:T(2,128)S(1)}, u32[]{:S(2)}, u32[]{:S(2)}) collective-permute-start(f32[18,2,4096]{2,1,0:T(2,128)S(1)} %copy.53), channel_id=1, source_target_pairs={{32,64},{96,128},{160,192},{224,256},{288,320},{352,384},{416,448}... | collective-permute-start | bytes 1769480 | tf_op jit(solution)/shard_map/ppermute | solution.py:90
  16.8 9.2 %collective-permute-done = f32[18,2,4096]{2,1,0:T(2,128)S(1)} collective-permute-done((f32[18,2,4096]{2,1,0:T(2,128)S(1)}, f32[18,2,4096]{2,1,0:T(2,128)S(1)}, u32[]{:S(2)}, u32[]{:S(2)}) %collective-permute-start) | collective-permute-done | bytes 589856 | tf_op jit(solution)/shard_map/ppermute | solution.py:90
  26.0 0.7 copy_select_fusion.1
  26.7 0.1 pad_maximum_fusion.11
  26.8 0.2 pad_maximum_fusion.4
  27.1 0.9 %fusion.28 = f32[1,6,4096]{2,0,1:T(1,128)S(1)} fusion(f32[1,6,4096]{2,0,1:T(1,128)S(1)} %pad_maximum_fusion.11, f32[1,6,4096]{2,1,0:T(8,128)S(1)} %get-tuple-element.10, pred[4096]{0:T(1024)(128)(4,1)S(1)} %get-tuple-element.17, pred[4096]{0:T(1024)(128)(4,1)S(1)} %get-tuple-element.18, f32[16,4,4096]{2,0,1:T(8,128)S(1)} %copy.50, ...), kind=kLoop, calls=%fused_computation.54 | loop fusion | flops 368640 | bytes 2531328 | tf_op jit(solution)/shard_map/add | solution.py:48
  28.0 0.6 multiply_add_fusion
  28.6 1.8 %fusion.6 = f32[16,6,4096]{2,0,1:T(8,128)S(1)} fusion(f32[16,6,4096]{2,0,1:T(8,128)S(1)} %pad_maximum_fusion.4, f32[17,2,4096]{2,0,1:T(8,128)S(1)} %bitcast.27, f32[16,4,4096]{2,0,1:T(8,128)S(1)} %copy.50, f32[1,4,4096]{2,0,1:T(1,128)S(1)} %broadcast_in_dim.108, f32[17,2,4096]{2,0,1:T(8,128)S(1)} %bitcast.31, f32[6,4096]{1,0:T(8,128)S(1)} %get-tuple-element.9, ...), kind=kLoop, calls=%fused_computation.7 | loop fusion | flops 5898240 | bytes 5480448 | tf_op jit(solution)/shard_map/add | solution.py:48
  30.4 0.1 slice.183
  30.5 1.2 %abs_reduce_fusion = (f32[4,4096]{1,0:T(4,128)S(1)}, f32[16,4,4096]{2,0,1:T(8,128)S(1)}) fusion(f32[16,4,4096]{2,0,1:T(8,128)S(1)} %slice.183, pred[4096]{0:T(1024)(128)(4,1)S(1)} %get-tuple-element.17, pred[4096]{0:T(1024)(128)(4,1)S(1)} %get-tuple-element.18, f32[16,6,4096]{2,0,1:T(8,128)S(1)} %fusion.6, f32[4,4096]{1,0:T(4,128)S(1)} %broadcast_multiply_fusion), kind=kLoop, calls=%fused_computation.28 | loop fusion | flops 3391488 | bytes 4333568 | tf_op jit(solution)/shard_map/reduce_sum | solution.py:99
  31.8 2.8 %fusion.11 = f32[32,17]{0,1:T(8,128)S(1)} fusion(f32[32,4,4096]{2,1,0:T(4,128)S(1)} %copy-done, f32[16,4,4096]{2,0,1:T(8,128)S(1)} %get-tuple-element.4, f32[1,4,4096]{2,0,1:T(1,128)S(1)} %multiply_add_fusion), kind=kOutput, calls=%fused_computation.22 | convolution fusion | flops 107233280 | bytes 3213440 | tf_op jit(solution)/shard_map/bzc,gzc->bg/dot_general | solution.py:100
  34.6 0.1 copy.61
  34.7 0.1 broadcast_in_dim.126
  34.8 0.6 broadcast_in_dim.127
  35.4 3.4 %all-to-all-start = ((f32[16,1,544]{2,1,0:T(1,128)}), f32[16,1,544]{2,1,0:T(1,128)S(1)}, u32[]{:S(2)}, u32[]{:S(2)}) async-start(f32[16,1,544]{2,1,0:T(1,128)} %broadcast_in_dim.127), calls=%async_computation | async-start | bytes 81920 | tf_op jit(solution)/shard_map/all_to_all | solution.py:62
  38.9 7.0 %all-to-all-done = f32[16,1,544]{2,1,0:T(1,128)S(1)} async-done(((f32[16,1,544]{2,1,0:T(1,128)}), f32[16,1,544]{2,1,0:T(1,128)S(1)}, u32[]{:S(2)}, u32[]{:S(2)}) %all-to-all-start) | async-done | bytes 34848 | tf_op jit(solution)/shard_map/all_to_all | solution.py:62
  45.9 0.1 reshape.39
  46.0 0.2 fusion.32
  46.2 0.7 pad_maximum_fusion.10
  46.9 12.9 %all-to-all-start.1 = ((f32[5,32,128]{2,0,1:T(8,128)}), f32[5,32,128]{2,0,1:T(8,128)S(1)}, u32[]{:S(2)}, u32[]{:S(2)}) async-start(f32[5,32,128]{2,0,1:T(8,128)} %pad_maximum_fusion.10), calls=%async_computation.1 | async-start | bytes 262144 | tf_op jit(solution)/shard_map/all_to_all | solution.py:74
  59.8 0.1 slice_reduce_fusion
  59.9 9.2 %all-to-all-done.1 = f32[5,32,128]{2,0,1:T(8,128)S(1)} async-done(((f32[5,32,128]{2,0,1:T(8,128)}), f32[5,32,128]{2,0,1:T(8,128)S(1)}, u32[]{:S(2)}, u32[]{:S(2)}) %all-to-all-start.1) | async-done | bytes 81952 | tf_op jit(solution)/shard_map/all_to_all | solution.py:74
  69.1 0.6 slice_add_fusion.2
  69.7 0.6 select_reduce_fusion.1
  (19 shorter events, 0.3 us)
Async XLA Ops:
  0.6 31.1 %copy-start = (f32[32,4,4096]{2,1,0:T(4,128)S(1)}, f32[32,4,4096]{2,1,0:T(4,128)}, u32[]{:S(2)}) copy-start(f32[32,4,4096]{2,1,0:T(4,128)} %param.10) | copy-start | bytes 6291460
  5.6 11.2 %collective-permute-start.1 = (f32[18,2,4096]{2,1,0:T(2,128)S(1)}, f32[18,2,4096]{2,1,0:T(2,128)S(1)}, u32[]{:S(2)}, u32[]{:S(2)}) collective-permute-start(f32[18,2,4096]{2,1,0:T(2,128)S(1)} %copy.54), channel_id=1, source_target_pairs={{0,32},{64,96},{128,160},{192,224},{256,288},{320,352},{384,416},{... | collective-permute-start | bytes 1769480 | tf_op jit(solution)/shard_map/ppermute | solution.py:91
  14.8 11.2 %collective-permute-start = (f32[18,2,4096]{2,1,0:T(2,128)S(1)}, f32[18,2,4096]{2,1,0:T(2,128)S(1)}, u32[]{:S(2)}, u32[]{:S(2)}) collective-permute-start(f32[18,2,4096]{2,1,0:T(2,128)S(1)} %copy.53), channel_id=1, source_target_pairs={{32,64},{96,128},{160,192},{224,256},{288,320},{352,384},{416,448}... | collective-permute-start | bytes 1769480 | tf_op jit(solution)/shard_map/ppermute | solution.py:90
  31.8 38.0 %copy-start.1 = (s32[128]{0:T(128)S(1)}, s32[128]{0:T(128)}, u32[]{:S(2)}) copy-start(s32[128]{0:T(128)} %param.11) | copy-start | bytes 1540
  35.4 10.4 %all-to-all-start = ((f32[16,1,544]{2,1,0:T(1,128)}), f32[16,1,544]{2,1,0:T(1,128)S(1)}, u32[]{:S(2)}, u32[]{:S(2)}) async-start(f32[16,1,544]{2,1,0:T(1,128)} %broadcast_in_dim.127), calls=%async_computation | async-start | bytes 81920 | tf_op jit(solution)/shard_map/all_to_all | solution.py:62
  46.9 22.2 %all-to-all-start.1 = ((f32[5,32,128]{2,0,1:T(8,128)}), f32[5,32,128]{2,0,1:T(8,128)S(1)}, u32[]{:S(2)}, u32[]{:S(2)}) async-start(f32[5,32,128]{2,0,1:T(8,128)} %pad_maximum_fusion.10), calls=%async_computation.1 | async-start | bytes 262144 | tf_op jit(solution)/shard_map/all_to_all | solution.py:74

commit v18 on v16

--- a/solution.py
+++ b/solution.py
@@ -87,7 +87,8 @@
     across = [(i, i + 1) for i in range(1, size - 1, 2)] + [(i, i - 1) for i in range(2, size, 2)]
     within = [(i, i + 1) for i in range(0, size, 2)] + [(i + 1, i) for i in range(0, size, 2)]
     far = lax.ppermute(jnp.where(even, lower, upper), "slab", across)
-    near = lax.ppermute(jnp.where(even, upper, lower), "slab", within)
+    inner, far = lax.optimization_barrier((jnp.where(even, upper, lower), far))
+    near = lax.ppermute(inner, "slab", within)
     before = jnp.where(even, far, near)
     after = jnp.where(even, near, far)
     fields = jnp.concatenate([before[:-1], body, after[:-1]], axis=1)

time: 70.3 us -> 72.3 us (1.028)
  starting transfers between devices: 27 us -> 28.3 us
    ppermute x1, starting transfers between devices: 8.79 us -> 1.92 us  [per_device(): near = lax.ppermute(inner, 'slab', within)]
    all_to_all x1, starting transfers between devices: 3.39 us -> 8.88 us  [exchange_sum(): received = lax.all_to_all(copies, axis, 0, 0, tiled=True)]
    ppermute x1, starting transfers between devices: 1.92 us -> 4.59 us  [per_device(): far = lax.ppermute(jnp.where(even, lower, upper), 'slab', across)]
    ppermute x1, waiting for transfers between devices: 0.01 us -> 1.95 us  [per_device(): near = lax.ppermute(inner, 'slab', within)]
    ppermute x1, waiting for transfers between devices: 9.25 us -> 7.55 us  [per_device(): far = lax.ppermute(jnp.where(even, lower, upper), 'slab', across)]
  transfers between devices with their start and end apart: 4 -> 4, of which waited for: 3 -> 4; matrix products, arithmetic and copies ran while one was open for 1% -> 0% of each run, Pallas kernels for 0% -> 0%
where the time goes in v18:
time: 72.3 us; the launch traced here: 72 us
  starting transfers between devices  28.3 us (39%)
  waiting for transfers between devices  25.7 us (36%)
  other arithmetic  8.46 us (12%)
  local copies, waits for them, and re-layouts  5.77 us (8%)
  matrix products  2.84 us (4%)
  between operations  0.88 us (1%)
    all_to_all x1, starting transfers between devices, exchange_scatter(): received = jnp.sum(lax.all_to_all(message, axis, 0, 0, tiled=True), axis=0)  12.9 us
    all_to_all x1, starting transfers between devices, exchange_sum(): received = lax.all_to_all(copies, axis, 0, 0, tiled=True)  8.88 us
    all_to_all x1, waiting for transfers between devices, exchange_scatter(): received = jnp.sum(lax.all_to_all(message, axis, 0, 0, tiled=True), axis=0)  8.82 us
    ppermute x1, waiting for transfers between devices, per_device(): far = lax.ppermute(jnp.where(even, lower, upper), 'slab', across)  7.55 us
    all_to_all x1, waiting for transfers between devices, exchange_sum(): received = lax.all_to_all(copies, axis, 0, 0, tiled=True)  7.41 us
    ppermute x1, starting transfers between devices, per_device(): far = lax.ppermute(jnp.where(even, lower, upper), 'slab', across)  4.59 us
    add x3, other arithmetic, update(): return middle + rate_field * (zsum + lateral(middle) - 6.0 * middle)  3.33 us
    dot_general x1, matrix products, per_device(): jnp.einsum('bzc,gzc->bg', direction_bank, fields, precision=lax.Precision...  2.84 us
  transfers between devices with their start and end apart: 4, of which 4 were waited for; matrix products, arithmetic and copies ran while one was open for 0% of the time, Pallas kernels for 0%

profile of v18, /device:TPU:1, one launch (start us, length us, event | category | flops | bytes accessed | tf_op | source)
XLA Modules:
  0.0 72.0 jit_solution(13222256451013314890)
XLA Ops:
  0.7 1.0 %broadcast_in_dim.106 = f32[1,4,4096]{2,0,1:T(1,128)S(1)} reshape(f32[4,4096]{1,0:T(4,128)} %param.6) | data formatting | bytes 131072 | tf_op jit(solution)/shard_map/broadcast_in_dim | solution.py:79
  1.7 1.1 %select_reduce_fusion = f32[4,4096]{1,0:T(4,128)S(1)} fusion(f32[8]{0:T(128)} %param.9, s32[4,4096]{1,0:T(4,128)} %param.8), kind=kLoop, calls=%fused_computation.40 | loop fusion | flops 376832 | bytes 131104 | tf_op jit(solution)/shard_map/reduce_sum | solution.py:31
  3.0 1.8 %copy.52 = f32[16,4,4096]{2,0,1:T(8,128)S(1)} copy(f32[16,4,4096]{2,1,0:T(4,128)} %param.7) | data formatting | bytes 2097152 | tf_op args[1]
  4.8 0.1 fusion.21
  4.9 0.2 fusion.23
  5.1 0.5 copy.55
  5.6 4.6 %collective-permute-start = (f32[18,2,4096]{2,1,0:T(2,128)S(1)}, f32[18,2,4096]{2,1,0:T(2,128)S(1)}, u32[]{:S(2)}, u32[]{:S(2)}) collective-permute-start(f32[18,2,4096]{2,1,0:T(2,128)S(1)} %copy.55), channel_id=1, source_target_pairs={{32,64},{96,128},{160,192},{224,256},{288,320},{352,384},{416,448}... | collective-permute-start | bytes 1769480 | tf_op jit(solution)/shard_map/ppermute | solution.py:89
  10.2 7.6 %collective-permute-done = f32[18,2,4096]{2,1,0:T(2,128)S(1)} collective-permute-done((f32[18,2,4096]{2,1,0:T(2,128)S(1)}, f32[18,2,4096]{2,1,0:T(2,128)S(1)}, u32[]{:S(2)}, u32[]{:S(2)}) %collective-permute-start) | collective-permute-done | bytes 589856 | tf_op jit(solution)/shard_map/ppermute | solution.py:89
  17.7 0.5 copy.56
  18.2 1.9 %collective-permute-start.1 = (f32[18,2,4096]{2,1,0:T(2,128)S(1)}, f32[18,2,4096]{2,1,0:T(2,128)S(1)}, u32[]{:S(2)}, u32[]{:S(2)}) collective-permute-start(f32[18,2,4096]{2,1,0:T(2,128)S(1)} %copy.56), channel_id=1, source_target_pairs={{0,32},{64,96},{128,160},{192,224},{256,288},{320,352},{384,416},{... | collective-permute-start | bytes 1769480 | tf_op jit(solution)/shard_map/ppermute | solution.py:91
  20.1 2.0 %collective-permute-done.1 = f32[18,2,4096]{2,1,0:T(2,128)S(1)} collective-permute-done((f32[18,2,4096]{2,1,0:T(2,128)S(1)}, f32[18,2,4096]{2,1,0:T(2,128)S(1)}, u32[]{:S(2)}, u32[]{:S(2)}) %collective-permute-start.1) | collective-permute-done | bytes 589856 | tf_op jit(solution)/shard_map/ppermute | solution.py:91
  22.1 0.7 copy_select_fusion.1
  22.8 0.1 pad_maximum_fusion.10
  22.9 0.2 pad_maximum_fusion.4
  23.1 0.9 %fusion.28 = f32[1,6,4096]{2,0,1:T(1,128)S(1)} fusion(f32[1,6,4096]{2,0,1:T(1,128)S(1)} %pad_maximum_fusion.10, f32[1,6,4096]{2,1,0:T(8,128)S(1)} %get-tuple-element.14, pred[4096]{0:T(1024)(128)(4,1)S(1)} %get-tuple-element.21, pred[4096]{0:T(1024)(128)(4,1)S(1)} %get-tuple-element.22, f32[16,4,4096]{2,0,1:T(8,128)S(1)} %copy.52, ...), kind=kLoop, calls=%fused_computation.53 | loop fusion | flops 368640 | bytes 2531328 | tf_op jit(solution)/shard_map/add | solution.py:48
  24.0 0.6 multiply_add_fusion
  24.6 1.8 %fusion.6 = f32[16,6,4096]{2,0,1:T(8,128)S(1)} fusion(f32[16,6,4096]{2,0,1:T(8,128)S(1)} %pad_maximum_fusion.4, f32[17,2,4096]{2,0,1:T(8,128)S(1)} %bitcast.32, f32[16,4,4096]{2,0,1:T(8,128)S(1)} %copy.52, f32[1,4,4096]{2,0,1:T(1,128)S(1)} %broadcast_in_dim.106, f32[17,2,4096]{2,0,1:T(8,128)S(1)} %bitcast.36, f32[6,4096]{1,0:T(8,128)S(1)} %get-tuple-element.13, ...), kind=kLoop, calls=%fused_computation.7 | loop fusion | flops 5898240 | bytes 5480448 | tf_op jit(solution)/shard_map/add | solution.py:48
  26.6 1.2 %abs_reduce_fusion = (f32[4,4096]{1,0:T(4,128)S(1)}, f32[16,4,4096]{2,0,1:T(8,128)S(1)}) fusion(f32[16,4,4096]{2,0,1:T(8,128)S(1)} %slice.183, pred[4096]{0:T(1024)(128)(4,1)S(1)} %get-tuple-element.21, pred[4096]{0:T(1024)(128)(4,1)S(1)} %get-tuple-element.22, f32[16,6,4096]{2,0,1:T(8,128)S(1)} %fusion.6, f32[4,4096]{1,0:T(4,128)S(1)} %broadcast_multiply_fusion), kind=kLoop, calls=%fused_computation.28 | loop fusion | flops 3391488 | bytes 4333568 | tf_op jit(solution)/shard_map/reduce_sum | solution.py:99
  27.8 2.8 %fusion.11 = f32[32,17]{0,1:T(8,128)S(1)} fusion(f32[32,4,4096]{2,1,0:T(4,128)S(1)} %copy-done, f32[16,4,4096]{2,0,1:T(8,128)S(1)} %get-tuple-element.8, f32[1,4,4096]{2,0,1:T(1,128)S(1)} %multiply_add_fusion), kind=kOutput, calls=%fused_computation.22 | convolution fusion | flops 107233280 | bytes 3213440 | tf_op jit(solution)/shard_map/bzc,gzc->bg/dot_general | solution.py:100
  30.7 0.1 copy.63
  30.7 0.1 broadcast_in_dim.124
  30.9 0.6 broadcast_in_dim.125
  31.5 8.9 %all-to-all-start = ((f32[16,1,544]{2,1,0:T(1,128)}), f32[16,1,544]{2,1,0:T(1,128)S(1)}, u32[]{:S(2)}, u32[]{:S(2)}) async-start(f32[16,1,544]{2,1,0:T(1,128)} %broadcast_in_dim.125), calls=%async_computation | async-start | bytes 81920 | tf_op jit(solution)/shard_map/all_to_all | solution.py:62
  40.4 7.4 %all-to-all-done = f32[16,1,544]{2,1,0:T(1,128)S(1)} async-done(((f32[16,1,544]{2,1,0:T(1,128)}), f32[16,1,544]{2,1,0:T(1,128)S(1)}, u32[]{:S(2)}, u32[]{:S(2)}) %all-to-all-start) | async-done | bytes 34848 | tf_op jit(solution)/shard_map/all_to_all | solution.py:62
  47.8 0.1 reshape.46
  47.9 0.2 fusion.32
  48.1 0.7 copy.65
  48.9 12.9 %all-to-all-start.1 = ((f32[32,1,544]{2,1,0:T(1,128)}), f32[32,1,544]{2,1,0:T(1,128)S(1)}, u32[]{:S(2)}, u32[]{:S(2)}) async-start(f32[32,1,544]{2,1,0:T(1,128)} %copy.65), calls=%async_computation.1 | async-start | bytes 163840 | tf_op jit(solution)/shard_map/all_to_all | solution.py:73
  61.8 0.1 slice_reduce_fusion
  61.9 8.8 %all-to-all-done.1 = f32[32,1,544]{2,1,0:T(1,128)S(1)} async-done(((f32[32,1,544]{2,1,0:T(1,128)}), f32[32,1,544]{2,1,0:T(1,128)S(1)}, u32[]{:S(2)}, u32[]{:S(2)}) %all-to-all-start.1) | async-done | bytes 69664 | tf_op jit(solution)/shard_map/all_to_all | solution.py:73
  70.8 0.6 bitcast_add_fusion
  71.4 0.6 select_reduce_fusion.1
  (20 shorter events, 0.5 us)
Async XLA Ops:
  0.6 27.2 %copy-start = (f32[32,4,4096]{2,1,0:T(4,128)S(1)}, f32[32,4,4096]{2,1,0:T(4,128)}, u32[]{:S(2)}) copy-start(f32[32,4,4096]{2,1,0:T(4,128)} %param.10) | copy-start | bytes 6291460
  5.6 12.2 %collective-permute-start = (f32[18,2,4096]{2,1,0:T(2,128)S(1)}, f32[18,2,4096]{2,1,0:T(2,128)S(1)}, u32[]{:S(2)}, u32[]{:S(2)}) collective-permute-start(f32[18,2,4096]{2,1,0:T(2,128)S(1)} %copy.55), channel_id=1, source_target_pairs={{32,64},{96,128},{160,192},{224,256},{288,320},{352,384},{416,448}... | collective-permute-start | bytes 1769480 | tf_op jit(solution)/shard_map/ppermute | solution.py:89
  18.2 3.9 %collective-permute-start.1 = (f32[18,2,4096]{2,1,0:T(2,128)S(1)}, f32[18,2,4096]{2,1,0:T(2,128)S(1)}, u32[]{:S(2)}, u32[]{:S(2)}) collective-permute-start(f32[18,2,4096]{2,1,0:T(2,128)S(1)} %copy.56), channel_id=1, source_target_pairs={{0,32},{64,96},{128,160},{192,224},{256,288},{320,352},{384,416},{... | collective-permute-start | bytes 1769480 | tf_op jit(solution)/shard_map/ppermute | solution.py:91
  27.8 43.6 %copy-start.1 = (s32[128]{0:T(128)S(1)}, s32[128]{0:T(128)}, u32[]{:S(2)}) copy-start(s32[128]{0:T(128)} %param.11) | copy-start | bytes 1540
  31.5 16.3 %all-to-all-start = ((f32[16,1,544]{2,1,0:T(1,128)}), f32[16,1,544]{2,1,0:T(1,128)S(1)}, u32[]{:S(2)}, u32[]{:S(2)}) async-start(f32[16,1,544]{2,1,0:T(1,128)} %broadcast_in_dim.125), calls=%async_computation | async-start | bytes 81920 | tf_op jit(solution)/shard_map/all_to_all | solution.py:62
  48.9 21.8 %all-to-all-start.1 = ((f32[32,1,544]{2,1,0:T(1,128)}), f32[32,1,544]{2,1,0:T(1,128)S(1)}, u32[]{:S(2)}, u32[]{:S(2)}) async-start(f32[32,1,544]{2,1,0:T(1,128)} %copy.65), calls=%async_computation.1 | async-start | bytes 163840 | tf_op jit(solution)/shard_map/all_to_all | solution.py:73
